TPU v7x, 256 devices: a whole 4x4x8 slice. The times are simulated.
256 devices in a mesh: energy: 64 (over z, y, core), atoms: 4 (over x).
Axes of the slice: x: 4, y: 4, z: 8, core: 2. Of those that a mesh axis runs over, the one named last changes fastest.
Arguments:
- green: bfloat16 [1024, 256, 288], P('energy', 'atoms'), may hold values from -6 to 6
- superop: bfloat16 [4, 288, 288], replicated, may hold values from -0.1875 to 0.1875
- phonon: bfloat16 [64, 2048], replicated, may hold values from -0.1875 to 0.1875
- owner: int32 [256, 1], P('atoms'), may hold values from 0 to 63; in each aligned block of 64 rows (0 to 63, 64 to 127, ...) at most 4 rows name the same one
- neighbours: int32 [256, 4], P('atoms'), may hold values from -1 to 255, as said below
Outputs:
- self_energy: bfloat16 [1024, 256, 288], P('energy', 'atoms')
Inputs may be any that keep to these rules, and one draw needn't show every extreme that they name: `owner`: within each aligned block of 64 atoms (one atom group) no domain holds more than 4 atoms, and some domain holds exactly 4. `neighbours`: each entry is -1 or the index of an atom at most 8 away from the row's atom; some entry lies exactly 8 above its row's atom, in the next atom group.
All inputs are finite; a program needn't handle non-finite values.
Results may differ from a plain program's by a relative error of at most 0.0049.
Values may be sent and summed in bfloat16 or wider, within the bound.
No kernel may reach another device: no remote copies, remote signals or barrier semaphores. Data moves between devices by JAX's collectives and lax.ppermute only.
A program may use at most 64 MiB of HBM per device.

v0:
```python
import jax
import jax.numpy as jnp
from jax import lax
from jax.sharding import PartitionSpec as P

SPLIT = 2
HALO = 8
ATOMS_DEV = 1


def padded(block, sides, width):
    for axis, dim in sides:
        count = lax.axis_size(axis)
        forward = [(i, i + 1) for i in range(count - 1)]
        backward = [(target, source) for source, target in forward]
        low = lax.ppermute(
            lax.slice_in_dim(block, block.shape[dim] - width, None, axis=dim), axis, forward
        )
        high = lax.ppermute(lax.slice_in_dim(block, 0, width, axis=dim), axis, backward)
        block = jnp.concatenate([low, block, high], axis=dim)
    return block


def toeplitz_rows(kernel_row, count):
    length = 2 * count
    flipped = kernel_row[::-1]
    tiled = jnp.tile(flipped, count)[: count * (length - 1)]
    return tiled.reshape(count, length - 1)[:, count - 1 : 2 * count - 1]


def per_device(green, superop, phonon, owner, neighbours):
    local_energies = green.shape[0]
    group_size = green.shape[1]
    comps = green.shape[2]
    slots = neighbours.shape[1]
    half_width = comps // SPLIT
    group = lax.axis_index("atoms")
    widened = padded(green, (("atoms", 1),), HALO)
    present = neighbours >= 0
    target_rows = jnp.where(present, neighbours - group * group_size + HALO, 0)
    picked = jnp.take(widened, target_rows.reshape(-1), axis=1)
    picked = jnp.where(present.reshape(1, -1, 1), picked, jnp.zeros_like(picked))
    coupled = jnp.dot(
        picked.reshape(local_energies * group_size, slots * comps),
        superop.reshape(slots * comps, comps),
        preferred_element_type=jnp.float32,
    )
    coupled = coupled.reshape(local_energies, group_size, comps).astype(jnp.bfloat16)
    count = local_energies * lax.axis_size("energy")
    energy_rank = lax.axis_index("energy")
    first_atom = energy_rank * ATOMS_DEV
    mine = lax.dynamic_slice_in_dim(owner[:, 0], first_atom, ATOMS_DEV)

    def build_kernel(domain):
        return toeplitz_rows(phonon[domain], count)

    kernels = jax.vmap(build_kernel)(mine)
    split_blocks = coupled.reshape(local_energies, group_size, SPLIT, half_width)
    product = jnp.einsum(
        "oph,hoiw->poiw",
        kernels,
        lax.all_to_all(split_blocks, "energy", split_axis=1, concat_axis=0, tiled=True),
        preferred_element_type=jnp.float32,
    )
    result = lax.all_to_all(
        product.astype(jnp.bfloat16), "energy", split_axis=0, concat_axis=1, tiled=True
    )
    result = result.reshape(local_energies, group_size, comps)
    return result


def solution(mesh):
    return jax.shard_map(
        per_device,
        mesh=mesh,
        in_specs=(P("energy", "atoms", None), P(), P(), P("atoms", None), P("atoms", None)),
        out_specs=P("energy", "atoms", None),
        check_vma=False,
    )
```

profile of v0, /device:TPU:1, one launch (start us, length us, event | category | flops | bytes accessed | tf_op | source)
XLA Modules:
  0.0 214.0 jit_solution(9396868010489294610)
XLA Ops:
  0.0 1.7 copy.36
  1.7 4.0 %collective-permute-start = (bf16[16,8,288]{2,0,1:T(8,128)(2,1)S(1)}, bf16[16,8,288]{2,0,1:T(8,128)(2,1)S(1)}, u32[]{:S(2)}, u32[]{:S(2)}) collective-permute-start(bf16[16,8,288]{2,0,1:T(8,128)(2,1)S(1)} %get-tuple-element.18), channel_id=1, source_target_pairs={{0,1},{1,2},{2,3},{4,5},{5,6},{6,7},{8,9},{9,10},{10,11},{12,13},{... | collective-permute-start | bytes 221192 | tf_op jit(solution)/shard_map/ppermute | solution.py:16
  5.7 1.3 collective-permute-start.1
  7.0 1.2 constant_dynamic-slice_fusion.1
  10.2 0.8 constant_dynamic-slice_fusion
  10.9 1.5 reverse
  12.4 0.5 broadcast_bitcast_fusion
  13.0 24.7 %copy.51 = bf16[1,1,1024,2048]{3,1,2,0:T(2,128)(2,1)} copy(bf16[1,1,1024,2048]{3,2,1,0:T(8,128)(2,1)S(1)} %broadcast_bitcast_fusion) | data formatting | bytes 8388608
  37.7 0.1 reshape.125
  37.8 0.1 copy.34
  38.0 0.1 broadcast_in_dim.34
  38.1 0.1 broadcast_in_dim.35
  38.2 0.1 copy.35
  38.3 0.1 broadcast_in_dim.37
  38.5 0.1 broadcast_in_dim.38
  38.6 0.2 pad_maximum_fusion
  38.8 2.8 %gather_fusion = bf16[256,16,288]{2,1,0:T(8,128)(2,1)} fusion(bf16[16,80,288]{2,0,1:T(8,128)(2,1)S(1)} %pad_maximum_fusion, s32[1024]{0:T(1024)S(1)} %pad_clamp_fusion), kind=kCustom, calls=%fused_computation | custom fusion | bytes 4719616 | tf_op jit(solution)/shard_map/jit(_take)/gather | solution.py:41
  41.6 3.2 %select_bitcast_fusion = bf16[16,256,288]{2,0,1:T(8,128)(2,1)S(1)} fusion(bf16[256,16,288]{2,1,0:T(8,128)(2,1)} %gather_fusion, pred[256,288]{1,0:T(8,128)(4,1)S(1)} %broadcast_in_dim.35, pred[256,288]{1,0:T(8,128)(4,1)S(1)} %broadcast_in_dim.38), kind=kLoop, calls=%fused_computation.2 | loop fusion | flops 2359296 | bytes 4866048 | tf_op jit(solution)/shard_map/jit(_where)/select_n | solution.py:42
  44.8 2.5 %copy.40 = bf16[16,256,288]{2,1,0:T(8,128)(2,1)} copy(bf16[16,256,288]{2,0,1:T(8,128)(2,1)S(1)} %select_bitcast_fusion) | data formatting | bytes 4718592 | tf_op jit(solution)/shard_map/jit(_where)/select_n | solution.py:42
  47.3 5.8 %select_n.60 = bf16[16,64,1152]{2,1,0:T(8,128)(2,1)S(1)} reshape(bf16[16,256,288]{2,1,0:T(8,128)(2,1)} %copy.40) | data formatting | bytes 4718592 | tf_op jit(solution)/shard_map/jit(_where)/select_n | solution.py:42
  53.1 2.3 %convolution_convert_fusion = bf16[16,64,288]{2,1,0:T(8,128)(2,1)} fusion(bf16[16,64,1152]{2,1,0:T(8,128)(2,1)S(1)} %select_n.60, bf16[1152,288,1]{1,0,2:T(8,128)(2,1)S(1)} %bitcast.36), kind=kOutput, calls=%fused_computation.6 | convolution fusion | flops 679772160 | bytes 3612672 | tf_op jit(solution)/shard_map/dot_general | solution.py:43
  55.4 3.1 %reshape.127 = bf16[16,64,2,144]{3,2,1,0:T(2,128)(2,1)S(1)} reshape(bf16[16,64,288]{2,1,0:T(8,128)(2,1)} %convolution_convert_fusion) | data formatting | bytes 1179648 | tf_op jit(solution)/shard_map/reshape | solution.py:58
  58.6 2.2 %copy.42 = bf16[16,64,2,144]{3,0,2,1:T(8,128)(2,1)} copy(bf16[16,64,2,144]{3,2,1,0:T(2,128)(2,1)S(1)} %reshape.127) | data formatting | bytes 1179648 | tf_op jit(solution)/shard_map/reshape | solution.py:58
  60.8 12.6 %all-to-all-start = ((bf16[16,64,2,144]{3,0,2,1:T(8,128)(2,1)}), bf16[16,64,2,144]{3,0,2,1:T(8,128)(2,1)S(1)}, u32[]{:S(2)}, u32[]{:S(2)}) async-start(bf16[16,64,2,144]{3,0,2,1:T(8,128)(2,1)} %copy.42), calls=%async_computation | async-start | bytes 2097152 | tf_op jit(solution)/shard_map/all_to_all | solution.py:62
  73.4 84.7 %slice_reduce_fusion = bf16[2096128]{0:T(1024)(128)(2,1)} fusion(bf16[1,2097152]{1,0:T(2,128)(2,1)} %bitcast.37), kind=kLoop, calls=%fused_computation.1 | loop fusion | bytes 8384512 | tf_op jit(solution)/shard_map/vmap()/slice | solution.py:27
  158.1 10.7 %reshape.129 = bf16[1,1024,2047]{2,1,0:T(8,128)(2,1)} reshape(bf16[2096128]{0:T(1024)(128)(2,1)} %slice_reduce_fusion) | data formatting | bytes 8384512 | tf_op jit(solution)/shard_map/vmap()/reshape | solution.py:28
  168.8 3.6 %fusion.2 = bf16[1024,1,2,144]{0,3,2,1:T(8,128)(2,1)S(1)} fusion(bf16[1024,2,144]{2,0,1:T(8,128)(2,1)S(1)} %bitcast.40, bf16[1,1024,2047]{2,1,0:T(8,128)(2,1)} %reshape.129), kind=kOutput, calls=%fused_computation.8 | convolution fusion | flops 604274688 | bytes 3276800 | tf_op jit(solution)/shard_map/oph,hoiw->poiw/dot_general | solution.py:59
  172.4 0.9 copy.45
  173.3 38.1 %all_to_all.30 = bf16[1024,1,2,144]{3,2,1,0:T(2,128)(2,1)S(1)} all-to-all(bf16[1024,1,2,144]{3,2,1,0:T(2,128)(2,1)S(1)} %copy.45), channel_id=1, replica_groups=mesh['energy'=64,'atoms'=4] {'energy'}, dimensions={0} | all-to-all | bytes 1179648 | tf_op jit(solution)/shard_map/all_to_all | solution.py:65
  211.4 0.1 copy.46
  211.5 1.1 copy.47
  212.6 1.4 reshape.131
  (14 shorter events, 0.3 us)
Async XLA Ops:
  0.0 53.1 %copy-start = (bf16[4,288,288]{2,1,0:T(8,128)(2,1)S(1)}, bf16[4,288,288]{2,1,0:T(8,128)(2,1)}, u32[]{:S(2)}) copy-start(bf16[4,288,288]{2,1,0:T(8,128)(2,1)} %param.6) | copy-start | bytes 1990660
  1.7 36.9 %collective-permute-start = (bf16[16,8,288]{2,0,1:T(8,128)(2,1)S(1)}, bf16[16,8,288]{2,0,1:T(8,128)(2,1)S(1)}, u32[]{:S(2)}, u32[]{:S(2)}) collective-permute-start(bf16[16,8,288]{2,0,1:T(8,128)(2,1)S(1)} %get-tuple-element.18), channel_id=1, source_target_pairs={{0,1},{1,2},{2,3},{4,5},{5,6},{6,7},{8,9},{9,10},{10,11},{12,13},{... | collective-permute-start | bytes 221192 | tf_op jit(solution)/shard_map/ppermute | solution.py:16
  5.7 33.0 %collective-permute-start.1 = (bf16[16,8,288]{2,0,1:T(8,128)(2,1)S(1)}, bf16[16,8,288]{2,0,1:T(8,128)(2,1)S(1)}, u32[]{:S(2)}, u32[]{:S(2)}) collective-permute-start(bf16[16,8,288]{2,0,1:T(8,128)(2,1)S(1)} %get-tuple-element.19), channel_id=1, source_target_pairs={{1,0},{2,1},{3,2},{5,4},{6,5},{7,6},{9,8},{10,9},{11,10},{13,12},{... | collective-permute-start | bytes 221192 | tf_op jit(solution)/shard_map/ppermute | solution.py:19
  12.9 24.7 %copy-start.1 = (s32[64,4]{0,1:T(4,128)S(1)}, s32[64,4]{0,1:T(4,128)}, u32[]{:S(2)}) copy-start(s32[64,4]{0,1:T(4,128)} %param.9) | copy-start | bytes 3076
  60.8 108.0 %all-to-all-start = ((bf16[16,64,2,144]{3,0,2,1:T(8,128)(2,1)}), bf16[16,64,2,144]{3,0,2,1:T(8,128)(2,1)S(1)}, u32[]{:S(2)}, u32[]{:S(2)}) async-start(bf16[16,64,2,144]{3,0,2,1:T(8,128)(2,1)} %copy.42), calls=%async_computation | async-start | bytes 2097152 | tf_op jit(solution)/shard_map/all_to_all | solution.py:62
where the time goes:
time: 216 us; the launch traced here: 214 us
  local copies, waits for them, and re-layouts  147 us (68%)
  blocking collectives  38.1 us (18%)
  starting transfers between devices  17.9 us (8%)
  matrix products  5.92 us (3%)
  other arithmetic  3.44 us (2%)
    slice x1, local copies, waits for them, and re-layouts, toeplitz_rows(): tiled = jnp.tile(flipped, count)[:count * (length - 1)]  84.7 us
    all_to_all x1, blocking collectives, per_device(): lax.all_to_all(product.astype(jnp.bfloat16), 'energy', split_axis=0, conc...  38.1 us
    unnamed x8, local copies, waits for them, and re-layouts  28.3 us
    all_to_all x1, starting transfers between devices, per_device(): lax.all_to_all(split_blocks, 'energy', split_axis=1, concat_axis=0, tiled...  12.6 us
    reshape x1, local copies, waits for them, and re-layouts, toeplitz_rows(): return tiled.reshape(count, length - 1)[:, count - 1:2 * count - 1]  10.7 us
    select_n x2, local copies, waits for them, and re-layouts, per_device(): jnp.where(present.reshape(1, -1, 1), picked, jnp.zeros_like(picked))  8.28 us
    reshape x2, local copies, waits for them, and re-layouts, per_device(): coupled.reshape(local_energies, group_size, SPLIT, half_width)  5.32 us
  transfers between devices with their start and end apart: 3, of which 0 were waited for; matrix products, arithmetic and copies ran while one was open for 58% of the time, Pallas kernels for 0%

commit v1 on v0

--- a/solution.py
+++ b/solution.py
@@ -1,9 +1,10 @@
 import jax
 import jax.numpy as jnp
 from jax import lax
+from jax.experimental import pallas as pl
+from jax.experimental.pallas import tpu as pltpu
 from jax.sharding import PartitionSpec as P
 
-SPLIT = 2
 HALO = 8
 ATOMS_DEV = 1
 
@@ -21,11 +22,37 @@
     return block
 
 
-def toeplitz_rows(kernel_row, count):
-    length = 2 * count
-    flipped = kernel_row[::-1]
-    tiled = jnp.tile(flipped, count)[: count * (length - 1)]
-    return tiled.reshape(count, length - 1)[:, count - 1 : 2 * count - 1]
+def toeplitz_kernel(domain_ref, phonon_ref, columns_ref, out_ref):
+    count = columns_ref.shape[0]
+    row = phonon_ref[0].astype(jnp.float32)
+    wide = jnp.broadcast_to(row, (count, 2 * count))
+    rolled = pltpu.roll(wide, shift=count + 1, axis=1, stride=1, stride_axis=0)
+    kernel = rolled[:, :count].astype(jnp.bfloat16)
+    out_ref[...] = jnp.dot(
+        kernel, columns_ref[...], preferred_element_type=jnp.float32
+    ).astype(out_ref.dtype)
+
+
+def toeplitz_apply(domain, phonon_rev, columns):
+    count, comps = columns.shape
+    return pl.pallas_call(
+        toeplitz_kernel,
+        out_shape=jax.ShapeDtypeStruct((count, comps), jnp.bfloat16),
+        grid_spec=pltpu.PrefetchScalarGridSpec(
+            num_scalar_prefetch=1,
+            grid=(1,),
+            in_specs=[
+                pl.BlockSpec((1, 1, 2 * count), lambda i, d: (d[0], 0, 0)),
+                pl.BlockSpec((count, comps), lambda i, d: (0, 0)),
+            ],
+            out_specs=pl.BlockSpec((count, comps), lambda i, d: (0, 0)),
+        ),
+        cost_estimate=pl.CostEstimate(
+            flops=2 * count * count * comps,
+            bytes_accessed=2 * (2 * count + 2 * count * comps),
+            transcendentals=0,
+        ),
+    )(domain, phonon_rev, columns)
 
 
 def per_device(green, superop, phonon, owner, neighbours):
@@ -33,7 +60,6 @@
     group_size = green.shape[1]
     comps = green.shape[2]
     slots = neighbours.shape[1]
-    half_width = comps // SPLIT
     group = lax.axis_index("atoms")
     widened = padded(green, (("atoms", 1),), HALO)
     present = neighbours >= 0
@@ -48,24 +74,13 @@
     coupled = coupled.reshape(local_energies, group_size, comps).astype(jnp.bfloat16)
     count = local_energies * lax.axis_size("energy")
     energy_rank = lax.axis_index("energy")
-    first_atom = energy_rank * ATOMS_DEV
-    mine = lax.dynamic_slice_in_dim(owner[:, 0], first_atom, ATOMS_DEV)
-
-    def build_kernel(domain):
-        return toeplitz_rows(phonon[domain], count)
-
-    kernels = jax.vmap(build_kernel)(mine)
-    split_blocks = coupled.reshape(local_energies, group_size, SPLIT, half_width)
-    product = jnp.einsum(
-        "oph,hoiw->poiw",
-        kernels,
-        lax.all_to_all(split_blocks, "energy", split_axis=1, concat_axis=0, tiled=True),
-        preferred_element_type=jnp.float32,
+    mine = lax.dynamic_slice_in_dim(owner[:, 0], energy_rank * ATOMS_DEV, ATOMS_DEV)
+    phonon_rev = phonon[:, ::-1].reshape(phonon.shape[0], 1, phonon.shape[1])
+    columns = lax.all_to_all(coupled, "energy", split_axis=1, concat_axis=0, tiled=True)
+    product = toeplitz_apply(mine, phonon_rev, columns.reshape(count, comps))
+    result = lax.all_to_all(
+        product.reshape(count, ATOMS_DEV, comps), "energy", split_axis=0, concat_axis=1, tiled=True
     )
-    result = lax.all_to_all(
-        product.astype(jnp.bfloat16), "energy", split_axis=0, concat_axis=1, tiled=True
-    )
-    result = result.reshape(local_energies, group_size, comps)
     return result
 
 

time: 216 us -> 102 us (0.47)
  local copies, waits for them, and re-layouts: 147 us -> 23.1 us
  waiting for transfers between devices: 0.01 us -> 21.9 us
  blocking collectives: 38.1 us -> 25.1 us
  matrix products: 5.92 us -> 1.44 us
  Pallas kernels: 0 us -> 3.97 us
  other arithmetic: 3.44 us -> 6.35 us
    slice x1 -> x0, local copies, waits for them, and re-layouts: 84.7 us -> none  [toeplitz_rows(): tiled = jnp.tile(flipped, count)[:count * (length - 1)]]
    unnamed x8 -> x12, local copies, waits for them, and re-layouts: 28.3 us -> 5.21 us
    all_to_all x1, waiting for transfers between devices: 0.01 us -> 19.5 us  [per_device(): lax.all_to_all(coupled, 'energy', split_axis=1, concat_axis=0, tiled=True)]
    reshape x4 -> x2, local copies, waits for them, and re-layouts: 17.4 us -> 1.72 us  [the longest x1 1.21 us: per_device(): phonon_rev = phonon[:, ::-1].reshape(phonon.shape[0], 1, phonon.shape[1])]
    all_to_all x1, blocking collectives: 38.1 us -> 25.1 us  [per_device(): lax.all_to_all(product.reshape(count, ATOMS_DEV, comps), 'energy', split_...]
    pallas_call x0 -> x1, Pallas kernels: none -> 3.97 us  [toeplitz_apply(): pl.pallas_call(toeplitz_kernel, out_shape=jax.ShapeDtypeStruct((count, co...]
    dot_general x1 -> x0, matrix products: 3.6 us -> none  [per_device(): jnp.einsum('oph,hoiw->poiw', kernels, lax.all_to_all(split_blocks, 'energ...]
    ppermute x1, waiting for transfers between devices: 0.01 us -> 2.38 us  [padded(): lax.ppermute(lax.slice_in_dim(block, 0, width, axis=dim), axis, backward)]
  transfers between devices with their start and end apart: 3 -> 3, of which waited for: 0 -> 2; matrix products, arithmetic and copies ran while one was open for 58% -> 5% of each run, Pallas kernels for 0% -> 0%
where the time goes in v1:
time: 102 us; the launch traced here: 101 us
  blocking collectives  25.1 us (25%)
  local copies, waits for them, and re-layouts  23.1 us (23%)
  waiting for transfers between devices  21.9 us (21%)
  starting transfers between devices  19 us (19%)
  other arithmetic  6.35 us (6%)
  Pallas kernels  3.97 us (4%)
  matrix products  1.44 us (1%)
    all_to_all x1, blocking collectives, per_device(): lax.all_to_all(product.reshape(count, ATOMS_DEV, comps), 'energy', split_...  25.1 us
    all_to_all x1, waiting for transfers between devices, per_device(): lax.all_to_all(coupled, 'energy', split_axis=1, concat_axis=0, tiled=True)  19.5 us
    all_to_all x1, starting transfers between devices, per_device(): lax.all_to_all(coupled, 'energy', split_axis=1, concat_axis=0, tiled=True)  13.8 us
    select_n x2, local copies, waits for them, and re-layouts, per_device(): jnp.where(present.reshape(1, -1, 1), picked, jnp.zeros_like(picked))  8.17 us
    unnamed x12, local copies, waits for them, and re-layouts  5.21 us
    pallas_call x1, Pallas kernels, toeplitz_apply(): pl.pallas_call(toeplitz_kernel, out_shape=jax.ShapeDtypeStruct((count, co...  3.97 us
    ppermute x1, starting transfers between devices, padded(): lax.ppermute(lax.slice_in_dim(block, block.shape[dim] - width, None, axis...  3.95 us
    select_n x1, other arithmetic, per_device(): jnp.where(present.reshape(1, -1, 1), picked, jnp.zeros_like(picked))  3.18 us
  transfers between devices with their start and end apart: 3, of which 2 were waited for; matrix products, arithmetic and copies ran while one was open for 5% of the time, Pallas kernels for 0%

profile of v1, /device:TPU:1, one launch (start us, length us, event | category | flops | bytes accessed | tf_op | source)
XLA Modules:
  0.0 101.0 jit_solution(6530910017291321052)
XLA Ops:
  0.0 1.7 %copy.36 = bf16[16,64,288]{2,0,1:T(8,128)(2,1)S(1)} copy(bf16[16,64,288]{2,1,0:T(8,128)(2,1)} %param.5) | data formatting | bytes 1179648 | tf_op args[0]
  1.7 4.0 %collective-permute-start = (bf16[16,8,288]{2,0,1:T(8,128)(2,1)S(1)}, bf16[16,8,288]{2,0,1:T(8,128)(2,1)S(1)}, u32[]{:S(2)}, u32[]{:S(2)}) collective-permute-start(bf16[16,8,288]{2,0,1:T(8,128)(2,1)S(1)} %get-tuple-element.7), channel_id=1, source_target_pairs={{0,1},{1,2},{2,3},{4,5},{5,6},{6,7},{8,9},{9,10},{10,11},{12,13},{... | collective-permute-start | bytes 221192 | tf_op jit(solution)/shard_map/ppermute | solution.py:17
  5.7 1.3 %collective-permute-start.1 = (bf16[16,8,288]{2,0,1:T(8,128)(2,1)S(1)}, bf16[16,8,288]{2,0,1:T(8,128)(2,1)S(1)}, u32[]{:S(2)}, u32[]{:S(2)}) collective-permute-start(bf16[16,8,288]{2,0,1:T(8,128)(2,1)S(1)} %get-tuple-element.8), channel_id=1, source_target_pairs={{1,0},{2,1},{3,2},{5,4},{6,5},{7,6},{9,8},{10,9},{11,10},{13,12},{... | collective-permute-start | bytes 221192 | tf_op jit(solution)/shard_map/ppermute | solution.py:20
  7.0 0.7 compare_and_fusion
  7.9 0.1 copy.34
  8.0 0.1 broadcast_in_dim.31
  8.1 0.1 broadcast_in_dim.32
  8.3 0.1 copy.35
  8.4 0.1 broadcast_in_dim.34
  8.5 0.1 broadcast_in_dim.35
  8.6 2.4 %collective-permute-done.1 = bf16[16,8,288]{2,0,1:T(8,128)(2,1)S(1)} collective-permute-done((bf16[16,8,288]{2,0,1:T(8,128)(2,1)S(1)}, bf16[16,8,288]{2,0,1:T(8,128)(2,1)S(1)}, u32[]{:S(2)}, u32[]{:S(2)}) %collective-permute-start.1) | collective-permute-done | bytes 73760 | tf_op jit(solution)/shard_map/ppermute | solution.py:20
  11.0 0.2 pad_maximum_fusion
  11.2 2.7 %gather_fusion = bf16[256,16,288]{2,1,0:T(8,128)(2,1)} fusion(bf16[16,80,288]{2,0,1:T(8,128)(2,1)S(1)} %pad_maximum_fusion, s32[1024]{0:T(1024)S(1)} %pad_clamp_fusion), kind=kCustom, calls=%fused_computation | custom fusion | bytes 4719616 | tf_op jit(solution)/shard_map/jit(_take)/gather | solution.py:67
  13.9 3.2 %select_bitcast_fusion = bf16[16,256,288]{2,0,1:T(8,128)(2,1)S(1)} fusion(bf16[256,16,288]{2,1,0:T(8,128)(2,1)} %gather_fusion, pred[256,288]{1,0:T(8,128)(4,1)S(1)} %broadcast_in_dim.32, pred[256,288]{1,0:T(8,128)(4,1)S(1)} %broadcast_in_dim.35), kind=kLoop, calls=%fused_computation.1 | loop fusion | flops 2359296 | bytes 4866048 | tf_op jit(solution)/shard_map/jit(_where)/select_n | solution.py:68
  17.1 2.4 %copy.40 = bf16[16,256,288]{2,1,0:T(8,128)(2,1)} copy(bf16[16,256,288]{2,0,1:T(8,128)(2,1)S(1)} %select_bitcast_fusion) | data formatting | bytes 4718592 | tf_op jit(solution)/shard_map/jit(_where)/select_n | solution.py:68
  19.5 5.8 %select_n.58 = bf16[16,64,1152]{2,1,0:T(8,128)(2,1)S(1)} reshape(bf16[16,256,288]{2,1,0:T(8,128)(2,1)} %copy.40) | data formatting | bytes 4718592 | tf_op jit(solution)/shard_map/jit(_where)/select_n | solution.py:68
  25.3 1.4 %convolution_convert_fusion = bf16[16,64,288]{2,1,0:T(8,128)(2,1)S(1)} fusion(bf16[16,64,1152]{2,1,0:T(8,128)(2,1)S(1)} %select_n.58, bf16[1152,288,1]{1,0,2:T(8,128)(2,1)S(1)} %bitcast.21), kind=kOutput, calls=%fused_computation.2 | convolution fusion | flops 679772160 | bytes 3612672 | tf_op jit(solution)/shard_map/dot_general | solution.py:69
  26.8 1.3 %copy.42 = bf16[16,64,288]{2,0,1:T(8,128)(2,1)} copy(bf16[16,64,288]{2,1,0:T(8,128)(2,1)S(1)} %convolution_convert_fusion) | data formatting | bytes 1179648 | tf_op jit(solution)/shard_map/convert_element_type | solution.py:74
  28.1 13.8 %all-to-all-start = ((bf16[16,64,288]{2,0,1:T(8,128)(2,1)}), bf16[16,64,288]{2,0,1:T(8,128)(2,1)S(1)}, u32[]{:S(2)}, u32[]{:S(2)}) async-start(bf16[16,64,288]{2,0,1:T(8,128)(2,1)} %copy.42), calls=%async_computation | async-start | bytes 1572864 | tf_op jit(solution)/shard_map/all_to_all | solution.py:79
  41.9 1.4 %rev.3 = bf16[64,2048]{1,0:T(8,128)(2,1)S(1)} reverse(bf16[64,2048]{1,0:T(8,128)(2,1)S(1)} %copy-done.2), dimensions={1} | reverse | bytes 524288 | tf_op jit(solution)/shard_map/rev | solution.py:78
  43.3 1.2 %copy.43.phonon_ref = bf16[64,1,2048]{2,1,0:T(2,128)(2,1)} copy(bf16[64,1,2048]{2,0,1:T(8,128)(2,1)S(1)} %bitcast.23) | data formatting | bytes 524288 | tf_op jit(solution)/shard_map/reshape | solution.py:78
  44.5 0.6 constant_dynamic-slice_fusion
  45.1 19.5 %all-to-all-done = bf16[16,64,288]{2,0,1:T(8,128)(2,1)S(1)} async-done(((bf16[16,64,288]{2,0,1:T(8,128)(2,1)}), bf16[16,64,288]{2,0,1:T(8,128)(2,1)S(1)}, u32[]{:S(2)}, u32[]{:S(2)}) %all-to-all-start) | async-done | bytes 589856 | tf_op jit(solution)/shard_map/all_to_all | solution.py:79
  64.6 0.9 copy-done.1
  65.5 4.0 %shard_map.55 = bf16[1024,288]{1,0:T(8,128)(2,1)} custom-call(s32[1]{0:T(128)} %bitcast.domain_ref, bf16[64,1,2048]{2,1,0:T(2,128)(2,1)} %copy.43.phonon_ref, bf16[1024,288]{1,0:T(8,128)(2,1)} %bitcast.24), custom_call_target="tpu_custom_call" | custom-call | flops 603979776 | bytes 1183744 | tf_op jit(solution)/shard_map/pallas_call | solution.py:38
  69.5 0.5 broadcast.95
  70.0 2.3 %reduce = bf16[1024,288]{1,0:T(8,128)(2,1)S(1)} reduce(bf16[1024,1,288]{2,0,1:T(8,128)(2,1)} %bitcast.25, bf16[]{:T(256)} %broadcast.95), dimensions={1}, to_apply=%copy.44.reduce_sub_computation | reduce | bytes 1179650 | tf_op jit(solution)/shard_map/reshape | solution.py:82
  72.2 1.1 %reshape.124 = bf16[64,2,2304]{2,1,0:T(2,128)(2,1)S(1)} reshape(bf16[1024,288]{1,0:T(8,128)(2,1)S(1)} %reduce) | data formatting | bytes 1179648
  73.3 25.1 %all_to_all.33 = bf16[64,2,2304]{2,1,0:T(2,128)(2,1)S(1)} all-to-all(bf16[64,2,2304]{2,1,0:T(2,128)(2,1)S(1)} %reshape.124), channel_id=1, replica_groups=mesh['energy'=64,'atoms'=4] {'energy'}, dimensions={0} | all-to-all | bytes 1179648 | tf_op jit(solution)/shard_map/all_to_all | solution.py:81
  98.4 1.4 %reshape.125 = bf16[1024,1,288]{2,1,0:T(2,128)(2,1)S(1)} reshape(bf16[64,2,2304]{2,1,0:T(2,128)(2,1)S(1)} %all_to_all.33) | data formatting | bytes 1179648
  99.8 0.1 copy.48
  100.0 1.1 %copy.45 = bf16[16,64,288]{2,1,0:T(8,128)(2,1)} copy(bf16[16,64,288]{2,0,1:T(8,128)(2,1)S(1)} %bitcast.22) | data formatting | bytes 1179648 | tf_op jit(solution)/shard_map/all_to_all | solution.py:81
  (13 shorter events, 0.3 us)
Async XLA Ops:
  0.0 25.3 %copy-start = (bf16[4,288,288]{2,1,0:T(8,128)(2,1)S(1)}, bf16[4,288,288]{2,1,0:T(8,128)(2,1)}, u32[]{:S(2)}) copy-start(bf16[4,288,288]{2,1,0:T(8,128)(2,1)} %param.6) | copy-start | bytes 1990660
  1.7 6.9 %collective-permute-start = (bf16[16,8,288]{2,0,1:T(8,128)(2,1)S(1)}, bf16[16,8,288]{2,0,1:T(8,128)(2,1)S(1)}, u32[]{:S(2)}, u32[]{:S(2)}) collective-permute-start(bf16[16,8,288]{2,0,1:T(8,128)(2,1)S(1)} %get-tuple-element.7), channel_id=1, source_target_pairs={{0,1},{1,2},{2,3},{4,5},{5,6},{6,7},{8,9},{9,10},{10,11},{12,13},{... | collective-permute-start | bytes 221192 | tf_op jit(solution)/shard_map/ppermute | solution.py:17
  5.7 5.4 %collective-permute-start.1 = (bf16[16,8,288]{2,0,1:T(8,128)(2,1)S(1)}, bf16[16,8,288]{2,0,1:T(8,128)(2,1)S(1)}, u32[]{:S(2)}, u32[]{:S(2)}) collective-permute-start(bf16[16,8,288]{2,0,1:T(8,128)(2,1)S(1)} %get-tuple-element.8), channel_id=1, source_target_pairs={{1,0},{2,1},{3,2},{5,4},{6,5},{7,6},{9,8},{10,9},{11,10},{13,12},{... | collective-permute-start | bytes 221192 | tf_op jit(solution)/shard_map/ppermute | solution.py:20
  25.3 16.6 %copy-start.2 = (bf16[64,2048]{1,0:T(8,128)(2,1)S(1)}, bf16[64,2048]{1,0:T(8,128)(2,1)}, u32[]{:S(2)}) copy-start(bf16[64,2048]{1,0:T(8,128)(2,1)} %param.7) | copy-start | bytes 786436
  26.7 17.7 %copy-start.3 = (s32[64,1]{0,1:T(1,128)S(1)}, s32[64,1]{0,1:T(1,128)}, u32[]{:S(2)}) copy-start(s32[64,1]{0,1:T(1,128)} %param.8) | copy-start | bytes 772
  28.1 36.5 %all-to-all-start = ((bf16[16,64,288]{2,0,1:T(8,128)(2,1)}), bf16[16,64,288]{2,0,1:T(8,128)(2,1)S(1)}, u32[]{:S(2)}, u32[]{:S(2)}) async-start(bf16[16,64,288]{2,0,1:T(8,128)(2,1)} %copy.42), calls=%async_computation | async-start | bytes 1572864 | tf_op jit(solution)/shard_map/all_to_all | solution.py:79
  64.6 0.9 copy-start.1

commit v2 on v1

--- a/solution.py
+++ b/solution.py
@@ -55,23 +55,49 @@
     )(domain, phonon_rev, columns)
 
 
+def neighbour_kernel(select_ref, widened_ref, superop_ref, out_ref):
+    energies, rows, comps = widened_ref.shape
+    atoms = select_ref.shape[1]
+    widened = widened_ref[...]
+    total = jnp.zeros((energies * atoms, comps), jnp.float32)
+    for slot in range(select_ref.shape[0]):
+        select = jnp.broadcast_to(select_ref[slot], (energies, atoms, rows))
+        picked = lax.dot_general(
+            select, widened, (((2,), (1,)), ((0,), (0,))), preferred_element_type=jnp.float32
+        )
+        picked = picked.astype(jnp.bfloat16).reshape(energies * atoms, comps)
+        total = total + jnp.dot(picked, superop_ref[slot], preferred_element_type=jnp.float32)
+    out_ref[...] = total.astype(out_ref.dtype).reshape(energies, atoms, comps)
+
+
+def neighbour_apply(select, widened, superop):
+    energies, rows, comps = widened.shape
+    slots, atoms, _ = select.shape
+    vmem = pl.BlockSpec(memory_space=pltpu.VMEM)
+    return pl.pallas_call(
+        neighbour_kernel,
+        out_shape=jax.ShapeDtypeStruct((energies, atoms, comps), jnp.bfloat16),
+        in_specs=[vmem, vmem, vmem],
+        out_specs=vmem,
+        cost_estimate=pl.CostEstimate(
+            flops=2 * slots * energies * atoms * comps * (rows + comps),
+            bytes_accessed=2 * (widened.size + superop.size + select.size + energies * atoms * comps),
+            transcendentals=0,
+        ),
+    )(select, widened, superop)
+
+
 def per_device(green, superop, phonon, owner, neighbours):
     local_energies = green.shape[0]
     group_size = green.shape[1]
     comps = green.shape[2]
-    slots = neighbours.shape[1]
     group = lax.axis_index("atoms")
     widened = padded(green, (("atoms", 1),), HALO)
     present = neighbours >= 0
-    target_rows = jnp.where(present, neighbours - group * group_size + HALO, 0)
-    picked = jnp.take(widened, target_rows.reshape(-1), axis=1)
-    picked = jnp.where(present.reshape(1, -1, 1), picked, jnp.zeros_like(picked))
-    coupled = jnp.dot(
-        picked.reshape(local_energies * group_size, slots * comps),
-        superop.reshape(slots * comps, comps),
-        preferred_element_type=jnp.float32,
-    )
-    coupled = coupled.reshape(local_energies, group_size, comps).astype(jnp.bfloat16)
+    target_rows = jnp.where(present, neighbours - group * group_size + HALO, -1)
+    rows = jnp.arange(widened.shape[1], dtype=jnp.int32)
+    select = (target_rows.T[:, :, None] == rows[None, None, :]).astype(jnp.bfloat16)
+    coupled = neighbour_apply(select, widened, superop)
     count = local_energies * lax.axis_size("energy")
     energy_rank = lax.axis_index("energy")
     mine = lax.dynamic_slice_in_dim(owner[:, 0], energy_rank * ATOMS_DEV, ATOMS_DEV)

time: 102 us -> 93.8 us (0.920)
  local copies, waits for them, and re-layouts: 23.1 us -> 11.8 us
  Pallas kernels: 3.97 us -> 9.28 us
  matrix products: 1.44 us -> 0 us
    select_n x3 -> x0, local copies, waits for them, and re-layouts: 8.26 us -> none  [the longest x2 8.17 us: per_device(): jnp.where(present.reshape(1, -1, 1), picked, jnp.zeros_like(picked))]
    pallas_call x0 -> x1, Pallas kernels: none -> 5.38 us  [neighbour_apply(): pl.pallas_call(neighbour_kernel, out_shape=jax.ShapeDtypeStruct((energies...]
    select_n x2 -> x0, other arithmetic: 3.19 us -> none  [the longest x1 3.18 us: per_device(): jnp.where(present.reshape(1, -1, 1), picked, jnp.zeros_like(picked))]
    gather x1 -> x0, local copies, waits for them, and re-layouts: 2.68 us -> none  [per_device(): picked = jnp.take(widened, target_rows.reshape(-1), axis=1)]
    pallas_call x0 -> x1, local copies, waits for them, and re-layouts: none -> 2.53 us  [neighbour_apply(): pl.pallas_call(neighbour_kernel, out_shape=jax.ShapeDtypeStruct((energies...]
    concatenate x1, other arithmetic: 0.2 us -> 2.2 us  [padded(): block = jnp.concatenate([low, block, high], axis=dim)]
    unnamed x12 -> x9, local copies, waits for them, and re-layouts: 5.21 us -> 3.53 us
    dot_general x1 -> x0, matrix products: 1.44 us -> none  [per_device(): jnp.dot(picked.reshape(local_energies * group_size, slots * comps), super...]
where the time goes in v2:
time: 93.8 us; the launch traced here: 93.3 us
  blocking collectives  25.1 us (27%)
  waiting for transfers between devices  22.2 us (24%)
  starting transfers between devices  19 us (20%)
  local copies, waits for them, and re-layouts  11.8 us (13%)
  Pallas kernels  9.28 us (10%)
  other arithmetic  5.88 us (6%)
    all_to_all x1, blocking collectives, per_device(): lax.all_to_all(product.reshape(count, ATOMS_DEV, comps), 'energy', split_...  25.1 us
    all_to_all x1, waiting for transfers between devices, per_device(): lax.all_to_all(coupled, 'energy', split_axis=1, concat_axis=0, tiled=True)  19.6 us
    all_to_all x1, starting transfers between devices, per_device(): lax.all_to_all(coupled, 'energy', split_axis=1, concat_axis=0, tiled=True)  13.8 us
    pallas_call x1, Pallas kernels, neighbour_apply(): pl.pallas_call(neighbour_kernel, out_shape=jax.ShapeDtypeStruct((energies...  5.38 us
    ppermute x1, starting transfers between devices, padded(): lax.ppermute(lax.slice_in_dim(block, block.shape[dim] - width, None, axis...  3.95 us
    pallas_call x1, Pallas kernels, toeplitz_apply(): pl.pallas_call(toeplitz_kernel, out_shape=jax.ShapeDtypeStruct((count, co...  3.9 us
    unnamed x9, local copies, waits for them, and re-layouts  3.53 us
    ppermute x1, waiting for transfers between devices, padded(): lax.ppermute(lax.slice_in_dim(block, 0, width, axis=dim), axis, backward)  2.63 us
  transfers between devices with their start and end apart: 3, of which 2 were waited for; matrix products, arithmetic and copies ran while one was open for 5% of the time, Pallas kernels for 0%

profile of v2, /device:TPU:1, one launch (start us, length us, event | category | flops | bytes accessed | tf_op | source)
XLA Modules:
  0.0 93.3 jit_solution(3832730317401277897)
XLA Ops:
  0.0 0.0 copy-start
  0.0 1.0 %fusion.1 = (bf16[16,8,288]{2,1,0:T(8,128)(2,1)S(1)}, bf16[16,8,288]{2,1,0:T(8,128)(2,1)S(1)}) fusion(bf16[16,64,288]{2,1,0:T(8,128)(2,1)} %param.5), kind=kLoop, calls=%fused_computation.5 | loop fusion | bytes 294912 | tf_op jit(solution)/shard_map/slice | solution.py:18
  1.0 4.0 %collective-permute-start = (bf16[16,8,288]{2,1,0:T(8,128)(2,1)S(1)}, bf16[16,8,288]{2,1,0:T(8,128)(2,1)S(1)}, u32[]{:S(2)}, u32[]{:S(2)}) collective-permute-start(bf16[16,8,288]{2,1,0:T(8,128)(2,1)S(1)} %get-tuple-element.5), channel_id=1, source_target_pairs={{0,1},{1,2},{2,3},{4,5},{5,6},{6,7},{8,9},{9,10},{10,11},{12,13},{... | collective-permute-start | bytes 221192 | tf_op jit(solution)/shard_map/ppermute | solution.py:17
  4.9 1.3 %collective-permute-start.1 = (bf16[16,8,288]{2,1,0:T(8,128)(2,1)S(1)}, bf16[16,8,288]{2,1,0:T(8,128)(2,1)S(1)}, u32[]{:S(2)}, u32[]{:S(2)}) collective-permute-start(bf16[16,8,288]{2,1,0:T(8,128)(2,1)S(1)} %get-tuple-element.6), channel_id=1, source_target_pairs={{1,0},{2,1},{3,2},{5,4},{6,5},{7,6},{9,8},{10,9},{11,10},{13,12},{... | collective-permute-start | bytes 221192 | tf_op jit(solution)/shard_map/ppermute | solution.py:20
  6.2 0.7 select_bitcast_fusion
  6.9 0.7 fusion.select_ref
  7.7 0.0 collective-permute-done
  7.7 2.6 %collective-permute-done.1 = bf16[16,8,288]{2,1,0:T(8,128)(2,1)S(1)} collective-permute-done((bf16[16,8,288]{2,1,0:T(8,128)(2,1)S(1)}, bf16[16,8,288]{2,1,0:T(8,128)(2,1)S(1)}, u32[]{:S(2)}, u32[]{:S(2)}) %collective-permute-start.1) | collective-permute-done | bytes 73760 | tf_op jit(solution)/shard_map/ppermute | solution.py:20
  10.3 2.2 %pad_maximum_fusion.widened_ref = bf16[16,80,288]{2,1,0:T(8,128)(2,1)} fusion(bf16[16,8,288]{2,1,0:T(8,128)(2,1)S(1)} %collective-permute-done.1, bf16[16,64,288]{2,1,0:T(8,128)(2,1)} %param.5, bf16[16,8,288]{2,1,0:T(8,128)(2,1)S(1)} %collective-permute-done), kind=kLoop, calls=%fused_computation | loop fusion | flops 2211840 | bytes 1474560 | tf_op jit(solution)/shard_map/concatenate | solution.py:21
  12.5 5.4 %shard_map.55 = bf16[16,64,288]{2,1,0:T(8,128)(2,1)} custom-call(bf16[4,64,80]{2,1,0:T(8,128)(2,1)} %fusion.select_ref, bf16[16,80,288]{2,1,0:T(8,128)(2,1)} %pad_maximum_fusion.widened_ref, bf16[4,288,288]{2,1,0:T(8,128)(2,1)} %superop_ref.1), custom_call_target="tpu_custom_call" | custom-call | flops 868220928 | bytes 2031616 | tf_op jit(solution)/shard_map/pallas_call | solution.py:77
  17.9 0.0 copy-start.2
  17.9 2.5 %copy.15 = bf16[16,64,288]{2,0,1:T(8,128)(2,1)} copy(bf16[16,64,288]{2,1,0:T(8,128)(2,1)} %shard_map.55) | data formatting | bytes 1179648 | tf_op jit(solution)/shard_map/pallas_call | solution.py:77
  20.4 13.8 %all-to-all-start = ((bf16[16,64,288]{2,0,1:T(8,128)(2,1)}), bf16[16,64,288]{2,0,1:T(8,128)(2,1)S(1)}, u32[]{:S(2)}, u32[]{:S(2)}) async-start(bf16[16,64,288]{2,0,1:T(8,128)(2,1)} %copy.15), calls=%async_computation | async-start | bytes 1572864 | tf_op jit(solution)/shard_map/all_to_all | solution.py:105
  34.2 0.0 copy-done.2
  34.2 1.4 %rev.3 = bf16[64,2048]{1,0:T(8,128)(2,1)S(1)} reverse(bf16[64,2048]{1,0:T(8,128)(2,1)S(1)} %copy-done.2), dimensions={1} | reverse | bytes 524288 | tf_op jit(solution)/shard_map/rev | solution.py:104
  35.6 1.2 %copy.16.phonon_ref = bf16[64,1,2048]{2,1,0:T(2,128)(2,1)} copy(bf16[64,1,2048]{2,0,1:T(8,128)(2,1)S(1)} %bitcast.16) | data formatting | bytes 524288 | tf_op jit(solution)/shard_map/reshape | solution.py:104
  36.8 0.0 copy-done
  36.8 0.6 constant_dynamic-slice_fusion
  37.3 19.6 %all-to-all-done = bf16[16,64,288]{2,0,1:T(8,128)(2,1)S(1)} async-done(((bf16[16,64,288]{2,0,1:T(8,128)(2,1)}), bf16[16,64,288]{2,0,1:T(8,128)(2,1)S(1)}, u32[]{:S(2)}, u32[]{:S(2)}) %all-to-all-start) | async-done | bytes 589856 | tf_op jit(solution)/shard_map/all_to_all | solution.py:105
  56.9 0.0 copy-start.1
  56.9 0.9 copy-done.1
  57.8 3.9 %shard_map.56 = bf16[1024,288]{1,0:T(8,128)(2,1)} custom-call(s32[1]{0:T(128)} %bitcast.domain_ref, bf16[64,1,2048]{2,1,0:T(2,128)(2,1)} %copy.16.phonon_ref, bf16[1024,288]{1,0:T(8,128)(2,1)} %bitcast.17), custom_call_target="tpu_custom_call" | custom-call | flops 603979776 | bytes 1183744 | tf_op jit(solution)/shard_map/pallas_call | solution.py:38
  61.7 0.5 broadcast.1
  62.2 2.3 %reduce = bf16[1024,288]{1,0:T(8,128)(2,1)S(1)} reduce(bf16[1024,1,288]{2,0,1:T(8,128)(2,1)} %bitcast.18, bf16[]{:T(256)} %broadcast.1), dimensions={1}, to_apply=%copy.17.reduce_sub_computation | reduce | bytes 1179650 | tf_op jit(solution)/shard_map/reshape | solution.py:108
  64.5 1.1 %reshape.15 = bf16[64,2,2304]{2,1,0:T(2,128)(2,1)S(1)} reshape(bf16[1024,288]{1,0:T(8,128)(2,1)S(1)} %reduce) | data formatting | bytes 1179648
  65.6 25.1 %all_to_all.33 = bf16[64,2,2304]{2,1,0:T(2,128)(2,1)S(1)} all-to-all(bf16[64,2,2304]{2,1,0:T(2,128)(2,1)S(1)} %reshape.15), channel_id=1, replica_groups=mesh['energy'=64,'atoms'=4] {'energy'}, dimensions={0} | all-to-all | bytes 1179648 | tf_op jit(solution)/shard_map/all_to_all | solution.py:107
  90.6 1.4 %reshape.16 = bf16[1024,1,288]{2,1,0:T(2,128)(2,1)S(1)} reshape(bf16[64,2,2304]{2,1,0:T(2,128)(2,1)S(1)} %all_to_all.33) | data formatting | bytes 1179648
  92.1 0.1 copy.19
  92.2 1.1 %copy.18 = bf16[16,64,288]{2,1,0:T(8,128)(2,1)} copy(bf16[16,64,288]{2,0,1:T(8,128)(2,1)S(1)} %bitcast.15) | data formatting | bytes 1179648 | tf_op jit(solution)/shard_map/all_to_all | solution.py:107
Async XLA Ops:
  0.0 36.8 %copy-start = (s32[64,1]{0,1:T(1,128)S(1)}, s32[64,1]{0,1:T(1,128)}, u32[]{:S(2)}) copy-start(s32[64,1]{0,1:T(1,128)} %param.8) | copy-start | bytes 772
  1.0 6.7 %collective-permute-start = (bf16[16,8,288]{2,1,0:T(8,128)(2,1)S(1)}, bf16[16,8,288]{2,1,0:T(8,128)(2,1)S(1)}, u32[]{:S(2)}, u32[]{:S(2)}) collective-permute-start(bf16[16,8,288]{2,1,0:T(8,128)(2,1)S(1)} %get-tuple-element.5), channel_id=1, source_target_pairs={{0,1},{1,2},{2,3},{4,5},{5,6},{6,7},{8,9},{9,10},{10,11},{12,13},{... | collective-permute-start | bytes 221192 | tf_op jit(solution)/shard_map/ppermute | solution.py:17
  4.9 5.4 %collective-permute-start.1 = (bf16[16,8,288]{2,1,0:T(8,128)(2,1)S(1)}, bf16[16,8,288]{2,1,0:T(8,128)(2,1)S(1)}, u32[]{:S(2)}, u32[]{:S(2)}) collective-permute-start(bf16[16,8,288]{2,1,0:T(8,128)(2,1)S(1)} %get-tuple-element.6), channel_id=1, source_target_pairs={{1,0},{2,1},{3,2},{5,4},{6,5},{7,6},{9,8},{10,9},{11,10},{13,12},{... | collective-permute-start | bytes 221192 | tf_op jit(solution)/shard_map/ppermute | solution.py:20
  17.9 16.3 %copy-start.2 = (bf16[64,2048]{1,0:T(8,128)(2,1)S(1)}, bf16[64,2048]{1,0:T(8,128)(2,1)}, u32[]{:S(2)}) copy-start(bf16[64,2048]{1,0:T(8,128)(2,1)} %param.7) | copy-start | bytes 786436
  20.4 36.5 %all-to-all-start = ((bf16[16,64,288]{2,0,1:T(8,128)(2,1)}), bf16[16,64,288]{2,0,1:T(8,128)(2,1)S(1)}, u32[]{:S(2)}, u32[]{:S(2)}) async-start(bf16[16,64,288]{2,0,1:T(8,128)(2,1)} %copy.15), calls=%async_computation | async-start | bytes 1572864 | tf_op jit(solution)/shard_map/all_to_all | solution.py:105
  56.9 0.9 copy-start.1

commit v3 on v2

--- a/solution.py
+++ b/solution.py
@@ -22,37 +22,35 @@
     return block
 
 
-def toeplitz_kernel(domain_ref, phonon_ref, columns_ref, out_ref):
+def toeplitz_kernel(owner_ref, phonon_ref, columns_ref, out_ref):
     count = columns_ref.shape[0]
-    row = phonon_ref[0].astype(jnp.float32)
+    domain = owner_ref[lax.axis_index("energy"), 0]
+    base = pl.multiple_of((domain // 16) * 16, 16)
+    block = phonon_ref[pl.ds(base, 16), :].astype(jnp.float32)
+    rows = lax.broadcasted_iota(jnp.int32, block.shape, 0)
+    row = jnp.sum(jnp.where(rows == domain - base, block, 0.0), axis=0, keepdims=True)
     wide = jnp.broadcast_to(row, (count, 2 * count))
-    rolled = pltpu.roll(wide, shift=count + 1, axis=1, stride=1, stride_axis=0)
-    kernel = rolled[:, :count].astype(jnp.bfloat16)
-    out_ref[...] = jnp.dot(
-        kernel, columns_ref[...], preferred_element_type=jnp.float32
+    rolled = pltpu.roll(wide, shift=count, axis=1, stride=1, stride_axis=0)
+    kernel_t = rolled[:, :count].astype(jnp.bfloat16)
+    out_ref[...] = lax.dot_general(
+        kernel_t, columns_ref[...], (((0,), (0,)), ((), ())), preferred_element_type=jnp.float32
     ).astype(out_ref.dtype)
 
 
-def toeplitz_apply(domain, phonon_rev, columns):
+def toeplitz_apply(owner, phonon, columns):
     count, comps = columns.shape
+    vmem = pl.BlockSpec(memory_space=pltpu.VMEM)
     return pl.pallas_call(
         toeplitz_kernel,
         out_shape=jax.ShapeDtypeStruct((count, comps), jnp.bfloat16),
-        grid_spec=pltpu.PrefetchScalarGridSpec(
-            num_scalar_prefetch=1,
-            grid=(1,),
-            in_specs=[
-                pl.BlockSpec((1, 1, 2 * count), lambda i, d: (d[0], 0, 0)),
-                pl.BlockSpec((count, comps), lambda i, d: (0, 0)),
-            ],
-            out_specs=pl.BlockSpec((count, comps), lambda i, d: (0, 0)),
-        ),
+        in_specs=[pl.BlockSpec(memory_space=pltpu.SMEM), vmem, vmem],
+        out_specs=vmem,
         cost_estimate=pl.CostEstimate(
             flops=2 * count * count * comps,
-            bytes_accessed=2 * (2 * count + 2 * count * comps),
+            bytes_accessed=2 * (phonon.size + 2 * count * comps),
             transcendentals=0,
         ),
-    )(domain, phonon_rev, columns)
+    )(owner, phonon, columns)
 
 
 def neighbour_kernel(select_ref, widened_ref, superop_ref, out_ref):
@@ -99,11 +97,8 @@
     select = (target_rows.T[:, :, None] == rows[None, None, :]).astype(jnp.bfloat16)
     coupled = neighbour_apply(select, widened, superop)
     count = local_energies * lax.axis_size("energy")
-    energy_rank = lax.axis_index("energy")
-    mine = lax.dynamic_slice_in_dim(owner[:, 0], energy_rank * ATOMS_DEV, ATOMS_DEV)
-    phonon_rev = phonon[:, ::-1].reshape(phonon.shape[0], 1, phonon.shape[1])
     columns = lax.all_to_all(coupled, "energy", split_axis=1, concat_axis=0, tiled=True)
-    product = toeplitz_apply(mine, phonon_rev, columns.reshape(count, comps))
+    product = toeplitz_apply(owner, phonon, columns.reshape(count, comps))
     result = lax.all_to_all(
         product.reshape(count, ATOMS_DEV, comps), "energy", split_axis=0, concat_axis=1, tiled=True
     )

time: 93.8 us -> 93.5 us (level)
  local copies, waits for them, and re-layouts: 11.8 us -> 9.25 us
  waiting for transfers between devices: 22.2 us -> 24.7 us
    all_to_all x1, waiting for transfers between devices: 19.6 us -> 22 us  [per_device(): lax.all_to_all(coupled, 'energy', split_axis=1, concat_axis=0, tiled=True)]
    rev x1 -> x0, local copies, waits for them, and re-layouts: 1.4 us -> none  [per_device(): phonon_rev = phonon[:, ::-1].reshape(phonon.shape[0], 1, phonon.shape[1])]
    reshape x1 -> x0, local copies, waits for them, and re-layouts: 1.2 us -> none  [per_device(): phonon_rev = phonon[:, ::-1].reshape(phonon.shape[0], 1, phonon.shape[1])]
    unnamed x9 -> x8, local copies, waits for them, and re-layouts: 3.53 us -> 4.23 us
  transfers between devices with their start and end apart: 3 -> 3, of which waited for: 2 -> 2; matrix products, arithmetic and copies ran while one was open for 5% -> 2% of each run, Pallas kernels for 0% -> 0%
where the time goes in v3:
time: 93.5 us; the launch traced here: 93.1 us
  blocking collectives  25.1 us (27%)
  waiting for transfers between devices  24.7 us (26%)
  starting transfers between devices  19 us (20%)
  local copies, waits for them, and re-layouts  9.25 us (10%)
  Pallas kernels  9.1 us (10%)
  other arithmetic  5.89 us (6%)
    all_to_all x1, blocking collectives, per_device(): lax.all_to_all(product.reshape(count, ATOMS_DEV, comps), 'energy', split_...  25.1 us
    all_to_all x1, waiting for transfers between devices, per_device(): lax.all_to_all(coupled, 'energy', split_axis=1, concat_axis=0, tiled=True)  22 us
    all_to_all x1, starting transfers between devices, per_device(): lax.all_to_all(coupled, 'energy', split_axis=1, concat_axis=0, tiled=True)  13.8 us
    pallas_call x1, Pallas kernels, neighbour_apply(): pl.pallas_call(neighbour_kernel, out_shape=jax.ShapeDtypeStruct((energies...  5.38 us
    unnamed x8, local copies, waits for them, and re-layouts  4.23 us
    ppermute x1, starting transfers between devices, padded(): lax.ppermute(lax.slice_in_dim(block, block.shape[dim] - width, None, axis...  3.95 us
    pallas_call x1, Pallas kernels, toeplitz_apply(): pl.pallas_call(toeplitz_kernel, out_shape=jax.ShapeDtypeStruct((count, co...  3.72 us
    ppermute x1, waiting for transfers between devices, padded(): lax.ppermute(lax.slice_in_dim(block, 0, width, axis=dim), axis, backward)  2.63 us
  transfers between devices with their start and end apart: 3, of which 2 were waited for; matrix products, arithmetic and copies ran while one was open for 2% of the time, Pallas kernels for 0%

profile of v3, /device:TPU:1, one launch (start us, length us, event | category | flops | bytes accessed | tf_op | source)
XLA Modules:
  0.0 93.1 jit_solution(16340293280469446030)
XLA Ops:
  0.0 1.0 %fusion.1 = (bf16[16,8,288]{2,1,0:T(8,128)(2,1)S(1)}, bf16[16,8,288]{2,1,0:T(8,128)(2,1)S(1)}) fusion(bf16[16,64,288]{2,1,0:T(8,128)(2,1)} %param.5), kind=kLoop, calls=%fused_computation.4 | loop fusion | bytes 294912 | tf_op jit(solution)/shard_map/slice | solution.py:18
  1.0 4.0 %collective-permute-start = (bf16[16,8,288]{2,1,0:T(8,128)(2,1)S(1)}, bf16[16,8,288]{2,1,0:T(8,128)(2,1)S(1)}, u32[]{:S(2)}, u32[]{:S(2)}) collective-permute-start(bf16[16,8,288]{2,1,0:T(8,128)(2,1)S(1)} %get-tuple-element.5), channel_id=1, source_target_pairs={{0,1},{1,2},{2,3},{4,5},{5,6},{6,7},{8,9},{9,10},{10,11},{12,13},{... | collective-permute-start | bytes 221192 | tf_op jit(solution)/shard_map/ppermute | solution.py:17
  4.9 1.3 %collective-permute-start.1 = (bf16[16,8,288]{2,1,0:T(8,128)(2,1)S(1)}, bf16[16,8,288]{2,1,0:T(8,128)(2,1)S(1)}, u32[]{:S(2)}, u32[]{:S(2)}) collective-permute-start(bf16[16,8,288]{2,1,0:T(8,128)(2,1)S(1)} %get-tuple-element.6), channel_id=1, source_target_pairs={{1,0},{2,1},{3,2},{5,4},{6,5},{7,6},{9,8},{10,9},{11,10},{13,12},{... | collective-permute-start | bytes 221192 | tf_op jit(solution)/shard_map/ppermute | solution.py:20
  6.2 0.7 select_bitcast_fusion
  6.9 0.7 fusion.select_ref
  7.7 0.0 collective-permute-done
  7.7 2.6 %collective-permute-done.1 = bf16[16,8,288]{2,1,0:T(8,128)(2,1)S(1)} collective-permute-done((bf16[16,8,288]{2,1,0:T(8,128)(2,1)S(1)}, bf16[16,8,288]{2,1,0:T(8,128)(2,1)S(1)}, u32[]{:S(2)}, u32[]{:S(2)}) %collective-permute-start.1) | collective-permute-done | bytes 73760 | tf_op jit(solution)/shard_map/ppermute | solution.py:20
  10.3 2.2 %pad_maximum_fusion.widened_ref = bf16[16,80,288]{2,1,0:T(8,128)(2,1)} fusion(bf16[16,8,288]{2,1,0:T(8,128)(2,1)S(1)} %collective-permute-done.1, bf16[16,64,288]{2,1,0:T(8,128)(2,1)} %param.5, bf16[16,8,288]{2,1,0:T(8,128)(2,1)S(1)} %collective-permute-done), kind=kLoop, calls=%fused_computation | loop fusion | flops 2211840 | bytes 1474560 | tf_op jit(solution)/shard_map/concatenate | solution.py:21
  12.5 5.4 %shard_map.55 = bf16[16,64,288]{2,1,0:T(8,128)(2,1)} custom-call(bf16[4,64,80]{2,1,0:T(8,128)(2,1)} %fusion.select_ref, bf16[16,80,288]{2,1,0:T(8,128)(2,1)} %pad_maximum_fusion.widened_ref, bf16[4,288,288]{2,1,0:T(8,128)(2,1)} %superop_ref.1), custom_call_target="tpu_custom_call" | custom-call | flops 868220928 | bytes 2031616 | tf_op jit(solution)/shard_map/pallas_call | solution.py:75
  17.9 0.0 copy-start.1
  17.9 2.5 %copy.13 = bf16[16,64,288]{2,0,1:T(8,128)(2,1)} copy(bf16[16,64,288]{2,1,0:T(8,128)(2,1)} %shard_map.55) | data formatting | bytes 1179648 | tf_op jit(solution)/shard_map/pallas_call | solution.py:75
  20.4 13.8 %all-to-all-start = ((bf16[16,64,288]{2,0,1:T(8,128)(2,1)}), bf16[16,64,288]{2,0,1:T(8,128)(2,1)S(1)}, u32[]{:S(2)}, u32[]{:S(2)}) async-start(bf16[16,64,288]{2,0,1:T(8,128)(2,1)} %copy.13), calls=%async_computation | async-start | bytes 1572864 | tf_op jit(solution)/shard_map/all_to_all | solution.py:100
  34.1 0.0 copy-done.1
  34.1 0.7 copy.14.owner_ref
  34.8 22.0 %all-to-all-done = bf16[16,64,288]{2,0,1:T(8,128)(2,1)S(1)} async-done(((bf16[16,64,288]{2,0,1:T(8,128)(2,1)}), bf16[16,64,288]{2,0,1:T(8,128)(2,1)S(1)}, u32[]{:S(2)}, u32[]{:S(2)}) %all-to-all-start) | async-done | bytes 589856 | tf_op jit(solution)/shard_map/all_to_all | solution.py:100
  56.9 0.0 copy-start
  56.9 0.9 copy-done
  57.8 3.7 %shard_map.56 = bf16[1024,288]{1,0:T(8,128)(2,1)} custom-call(s32[64,1]{1,0:T(8,128)} %copy.14.owner_ref, bf16[64,2048]{1,0:T(8,128)(2,1)} %phonon_ref.1, bf16[1024,288]{1,0:T(8,128)(2,1)} %bitcast.14), custom_call_target="tpu_custom_call" | custom-call | flops 603979776 | bytes 1441792 | tf_op jit(solution)/shard_map/pallas_call | solution.py:43
  61.5 0.5 broadcast.1
  62.0 2.3 %reduce = bf16[1024,288]{1,0:T(8,128)(2,1)S(1)} reduce(bf16[1024,1,288]{2,0,1:T(8,128)(2,1)} %bitcast.15, bf16[]{:T(256)} %broadcast.1), dimensions={1}, to_apply=%copy.15.reduce_sub_computation | reduce | bytes 1179650 | tf_op jit(solution)/shard_map/reshape | solution.py:103
  64.3 1.1 %reshape.10 = bf16[64,2,2304]{2,1,0:T(2,128)(2,1)S(1)} reshape(bf16[1024,288]{1,0:T(8,128)(2,1)S(1)} %reduce) | data formatting | bytes 1179648
  65.3 25.1 %all_to_all.33 = bf16[64,2,2304]{2,1,0:T(2,128)(2,1)S(1)} all-to-all(bf16[64,2,2304]{2,1,0:T(2,128)(2,1)S(1)} %reshape.10), channel_id=1, replica_groups=mesh['energy'=64,'atoms'=4] {'energy'}, dimensions={0} | all-to-all | bytes 1179648 | tf_op jit(solution)/shard_map/all_to_all | solution.py:102
  90.4 1.4 %reshape.11 = bf16[1024,1,288]{2,1,0:T(2,128)(2,1)S(1)} reshape(bf16[64,2,2304]{2,1,0:T(2,128)(2,1)S(1)} %all_to_all.33) | data formatting | bytes 1179648
  91.9 0.1 copy.17
  92.0 1.1 %copy.16 = bf16[16,64,288]{2,1,0:T(8,128)(2,1)} copy(bf16[16,64,288]{2,0,1:T(8,128)(2,1)S(1)} %bitcast.13) | data formatting | bytes 1179648 | tf_op jit(solution)/shard_map/all_to_all | solution.py:102
Async XLA Ops:
  1.0 6.7 %collective-permute-start = (bf16[16,8,288]{2,1,0:T(8,128)(2,1)S(1)}, bf16[16,8,288]{2,1,0:T(8,128)(2,1)S(1)}, u32[]{:S(2)}, u32[]{:S(2)}) collective-permute-start(bf16[16,8,288]{2,1,0:T(8,128)(2,1)S(1)} %get-tuple-element.5), channel_id=1, source_target_pairs={{0,1},{1,2},{2,3},{4,5},{5,6},{6,7},{8,9},{9,10},{10,11},{12,13},{... | collective-permute-start | bytes 221192 | tf_op jit(solution)/shard_map/ppermute | solution.py:17
  4.9 5.4 %collective-permute-start.1 = (bf16[16,8,288]{2,1,0:T(8,128)(2,1)S(1)}, bf16[16,8,288]{2,1,0:T(8,128)(2,1)S(1)}, u32[]{:S(2)}, u32[]{:S(2)}) collective-permute-start(bf16[16,8,288]{2,1,0:T(8,128)(2,1)S(1)} %get-tuple-element.6), channel_id=1, source_target_pairs={{1,0},{2,1},{3,2},{5,4},{6,5},{7,6},{9,8},{10,9},{11,10},{13,12},{... | collective-permute-start | bytes 221192 | tf_op jit(solution)/shard_map/ppermute | solution.py:20
  17.9 16.3 %copy-start.1 = (s32[64,1]{0,1:T(1,128)S(1)}, s32[64,1]{0,1:T(1,128)}, u32[]{:S(2)}) copy-start(s32[64,1]{0,1:T(1,128)} %param.8) | copy-start | bytes 772
  20.4 36.5 %all-to-all-start = ((bf16[16,64,288]{2,0,1:T(8,128)(2,1)}), bf16[16,64,288]{2,0,1:T(8,128)(2,1)S(1)}, u32[]{:S(2)}, u32[]{:S(2)}) async-start(bf16[16,64,288]{2,0,1:T(8,128)(2,1)} %copy.13), calls=%async_computation | async-start | bytes 1572864 | tf_op jit(solution)/shard_map/all_to_all | solution.py:100
  56.9 0.9 copy-start

commit v4 on v3

--- a/solution.py
+++ b/solution.py
@@ -97,7 +97,9 @@
     select = (target_rows.T[:, :, None] == rows[None, None, :]).astype(jnp.bfloat16)
     coupled = neighbour_apply(select, widened, superop)
     count = local_energies * lax.axis_size("energy")
-    columns = lax.all_to_all(coupled, "energy", split_axis=1, concat_axis=0, tiled=True)
+    peers = lax.axis_size("energy")
+    outgoing = jnp.transpose(coupled, (1, 0, 2)).reshape(peers, 2, local_energies * comps // 2)
+    columns = lax.all_to_all(outgoing, "energy", split_axis=0, concat_axis=0, tiled=True)
     product = toeplitz_apply(owner, phonon, columns.reshape(count, comps))
     result = lax.all_to_all(
         product.reshape(count, ATOMS_DEV, comps), "energy", split_axis=0, concat_axis=1, tiled=True

time: 93.5 us -> 91.5 us (0.979)
  waiting for transfers between devices: 24.7 us -> 21 us
  local copies, waits for them, and re-layouts: 9.25 us -> 11.4 us
    reshape x0 -> x2, local copies, waits for them, and re-layouts: none -> 3.93 us  [the longest x1 2.05 us: per_device(): product = toeplitz_apply(owner, phonon, columns.reshape(count, comps))]
    all_to_all x1, waiting for transfers between devices: 22 us -> 18.3 us  [per_device(): lax.all_to_all(outgoing, 'energy', split_axis=0, concat_axis=0, tiled=True)]
    pallas_call x1 -> x0, local copies, waits for them, and re-layouts: 2.49 us -> none  [neighbour_apply(): pl.pallas_call(neighbour_kernel, out_shape=jax.ShapeDtypeStruct((energies...]
    transpose x0 -> x1, local copies, waits for them, and re-layouts: none -> 1.59 us  [per_device(): jnp.transpose(coupled, (1, 0, 2))]
    unnamed x8 -> x6, local copies, waits for them, and re-layouts: 4.23 us -> 3.34 us
where the time goes in v4:
time: 91.5 us; the launch traced here: 91 us
  blocking collectives  24.6 us (27%)
  waiting for transfers between devices  21 us (23%)
  starting transfers between devices  19 us (21%)
  local copies, waits for them, and re-layouts  11.4 us (12%)
  Pallas kernels  9.09 us (10%)
  other arithmetic  5.88 us (6%)
    all_to_all x1, blocking collectives, per_device(): lax.all_to_all(product.reshape(count, ATOMS_DEV, comps), 'energy', split_...  24.6 us
    all_to_all x1, waiting for transfers between devices, per_device(): lax.all_to_all(outgoing, 'energy', split_axis=0, concat_axis=0, tiled=True)  18.3 us
    all_to_all x1, starting transfers between devices, per_device(): lax.all_to_all(outgoing, 'energy', split_axis=0, concat_axis=0, tiled=True)  13.8 us
    pallas_call x1, Pallas kernels, neighbour_apply(): pl.pallas_call(neighbour_kernel, out_shape=jax.ShapeDtypeStruct((energies...  5.38 us
    ppermute x1, starting transfers between devices, padded(): lax.ppermute(lax.slice_in_dim(block, block.shape[dim] - width, None, axis...  3.95 us
    pallas_call x1, Pallas kernels, toeplitz_apply(): pl.pallas_call(toeplitz_kernel, out_shape=jax.ShapeDtypeStruct((count, co...  3.71 us
    unnamed x6, local copies, waits for them, and re-layouts  3.34 us
    ppermute x1, waiting for transfers between devices, padded(): lax.ppermute(lax.slice_in_dim(block, 0, width, axis=dim), axis, backward)  2.64 us
  transfers between devices with their start and end apart: 3, of which 2 were waited for; matrix products, arithmetic and copies ran while one was open for 2% of the time, Pallas kernels for 0%

profile of v4, /device:TPU:1, one launch (start us, length us, event | category | flops | bytes accessed | tf_op | source)
XLA Modules:
  0.0 91.0 jit_solution(1723655027781820248)
XLA Ops:
  0.0 1.0 %fusion.1 = (bf16[16,8,288]{2,1,0:T(8,128)(2,1)S(1)}, bf16[16,8,288]{2,1,0:T(8,128)(2,1)S(1)}) fusion(bf16[16,64,288]{2,1,0:T(8,128)(2,1)} %param.5), kind=kLoop, calls=%fused_computation.4 | loop fusion | bytes 294912 | tf_op jit(solution)/shard_map/slice | solution.py:18
  1.0 4.0 %collective-permute-start = (bf16[16,8,288]{2,1,0:T(8,128)(2,1)S(1)}, bf16[16,8,288]{2,1,0:T(8,128)(2,1)S(1)}, u32[]{:S(2)}, u32[]{:S(2)}) collective-permute-start(bf16[16,8,288]{2,1,0:T(8,128)(2,1)S(1)} %get-tuple-element.5), channel_id=1, source_target_pairs={{0,1},{1,2},{2,3},{4,5},{5,6},{6,7},{8,9},{9,10},{10,11},{12,13},{... | collective-permute-start | bytes 221192 | tf_op jit(solution)/shard_map/ppermute | solution.py:17
  4.9 1.3 %collective-permute-start.1 = (bf16[16,8,288]{2,1,0:T(8,128)(2,1)S(1)}, bf16[16,8,288]{2,1,0:T(8,128)(2,1)S(1)}, u32[]{:S(2)}, u32[]{:S(2)}) collective-permute-start(bf16[16,8,288]{2,1,0:T(8,128)(2,1)S(1)} %get-tuple-element.6), channel_id=1, source_target_pairs={{1,0},{2,1},{3,2},{5,4},{6,5},{7,6},{9,8},{10,9},{11,10},{13,12},{... | collective-permute-start | bytes 221192 | tf_op jit(solution)/shard_map/ppermute | solution.py:20
  6.2 0.7 select_bitcast_fusion
  6.9 0.7 fusion.select_ref
  7.6 0.0 collective-permute-done
  7.6 2.6 %collective-permute-done.1 = bf16[16,8,288]{2,1,0:T(8,128)(2,1)S(1)} collective-permute-done((bf16[16,8,288]{2,1,0:T(8,128)(2,1)S(1)}, bf16[16,8,288]{2,1,0:T(8,128)(2,1)S(1)}, u32[]{:S(2)}, u32[]{:S(2)}) %collective-permute-start.1) | collective-permute-done | bytes 73760 | tf_op jit(solution)/shard_map/ppermute | solution.py:20
  10.3 2.2 %pad_maximum_fusion.widened_ref = bf16[16,80,288]{2,1,0:T(8,128)(2,1)} fusion(bf16[16,8,288]{2,1,0:T(8,128)(2,1)S(1)} %collective-permute-done.1, bf16[16,64,288]{2,1,0:T(8,128)(2,1)} %param.5, bf16[16,8,288]{2,1,0:T(8,128)(2,1)S(1)} %collective-permute-done), kind=kLoop, calls=%fused_computation | loop fusion | flops 2211840 | bytes 1474560 | tf_op jit(solution)/shard_map/concatenate | solution.py:21
  12.5 5.4 %shard_map.55 = bf16[16,64,288]{2,1,0:T(8,128)(2,1)} custom-call(bf16[4,64,80]{2,1,0:T(8,128)(2,1)} %fusion.select_ref, bf16[16,80,288]{2,1,0:T(8,128)(2,1)} %pad_maximum_fusion.widened_ref, bf16[4,288,288]{2,1,0:T(8,128)(2,1)} %superop_ref.1), custom_call_target="tpu_custom_call" | custom-call | flops 868220928 | bytes 2031616 | tf_op jit(solution)/shard_map/pallas_call | solution.py:75
  17.9 1.6 %copy.15 = bf16[64,16,288]{2,1,0:T(8,128)(2,1)S(1)} copy(bf16[64,16,288]{2,0,1:T(8,128)(2,1)} %bitcast.11) | data formatting | bytes 1179648 | tf_op jit(solution)/shard_map/transpose | solution.py:101
  19.5 0.0 copy-start
  19.5 1.9 %reshape.10 = bf16[64,2,2304]{2,1,0:T(2,128)(2,1)} reshape(bf16[64,16,288]{2,1,0:T(8,128)(2,1)S(1)} %copy.15) | data formatting | bytes 1179648 | tf_op jit(solution)/shard_map/reshape | solution.py:101
  21.4 13.8 %all-to-all-start = ((bf16[64,2,2304]{2,1,0:T(2,128)(2,1)}), bf16[64,2,2304]{2,1,0:T(2,128)(2,1)S(1)}, u32[]{:S(2)}, u32[]{:S(2)}) async-start(bf16[64,2,2304]{2,1,0:T(2,128)(2,1)} %reshape.10), calls=%async_computation | async-start | bytes 1179648 | tf_op jit(solution)/shard_map/all_to_all | solution.py:102
  35.1 0.0 copy-done
  35.1 0.7 copy.16.owner_ref
  35.8 18.3 %all-to-all-done = bf16[64,2,2304]{2,1,0:T(2,128)(2,1)S(1)} async-done(((bf16[64,2,2304]{2,1,0:T(2,128)(2,1)}), bf16[64,2,2304]{2,1,0:T(2,128)(2,1)S(1)}, u32[]{:S(2)}, u32[]{:S(2)}) %all-to-all-start) | async-done | bytes 589856 | tf_op jit(solution)/shard_map/all_to_all | solution.py:102
  54.2 2.0 %reshape.11.columns_ref = bf16[1024,288]{1,0:T(8,128)(2,1)} reshape(bf16[64,2,2304]{2,1,0:T(2,128)(2,1)S(1)} %all-to-all-done) | data formatting | bytes 1179648 | tf_op jit(solution)/shard_map/reshape | solution.py:103
  56.2 3.7 %shard_map.56 = bf16[1024,288]{1,0:T(8,128)(2,1)} custom-call(s32[64,1]{1,0:T(8,128)} %copy.16.owner_ref, bf16[64,2048]{1,0:T(8,128)(2,1)} %phonon_ref.1, bf16[1024,288]{1,0:T(8,128)(2,1)} %reshape.11.columns_ref), custom_call_target="tpu_custom_call" | custom-call | flops 603979776 | bytes 1441792 | tf_op jit(solution)/shard_map/pallas_call | solution.py:43
  59.9 0.5 broadcast.1
  60.4 2.3 %reduce = bf16[1024,288]{1,0:T(8,128)(2,1)S(1)} reduce(bf16[1024,1,288]{2,0,1:T(8,128)(2,1)} %bitcast.10, bf16[]{:T(256)} %broadcast.1), dimensions={1}, to_apply=%copy.17.reduce_sub_computation | reduce | bytes 1179650 | tf_op jit(solution)/shard_map/reshape | solution.py:105
  62.7 1.1 %reshape.13 = bf16[64,2,2304]{2,1,0:T(2,128)(2,1)S(1)} reshape(bf16[1024,288]{1,0:T(8,128)(2,1)S(1)} %reduce) | data formatting | bytes 1179648
  63.8 24.6 %all_to_all.23 = bf16[64,2,2304]{2,1,0:T(2,128)(2,1)S(1)} all-to-all(bf16[64,2,2304]{2,1,0:T(2,128)(2,1)S(1)} %reshape.13), channel_id=1, replica_groups=mesh['energy'=64,'atoms'=4] {'energy'}, dimensions={0} | all-to-all | bytes 1179648 | tf_op jit(solution)/shard_map/all_to_all | solution.py:104
  88.4 1.4 %reshape.14 = bf16[1024,1,288]{2,1,0:T(2,128)(2,1)S(1)} reshape(bf16[64,2,2304]{2,1,0:T(2,128)(2,1)S(1)} %all_to_all.23) | data formatting | bytes 1179648
  89.9 0.1 copy.19
  90.0 1.1 %copy.18 = bf16[16,64,288]{2,1,0:T(8,128)(2,1)} copy(bf16[16,64,288]{2,0,1:T(8,128)(2,1)S(1)} %bitcast.9) | data formatting | bytes 1179648 | tf_op jit(solution)/shard_map/all_to_all | solution.py:104
Async XLA Ops:
  1.0 6.7 %collective-permute-start = (bf16[16,8,288]{2,1,0:T(8,128)(2,1)S(1)}, bf16[16,8,288]{2,1,0:T(8,128)(2,1)S(1)}, u32[]{:S(2)}, u32[]{:S(2)}) collective-permute-start(bf16[16,8,288]{2,1,0:T(8,128)(2,1)S(1)} %get-tuple-element.5), channel_id=1, source_target_pairs={{0,1},{1,2},{2,3},{4,5},{5,6},{6,7},{8,9},{9,10},{10,11},{12,13},{... | collective-permute-start | bytes 221192 | tf_op jit(solution)/shard_map/ppermute | solution.py:17
  4.9 5.4 %collective-permute-start.1 = (bf16[16,8,288]{2,1,0:T(8,128)(2,1)S(1)}, bf16[16,8,288]{2,1,0:T(8,128)(2,1)S(1)}, u32[]{:S(2)}, u32[]{:S(2)}) collective-permute-start(bf16[16,8,288]{2,1,0:T(8,128)(2,1)S(1)} %get-tuple-element.6), channel_id=1, source_target_pairs={{1,0},{2,1},{3,2},{5,4},{6,5},{7,6},{9,8},{10,9},{11,10},{13,12},{... | collective-permute-start | bytes 221192 | tf_op jit(solution)/shard_map/ppermute | solution.py:20
  19.5 15.7 %copy-start = (s32[64,1]{0,1:T(1,128)S(1)}, s32[64,1]{0,1:T(1,128)}, u32[]{:S(2)}) copy-start(s32[64,1]{0,1:T(1,128)} %param.8) | copy-start | bytes 772
  21.4 32.8 %all-to-all-start = ((bf16[64,2,2304]{2,1,0:T(2,128)(2,1)}), bf16[64,2,2304]{2,1,0:T(2,128)(2,1)S(1)}, u32[]{:S(2)}, u32[]{:S(2)}) async-start(bf16[64,2,2304]{2,1,0:T(2,128)(2,1)} %reshape.10), calls=%async_computation | async-start | bytes 1179648 | tf_op jit(solution)/shard_map/all_to_all | solution.py:102

commit v5 on v4

--- a/solution.py
+++ b/solution.py
@@ -24,7 +24,7 @@
 
 def toeplitz_kernel(owner_ref, phonon_ref, columns_ref, out_ref):
     count = columns_ref.shape[0]
-    domain = owner_ref[lax.axis_index("energy"), 0]
+    domain = owner_ref[0]
     base = pl.multiple_of((domain // 16) * 16, 16)
     block = phonon_ref[pl.ds(base, 16), :].astype(jnp.float32)
     rows = lax.broadcasted_iota(jnp.int32, block.shape, 0)
@@ -99,8 +99,10 @@
     count = local_energies * lax.axis_size("energy")
     peers = lax.axis_size("energy")
     outgoing = jnp.transpose(coupled, (1, 0, 2)).reshape(peers, 2, local_energies * comps // 2)
+    mine = lax.dynamic_slice_in_dim(owner[:, 0], lax.axis_index("energy"), 1)
+    mine, outgoing = lax.optimization_barrier((mine, outgoing))
     columns = lax.all_to_all(outgoing, "energy", split_axis=0, concat_axis=0, tiled=True)
-    product = toeplitz_apply(owner, phonon, columns.reshape(count, comps))
+    product = toeplitz_apply(mine, phonon, columns.reshape(count, comps))
     result = lax.all_to_all(
         product.reshape(count, ATOMS_DEV, comps), "energy", split_axis=0, concat_axis=1, tiled=True
     )

time: 91.5 us -> 91.1 us (level)
  blocking collectives: 24.6 us -> 57.2 us
  waiting for transfers between devices: 21 us -> 2.04 us
  starting transfers between devices: 19 us -> 5.24 us
    all_to_all x0 -> x1, blocking collectives: none -> 32.6 us  [per_device(): lax.all_to_all(outgoing, 'energy', split_axis=0, concat_axis=0, tiled=True)]
    all_to_all x1 -> x0, waiting for transfers between devices: 18.3 us -> none  [per_device(): lax.all_to_all(outgoing, 'energy', split_axis=0, concat_axis=0, tiled=True)]
    all_to_all x1 -> x0, starting transfers between devices: 13.8 us -> none  [per_device(): lax.all_to_all(outgoing, 'energy', split_axis=0, concat_axis=0, tiled=True)]
    unnamed x6 -> x5, local copies, waits for them, and re-layouts: 3.34 us -> 2.65 us
  transfers between devices with their start and end apart: 3 -> 2, of which waited for: 2 -> 1; matrix products, arithmetic and copies ran while one was open for 2% -> 2% of each run, Pallas kernels for 0% -> 0%
where the time goes in v5:
time: 91.1 us; the launch traced here: 90.6 us
  blocking collectives  57.2 us (63%)
  local copies, waits for them, and re-layouts  10.5 us (12%)
  Pallas kernels  9.69 us (11%)
  other arithmetic  5.86 us (6%)
  starting transfers between devices  5.24 us (6%)
  waiting for transfers between devices  2.04 us (2%)
    all_to_all x1, blocking collectives, per_device(): lax.all_to_all(outgoing, 'energy', split_axis=0, concat_axis=0, tiled=True)  32.6 us
    all_to_all x1, blocking collectives, per_device(): lax.all_to_all(product.reshape(count, ATOMS_DEV, comps), 'energy', split_...  24.6 us
    pallas_call x1, Pallas kernels, neighbour_apply(): pl.pallas_call(neighbour_kernel, out_shape=jax.ShapeDtypeStruct((energies...  5.38 us
    pallas_call x1, Pallas kernels, toeplitz_apply(): pl.pallas_call(toeplitz_kernel, out_shape=jax.ShapeDtypeStruct((count, co...  4.31 us
    ppermute x1, starting transfers between devices, padded(): lax.ppermute(lax.slice_in_dim(block, block.shape[dim] - width, None, axis...  3.95 us
    unnamed x5, local copies, waits for them, and re-layouts  2.65 us
    reshape x1, other arithmetic, per_device(): product.reshape(count, ATOMS_DEV, comps)  2.26 us
    concatenate x1, other arithmetic, padded(): block = jnp.concatenate([low, block, high], axis=dim)  2.2 us
  transfers between devices with their start and end apart: 2, of which 1 were waited for; matrix products, arithmetic and copies ran while one was open for 2% of the time, Pallas kernels for 0%

profile of v5, /device:TPU:1, one launch (start us, length us, event | category | flops | bytes accessed | tf_op | source)
XLA Modules:
  0.0 90.6 jit_solution(16347409639034923408)
XLA Ops:
  0.0 0.0 copy-start
  0.0 1.0 %fusion.1 = (bf16[16,8,288]{2,1,0:T(8,128)(2,1)S(1)}, bf16[16,8,288]{2,1,0:T(8,128)(2,1)S(1)}) fusion(bf16[16,64,288]{2,1,0:T(8,128)(2,1)} %param.5), kind=kLoop, calls=%fused_computation.5 | loop fusion | bytes 294912 | tf_op jit(solution)/shard_map/slice | solution.py:18
  1.0 4.0 %collective-permute-start = (bf16[16,8,288]{2,1,0:T(8,128)(2,1)S(1)}, bf16[16,8,288]{2,1,0:T(8,128)(2,1)S(1)}, u32[]{:S(2)}, u32[]{:S(2)}) collective-permute-start(bf16[16,8,288]{2,1,0:T(8,128)(2,1)S(1)} %get-tuple-element.9), channel_id=1, source_target_pairs={{0,1},{1,2},{2,3},{4,5},{5,6},{6,7},{8,9},{9,10},{10,11},{12,13},{... | collective-permute-start | bytes 221192 | tf_op jit(solution)/shard_map/ppermute | solution.py:17
  4.9 1.3 %collective-permute-start.1 = (bf16[16,8,288]{2,1,0:T(8,128)(2,1)S(1)}, bf16[16,8,288]{2,1,0:T(8,128)(2,1)S(1)}, u32[]{:S(2)}, u32[]{:S(2)}) collective-permute-start(bf16[16,8,288]{2,1,0:T(8,128)(2,1)S(1)} %get-tuple-element.10), channel_id=1, source_target_pairs={{1,0},{2,1},{3,2},{5,4},{6,5},{7,6},{9,8},{10,9},{11,10},{13,12},{... | collective-permute-start | bytes 221192 | tf_op jit(solution)/shard_map/ppermute | solution.py:20
  6.2 0.7 select_bitcast_fusion
  6.9 0.7 fusion.select_ref
  7.7 0.0 copy-done
  7.7 0.6 constant_dynamic-slice_fusion
  8.3 0.0 collective-permute-done
  8.3 2.0 %collective-permute-done.1 = bf16[16,8,288]{2,1,0:T(8,128)(2,1)S(1)} collective-permute-done((bf16[16,8,288]{2,1,0:T(8,128)(2,1)S(1)}, bf16[16,8,288]{2,1,0:T(8,128)(2,1)S(1)}, u32[]{:S(2)}, u32[]{:S(2)}) %collective-permute-start.1) | collective-permute-done | bytes 73760 | tf_op jit(solution)/shard_map/ppermute | solution.py:20
  10.3 2.2 %pad_maximum_fusion.widened_ref = bf16[16,80,288]{2,1,0:T(8,128)(2,1)} fusion(bf16[16,8,288]{2,1,0:T(8,128)(2,1)S(1)} %collective-permute-done.1, bf16[16,64,288]{2,1,0:T(8,128)(2,1)} %param.5, bf16[16,8,288]{2,1,0:T(8,128)(2,1)S(1)} %collective-permute-done), kind=kLoop, calls=%fused_computation | loop fusion | flops 2211840 | bytes 1474560 | tf_op jit(solution)/shard_map/concatenate | solution.py:21
  12.5 5.4 %shard_map.55 = bf16[16,64,288]{2,1,0:T(8,128)(2,1)} custom-call(bf16[4,64,80]{2,1,0:T(8,128)(2,1)} %fusion.select_ref, bf16[16,80,288]{2,1,0:T(8,128)(2,1)} %pad_maximum_fusion.widened_ref, bf16[4,288,288]{2,1,0:T(8,128)(2,1)} %superop_ref.1), custom_call_target="tpu_custom_call" | custom-call | flops 868220928 | bytes 2031616 | tf_op jit(solution)/shard_map/pallas_call | solution.py:75
  17.9 1.6 %copy.12 = bf16[64,16,288]{2,1,0:T(8,128)(2,1)S(1)} copy(bf16[64,16,288]{2,0,1:T(8,128)(2,1)} %bitcast.12) | data formatting | bytes 1179648 | tf_op jit(solution)/shard_map/transpose | solution.py:101
  19.5 1.1 %reshape.11 = bf16[64,2,2304]{2,1,0:T(2,128)(2,1)S(1)} reshape(bf16[64,16,288]{2,1,0:T(8,128)(2,1)S(1)} %copy.12) | data formatting | bytes 1179648 | tf_op jit(solution)/shard_map/reshape | solution.py:101
  20.5 32.6 %all_to_all.23 = bf16[64,2,2304]{2,1,0:T(2,128)(2,1)S(1)} all-to-all(bf16[64,2,2304]{2,1,0:T(2,128)(2,1)S(1)} %reshape.11), channel_id=1, replica_groups=mesh['energy'=64,'atoms'=4] {'energy'}, dimensions={0} | all-to-all | bytes 1179648 | tf_op jit(solution)/shard_map/all_to_all | solution.py:104
  53.1 2.0 %reshape.12.columns_ref = bf16[1024,288]{1,0:T(8,128)(2,1)} reshape(bf16[64,2,2304]{2,1,0:T(2,128)(2,1)S(1)} %all_to_all.23) | data formatting | bytes 1179648 | tf_op jit(solution)/shard_map/reshape | solution.py:105
  55.2 4.3 %shard_map.56 = bf16[1024,288]{1,0:T(8,128)(2,1)} custom-call(s32[1]{0:T(128)} %bitcast.owner_ref, bf16[64,2048]{1,0:T(8,128)(2,1)} %phonon_ref.1, bf16[1024,288]{1,0:T(8,128)(2,1)} %reshape.12.columns_ref), custom_call_target="tpu_custom_call" | custom-call | flops 603979776 | bytes 1441792 | tf_op jit(solution)/shard_map/pallas_call | solution.py:43
  59.5 0.5 broadcast.1
  60.0 2.3 %reduce = bf16[1024,288]{1,0:T(8,128)(2,1)S(1)} reduce(bf16[1024,1,288]{2,0,1:T(8,128)(2,1)} %bitcast.11, bf16[]{:T(256)} %broadcast.1), dimensions={1}, to_apply=%copy.13.reduce_sub_computation | reduce | bytes 1179650 | tf_op jit(solution)/shard_map/reshape | solution.py:107
  62.3 1.1 %reshape.14 = bf16[64,2,2304]{2,1,0:T(2,128)(2,1)S(1)} reshape(bf16[1024,288]{1,0:T(8,128)(2,1)S(1)} %reduce) | data formatting | bytes 1179648
  63.3 24.6 %all_to_all.24 = bf16[64,2,2304]{2,1,0:T(2,128)(2,1)S(1)} all-to-all(bf16[64,2,2304]{2,1,0:T(2,128)(2,1)S(1)} %reshape.14), channel_id=1, replica_groups=mesh['energy'=64,'atoms'=4] {'energy'}, dimensions={0} | all-to-all | bytes 1179648 | tf_op jit(solution)/shard_map/all_to_all | solution.py:106
  88.0 1.4 %reshape.15 = bf16[1024,1,288]{2,1,0:T(2,128)(2,1)S(1)} reshape(bf16[64,2,2304]{2,1,0:T(2,128)(2,1)S(1)} %all_to_all.24) | data formatting | bytes 1179648
  89.4 0.1 copy.15
  89.6 1.1 %copy.14 = bf16[16,64,288]{2,1,0:T(8,128)(2,1)} copy(bf16[16,64,288]{2,0,1:T(8,128)(2,1)S(1)} %bitcast.10) | data formatting | bytes 1179648 | tf_op jit(solution)/shard_map/all_to_all | solution.py:106
Async XLA Ops:
  0.0 7.7 %copy-start = (s32[64,1]{0,1:T(1,128)S(1)}, s32[64,1]{0,1:T(1,128)}, u32[]{:S(2)}) copy-start(s32[64,1]{0,1:T(1,128)} %param.8) | copy-start | bytes 772
  1.0 7.3 %collective-permute-start = (bf16[16,8,288]{2,1,0:T(8,128)(2,1)S(1)}, bf16[16,8,288]{2,1,0:T(8,128)(2,1)S(1)}, u32[]{:S(2)}, u32[]{:S(2)}) collective-permute-start(bf16[16,8,288]{2,1,0:T(8,128)(2,1)S(1)} %get-tuple-element.9), channel_id=1, source_target_pairs={{0,1},{1,2},{2,3},{4,5},{5,6},{6,7},{8,9},{9,10},{10,11},{12,13},{... | collective-permute-start | bytes 221192 | tf_op jit(solution)/shard_map/ppermute | solution.py:17
  4.9 5.4 %collective-permute-start.1 = (bf16[16,8,288]{2,1,0:T(8,128)(2,1)S(1)}, bf16[16,8,288]{2,1,0:T(8,128)(2,1)S(1)}, u32[]{:S(2)}, u32[]{:S(2)}) collective-permute-start(bf16[16,8,288]{2,1,0:T(8,128)(2,1)S(1)} %get-tuple-element.10), channel_id=1, source_target_pairs={{1,0},{2,1},{3,2},{5,4},{6,5},{7,6},{9,8},{10,9},{11,10},{13,12},{... | collective-permute-start | bytes 221192 | tf_op jit(solution)/shard_map/ppermute | solution.py:20

commit v6 on v5

--- a/solution.py
+++ b/solution.py
@@ -6,20 +6,8 @@
 from jax.sharding import PartitionSpec as P
 
 HALO = 8
+EDGE = 16
 ATOMS_DEV = 1
-
-
-def padded(block, sides, width):
-    for axis, dim in sides:
-        count = lax.axis_size(axis)
-        forward = [(i, i + 1) for i in range(count - 1)]
-        backward = [(target, source) for source, target in forward]
-        low = lax.ppermute(
-            lax.slice_in_dim(block, block.shape[dim] - width, None, axis=dim), axis, forward
-        )
-        high = lax.ppermute(lax.slice_in_dim(block, 0, width, axis=dim), axis, backward)
-        block = jnp.concatenate([low, block, high], axis=dim)
-    return block
 
 
 def toeplitz_kernel(owner_ref, phonon_ref, columns_ref, out_ref):
@@ -53,49 +41,81 @@
     )(owner, phonon, columns)
 
 
-def neighbour_kernel(select_ref, widened_ref, superop_ref, out_ref):
-    energies, rows, comps = widened_ref.shape
-    atoms = select_ref.shape[1]
-    widened = widened_ref[...]
+def couple_rows(select_refs, source_refs, superop_ref):
+    energies, _, comps = source_refs[0].shape
+    atoms = select_refs[0].shape[1]
+    sources = [ref[...] for ref in source_refs]
     total = jnp.zeros((energies * atoms, comps), jnp.float32)
-    for slot in range(select_ref.shape[0]):
-        select = jnp.broadcast_to(select_ref[slot], (energies, atoms, rows))
-        picked = lax.dot_general(
-            select, widened, (((2,), (1,)), ((0,), (0,))), preferred_element_type=jnp.float32
-        )
+    for slot in range(select_refs[0].shape[0]):
+        picked = jnp.zeros((energies, atoms, comps), jnp.float32)
+        for select_ref, source in zip(select_refs, sources):
+            select = jnp.broadcast_to(select_ref[slot], (energies, atoms, source.shape[1]))
+            picked = picked + lax.dot_general(
+                select, source, (((2,), (1,)), ((0,), (0,))), preferred_element_type=jnp.float32
+            )
         picked = picked.astype(jnp.bfloat16).reshape(energies * atoms, comps)
         total = total + jnp.dot(picked, superop_ref[slot], preferred_element_type=jnp.float32)
-    out_ref[...] = total.astype(out_ref.dtype).reshape(energies, atoms, comps)
+    return total.astype(jnp.bfloat16).reshape(energies, atoms, comps)
 
 
-def neighbour_apply(select, widened, superop):
-    energies, rows, comps = widened.shape
-    slots, atoms, _ = select.shape
+def interior_kernel(select_ref, green_ref, superop_ref, out_ref):
+    out_ref[...] = couple_rows([select_ref], [green_ref], superop_ref)
+
+
+def edge_kernel(low_sel, mid_sel, high_sel, low_ref, green_ref, high_ref, superop_ref, base_ref, out_ref):
+    edges = couple_rows([low_sel, mid_sel, high_sel], [low_ref, green_ref, high_ref], superop_ref)
+    width = low_ref.shape[1]
+    atoms = out_ref.shape[1]
+    out_ref[...] = base_ref[...]
+    out_ref[:, :width, :] = edges[:, :width, :]
+    out_ref[:, atoms - width:, :] = edges[:, width:, :]
+
+
+def couple_call(kernel, args, out_shape, flops):
     vmem = pl.BlockSpec(memory_space=pltpu.VMEM)
     return pl.pallas_call(
-        neighbour_kernel,
-        out_shape=jax.ShapeDtypeStruct((energies, atoms, comps), jnp.bfloat16),
-        in_specs=[vmem, vmem, vmem],
+        kernel,
+        out_shape=jax.ShapeDtypeStruct(out_shape, jnp.bfloat16),
+        in_specs=[vmem] * len(args),
         out_specs=vmem,
         cost_estimate=pl.CostEstimate(
-            flops=2 * slots * energies * atoms * comps * (rows + comps),
-            bytes_accessed=2 * (widened.size + superop.size + select.size + energies * atoms * comps),
+            flops=flops,
+            bytes_accessed=sum(2 * a.size for a in args) + 2 * out_shape[0] * out_shape[1] * out_shape[2],
             transcendentals=0,
         ),
-    )(select, widened, superop)
+    )(*args)
 
 
 def per_device(green, superop, phonon, owner, neighbours):
     local_energies = green.shape[0]
     group_size = green.shape[1]
     comps = green.shape[2]
+    slots = neighbours.shape[1]
     group = lax.axis_index("atoms")
-    widened = padded(green, (("atoms", 1),), HALO)
+    groups = lax.axis_size("atoms")
+    forward = [(i, i + 1) for i in range(groups - 1)]
+    backward = [(i + 1, i) for i in range(groups - 1)]
+    low = lax.ppermute(green[:, group_size - EDGE:, :], "atoms", forward)
+    high = lax.ppermute(green[:, :EDGE, :], "atoms", backward)
     present = neighbours >= 0
-    target_rows = jnp.where(present, neighbours - group * group_size + HALO, -1)
-    rows = jnp.arange(widened.shape[1], dtype=jnp.int32)
-    select = (target_rows.T[:, :, None] == rows[None, None, :]).astype(jnp.bfloat16)
-    coupled = neighbour_apply(select, widened, superop)
+    target = jnp.where(present, neighbours - group * group_size, -4 * group_size).T
+    mid_rows = jnp.arange(group_size, dtype=jnp.int32)
+    edge_rows = jnp.arange(EDGE, dtype=jnp.int32)
+    select_mid = (target[:, :, None] == mid_rows).astype(jnp.bfloat16)
+    edge_target = jnp.concatenate([target[:, :EDGE], target[:, group_size - EDGE:]], axis=1)
+    select_low = (edge_target[:, :, None] == edge_rows - EDGE).astype(jnp.bfloat16)
+    select_edge = (edge_target[:, :, None] == mid_rows).astype(jnp.bfloat16)
+    select_high = (edge_target[:, :, None] == edge_rows + group_size).astype(jnp.bfloat16)
+    shape = (local_energies, group_size, comps)
+    base = couple_call(
+        interior_kernel, (select_mid, green, superop), shape,
+        2 * slots * local_energies * group_size * comps * (group_size + comps),
+    )
+    coupled = couple_call(
+        edge_kernel,
+        (select_low, select_edge, select_high, low, green, high, superop, base), shape,
+        2 * slots * local_energies * 2 * EDGE * comps * (group_size + 2 * EDGE + comps),
+    )
     count = local_energies * lax.axis_size("energy")
     peers = lax.axis_size("energy")
     outgoing = jnp.transpose(coupled, (1, 0, 2)).reshape(peers, 2, local_energies * comps // 2)

time: 91.1 us -> 94.8 us (1.041)
  Pallas kernels: 9.69 us -> 15.2 us
  waiting for transfers between devices: 2.04 us -> 0.01 us
  local copies, waits for them, and re-layouts: 10.5 us -> 11.5 us
    pallas_call x1 -> x2, Pallas kernels: 5.38 us -> 10.8 us  [couple_call(): pl.pallas_call(kernel, out_shape=jax.ShapeDtypeStruct(out_shape, jnp.bflo...]
    concatenate x1, other arithmetic: 2.2 us -> 0.07 us  [per_device(): jnp.concatenate([target[:, :EDGE], target[:, group_size - EDGE:]], axis=1)]
    ppermute x2, waiting for transfers between devices: 2.04 us -> 0.01 us  [the longest x1 0.01 us: per_device(): high = lax.ppermute(green[:, :EDGE, :], 'atoms', backward)]
    convert_element_type x1 -> x3, other arithmetic: 0.72 us -> 2.13 us  [the longest x1 0.73 us: per_device(): select_mid = (target[:, :, None] == mid_rows).astype(jnp.bfloat16)]
    unnamed x5 -> x9, local copies, waits for them, and re-layouts: 2.65 us -> 3.38 us
  transfers between devices with their start and end apart: 2 -> 2, of which waited for: 1 -> 0; matrix products, arithmetic and copies ran while one was open for 2% -> 4% of each run, Pallas kernels for 0% -> 6%
where the time goes in v6:
time: 94.8 us; the launch traced here: 94.3 us
  blocking collectives  56.6 us (60%)
  Pallas kernels  15.2 us (16%)
  local copies, waits for them, and re-layouts  11.5 us (12%)
  starting transfers between devices  5.88 us (6%)
  other arithmetic  5.15 us (5%)
    all_to_all x1, blocking collectives, per_device(): lax.all_to_all(outgoing, 'energy', split_axis=0, concat_axis=0, tiled=True)  32 us
    all_to_all x1, blocking collectives, per_device(): lax.all_to_all(product.reshape(count, ATOMS_DEV, comps), 'energy', split_...  24.6 us
    pallas_call x2, Pallas kernels, couple_call(): pl.pallas_call(kernel, out_shape=jax.ShapeDtypeStruct(out_shape, jnp.bflo...  10.8 us
    ppermute x1, starting transfers between devices, per_device(): low = lax.ppermute(green[:, group_size - EDGE:, :], 'atoms', forward)  4.58 us
    pallas_call x1, Pallas kernels, toeplitz_apply(): pl.pallas_call(toeplitz_kernel, out_shape=jax.ShapeDtypeStruct((count, co...  4.33 us
    unnamed x9, local copies, waits for them, and re-layouts  3.38 us
    reshape x1, other arithmetic, per_device(): product.reshape(count, ATOMS_DEV, comps)  2.26 us
    reshape x1, local copies, waits for them, and re-layouts, per_device(): product = toeplitz_apply(mine, phonon, columns.reshape(count, comps))  2.05 us
  transfers between devices with their start and end apart: 2, of which 0 were waited for; matrix products, arithmetic and copies ran while one was open for 4% of the time, Pallas kernels for 6%

profile of v6, /device:TPU:1, one launch (start us, length us, event | category | flops | bytes accessed | tf_op | source)
XLA Modules:
  0.0 94.3 jit_solution(7720686905155179942)
XLA Ops:
  0.0 0.0 copy-start
  0.0 1.1 %fusion.2 = (bf16[16,16,288]{2,1,0:T(8,128)(2,1)S(1)}, bf16[16,16,288]{2,1,0:T(8,128)(2,1)S(1)}) fusion(bf16[16,64,288]{2,1,0:T(8,128)(2,1)} %green_ref.3), kind=kLoop, calls=%fused_computation.11 | loop fusion | bytes 589824 | tf_op jit(solution)/shard_map/slice | solution.py:99
  1.1 1.3 %collective-permute-start.1 = (bf16[16,16,288]{2,1,0:T(8,128)(2,1)S(1)}, bf16[16,16,288]{2,1,0:T(8,128)(2,1)S(1)}, u32[]{:S(2)}, u32[]{:S(2)}) collective-permute-start(bf16[16,16,288]{2,1,0:T(8,128)(2,1)S(1)} %get-tuple-element.9), channel_id=1, source_target_pairs={{1,0},{2,1},{3,2},{5,4},{6,5},{7,6},{9,8},{10,9},{11,10},{13,12},{... | collective-permute-start | bytes 442376 | tf_op jit(solution)/shard_map/ppermute | solution.py:99
  2.4 4.6 %collective-permute-start = (bf16[16,16,288]{2,1,0:T(8,128)(2,1)S(1)}, bf16[16,16,288]{2,1,0:T(8,128)(2,1)S(1)}, u32[]{:S(2)}, u32[]{:S(2)}) collective-permute-start(bf16[16,16,288]{2,1,0:T(8,128)(2,1)S(1)} %get-tuple-element.10), channel_id=1, source_target_pairs={{0,1},{1,2},{2,3},{4,5},{5,6},{6,7},{8,9},{9,10},{10,11},{12,13},{... | collective-permute-start | bytes 442376 | tf_op jit(solution)/shard_map/ppermute | solution.py:98
  7.0 0.7 select_bitcast_fusion
  7.7 0.1 fusion.3
  7.8 0.7 fusion.select_ref
  8.5 0.1 pad_add_fusion
  8.6 0.7 compare_convert_fusion
  9.3 0.7 fusion.1.mid_sel
  10.0 0.0 copy-done
  10.0 0.6 constant_dynamic-slice_fusion
  10.6 5.3 %shard_map.55.base_ref = bf16[16,64,288]{2,1,0:T(8,128)(2,1)} custom-call(bf16[4,64,64]{2,1,0:T(8,128)(2,1)} %fusion.select_ref, bf16[16,64,288]{2,1,0:T(8,128)(2,1)} %green_ref.3, bf16[4,288,288]{2,1,0:T(8,128)(2,1)} %superop_ref.3), custom_call_target="tpu_custom_call" | custom-call | flops 830472192 | bytes 1875968 | tf_op jit(solution)/shard_map/pallas_call | solution.py:76
  15.9 0.0 collective-permute-done.1.high_ref
  15.9 0.0 copy-start.1
  15.9 0.0 collective-permute-done.low_ref
  15.9 0.0 copy-start.2
  15.9 0.7 copy-done.1
  16.6 0.1 copy-done.2
  16.6 5.6 %shard_map.56 = bf16[16,64,288]{2,1,0:T(8,128)(2,1)} custom-call(bf16[4,32,16]{2,1,0:T(8,128)(2,1)} %get-tuple-element.12.low_sel, bf16[4,32,64]{2,1,0:T(8,128)(2,1)} %fusion.1.mid_sel, bf16[4,32,16]{2,1,0:T(8,128)(2,1)} %get-tuple-element.11.high_sel, bf16[16,16,288]{2,1,0:T(8,128)(2,1)} %copy-done.2, bf16[16,64,288]{2,1,0:T(8,128)(2,1)} %green_ref.3, ...), custom_call_target="tpu_custom_call" | custom-call | flops 452984832 | bytes 2752512 | tf_op jit(solution)/shard_map/pallas_call | solution.py:76
  22.2 1.6 %copy.12 = bf16[64,16,288]{2,1,0:T(8,128)(2,1)S(1)} copy(bf16[64,16,288]{2,0,1:T(8,128)(2,1)} %bitcast.10) | data formatting | bytes 1179648 | tf_op jit(solution)/shard_map/transpose | solution.py:121
  23.8 1.1 %reshape.20 = bf16[64,2,2304]{2,1,0:T(2,128)(2,1)S(1)} reshape(bf16[64,16,288]{2,1,0:T(8,128)(2,1)S(1)} %copy.12) | data formatting | bytes 1179648 | tf_op jit(solution)/shard_map/reshape | solution.py:121
  24.9 32.0 %all_to_all.23 = bf16[64,2,2304]{2,1,0:T(2,128)(2,1)S(1)} all-to-all(bf16[64,2,2304]{2,1,0:T(2,128)(2,1)S(1)} %reshape.20), channel_id=1, replica_groups=mesh['energy'=64,'atoms'=4] {'energy'}, dimensions={0} | all-to-all | bytes 1179648 | tf_op jit(solution)/shard_map/all_to_all | solution.py:124
  56.8 2.0 %reshape.21.columns_ref = bf16[1024,288]{1,0:T(8,128)(2,1)} reshape(bf16[64,2,2304]{2,1,0:T(2,128)(2,1)S(1)} %all_to_all.23) | data formatting | bytes 1179648 | tf_op jit(solution)/shard_map/reshape | solution.py:125
  58.9 4.3 %shard_map.57 = bf16[1024,288]{1,0:T(8,128)(2,1)} custom-call(s32[1]{0:T(128)} %bitcast.owner_ref, bf16[64,2048]{1,0:T(8,128)(2,1)} %phonon_ref.1, bf16[1024,288]{1,0:T(8,128)(2,1)} %reshape.21.columns_ref), custom_call_target="tpu_custom_call" | custom-call | flops 603979776 | bytes 1441792 | tf_op jit(solution)/shard_map/pallas_call | solution.py:31
  63.2 0.5 broadcast.21
  63.7 2.3 %reduce = bf16[1024,288]{1,0:T(8,128)(2,1)S(1)} reduce(bf16[1024,1,288]{2,0,1:T(8,128)(2,1)} %bitcast.12, bf16[]{:T(256)} %broadcast.21), dimensions={1}, to_apply=%copy.13.reduce_sub_computation | reduce | bytes 1179650 | tf_op jit(solution)/shard_map/reshape | solution.py:127
  66.0 1.1 %reshape.23 = bf16[64,2,2304]{2,1,0:T(2,128)(2,1)S(1)} reshape(bf16[1024,288]{1,0:T(8,128)(2,1)S(1)} %reduce) | data formatting | bytes 1179648
  67.0 24.6 %all_to_all.24 = bf16[64,2,2304]{2,1,0:T(2,128)(2,1)S(1)} all-to-all(bf16[64,2,2304]{2,1,0:T(2,128)(2,1)S(1)} %reshape.23), channel_id=1, replica_groups=mesh['energy'=64,'atoms'=4] {'energy'}, dimensions={0} | all-to-all | bytes 1179648 | tf_op jit(solution)/shard_map/all_to_all | solution.py:126
  91.7 1.4 %reshape.24 = bf16[1024,1,288]{2,1,0:T(2,128)(2,1)S(1)} reshape(bf16[64,2,2304]{2,1,0:T(2,128)(2,1)S(1)} %all_to_all.24) | data formatting | bytes 1179648
  93.1 0.1 copy.15
  93.3 1.1 %copy.14 = bf16[16,64,288]{2,1,0:T(8,128)(2,1)} copy(bf16[16,64,288]{2,0,1:T(8,128)(2,1)S(1)} %bitcast.11) | data formatting | bytes 1179648 | tf_op jit(solution)/shard_map/all_to_all | solution.py:126
  (1 shorter events, 0.0 us)
Async XLA Ops:
  0.0 10.0 %copy-start = (s32[64,1]{0,1:T(1,128)S(1)}, s32[64,1]{0,1:T(1,128)}, u32[]{:S(2)}) copy-start(s32[64,1]{0,1:T(1,128)} %param.8) | copy-start | bytes 772
  1.1 14.8 %collective-permute-start.1 = (bf16[16,16,288]{2,1,0:T(8,128)(2,1)S(1)}, bf16[16,16,288]{2,1,0:T(8,128)(2,1)S(1)}, u32[]{:S(2)}, u32[]{:S(2)}) collective-permute-start(bf16[16,16,288]{2,1,0:T(8,128)(2,1)S(1)} %get-tuple-element.9), channel_id=1, source_target_pairs={{1,0},{2,1},{3,2},{5,4},{6,5},{7,6},{9,8},{10,9},{11,10},{13,12},{... | collective-permute-start | bytes 442376 | tf_op jit(solution)/shard_map/ppermute | solution.py:99
  2.4 13.5 %collective-permute-start = (bf16[16,16,288]{2,1,0:T(8,128)(2,1)S(1)}, bf16[16,16,288]{2,1,0:T(8,128)(2,1)S(1)}, u32[]{:S(2)}, u32[]{:S(2)}) collective-permute-start(bf16[16,16,288]{2,1,0:T(8,128)(2,1)S(1)} %get-tuple-element.10), channel_id=1, source_target_pairs={{0,1},{1,2},{2,3},{4,5},{5,6},{6,7},{8,9},{9,10},{10,11},{12,13},{... | collective-permute-start | bytes 442376 | tf_op jit(solution)/shard_map/ppermute | solution.py:98
  15.9 0.7 copy-start.1
  15.9 0.7 copy-start.2

commit v7 on v5

v7 whole, which is shorter than its diff:
```python
import jax
import jax.numpy as jnp
from jax import lax
from jax.experimental import pallas as pl
from jax.experimental.pallas import tpu as pltpu
from jax.sharding import PartitionSpec as P

HALO = 8
EDGE = 16
ATOMS_DEV = 1


def toeplitz_kernel(owner_ref, phonon_ref, columns_ref, out_ref):
    count = columns_ref.shape[0]
    domain = owner_ref[0]
    base = pl.multiple_of((domain // 16) * 16, 16)
    block = phonon_ref[pl.ds(base, 16), :].astype(jnp.float32)
    rows = lax.broadcasted_iota(jnp.int32, block.shape, 0)
    row = jnp.sum(jnp.where(rows == domain - base, block, 0.0), axis=0, keepdims=True)
    wide = jnp.broadcast_to(row, (count, 2 * count))
    rolled = pltpu.roll(wide, shift=count, axis=1, stride=1, stride_axis=0)
    kernel_t = rolled[:, :count].astype(jnp.bfloat16)
    out_ref[...] = lax.dot_general(
        kernel_t, columns_ref[...], (((0,), (0,)), ((), ())), preferred_element_type=jnp.float32
    ).astype(out_ref.dtype)


def toeplitz_apply(owner, phonon, columns):
    count, comps = columns.shape
    vmem = pl.BlockSpec(memory_space=pltpu.VMEM)
    return pl.pallas_call(
        toeplitz_kernel,
        out_shape=jax.ShapeDtypeStruct((count, comps), jnp.bfloat16),
        in_specs=[pl.BlockSpec(memory_space=pltpu.SMEM), vmem, vmem],
        out_specs=vmem,
        cost_estimate=pl.CostEstimate(
            flops=2 * count * count * comps,
            bytes_accessed=2 * (phonon.size + 2 * count * comps),
            transcendentals=0,
        ),
    )(owner, phonon, columns)


def neighbour_kernel(index_ref, low_ref, green_ref, high_ref, superop_ref, out_ref, rows_ref, picked_ref):
    width = low_ref.shape[0]
    atoms, energies, comps = green_ref.shape
    slots = superop_ref.shape[0]
    rows_ref[:width] = low_ref[...]
    rows_ref[width:width + atoms] = green_ref[...]
    rows_ref[width + atoms:2 * width + atoms] = high_ref[...]
    rows_ref[2 * width + atoms] = jnp.zeros((energies, comps), rows_ref.dtype)

    def pick(atom, carry):
        for slot in range(slots):
            picked_ref[slot, atom] = rows_ref[index_ref[atom * slots + slot]]
        return carry

    lax.fori_loop(0, atoms, pick, 0, unroll=8)
    total = jnp.zeros((atoms * energies, comps), jnp.float32)
    for slot in range(slots):
        total = total + jnp.dot(
            picked_ref[slot].reshape(atoms * energies, comps),
            superop_ref[slot],
            preferred_element_type=jnp.float32,
        )
    out_ref[...] = total.astype(out_ref.dtype).reshape(atoms, energies, comps)


def neighbour_apply(index, low, green_t, high, superop):
    width = low.shape[0]
    atoms, energies, comps = green_t.shape
    slots = superop.shape[0]
    vmem = pl.BlockSpec(memory_space=pltpu.VMEM)
    return pl.pallas_call(
        neighbour_kernel,
        out_shape=jax.ShapeDtypeStruct(green_t.shape, jnp.bfloat16),
        in_specs=[pl.BlockSpec(memory_space=pltpu.SMEM)] + [vmem] * 4,
        out_specs=vmem,
        scratch_shapes=[
            pltpu.VMEM((2 * width + atoms + 1, energies, comps), jnp.bfloat16),
            pltpu.VMEM((slots, atoms, energies, comps), jnp.bfloat16),
        ],
        cost_estimate=pl.CostEstimate(
            flops=2 * slots * atoms * energies * comps * comps,
            bytes_accessed=2 * (2 * low.size + 2 * green_t.size + superop.size),
            transcendentals=0,
        ),
    )(index, low, green_t, high, superop)


def per_device(green, superop, phonon, owner, neighbours):
    local_energies = green.shape[0]
    group_size = green.shape[1]
    comps = green.shape[2]
    group = lax.axis_index("atoms")
    groups = lax.axis_size("atoms")
    green_t = jnp.transpose(green, (1, 0, 2))
    forward = [(i, i + 1) for i in range(groups - 1)]
    backward = [(i + 1, i) for i in range(groups - 1)]
    low = lax.ppermute(green_t[group_size - EDGE:], "atoms", forward)
    high = lax.ppermute(green_t[:EDGE], "atoms", backward)
    present = neighbours >= 0
    index = jnp.where(present, neighbours - group * group_size + EDGE, 2 * EDGE + group_size)
    coupled = neighbour_apply(index.reshape(-1), low, green_t, high, superop)
    count = local_energies * lax.axis_size("energy")
    peers = lax.axis_size("energy")
    outgoing = coupled.reshape(peers, 2, local_energies * comps // 2)
    mine = lax.dynamic_slice_in_dim(owner[:, 0], lax.axis_index("energy"), 1)
    mine, outgoing = lax.optimization_barrier((mine, outgoing))
    columns = lax.all_to_all(outgoing, "energy", split_axis=0, concat_axis=0, tiled=True)
    product = toeplitz_apply(mine, phonon, columns.reshape(count, comps))
    result = lax.all_to_all(
        product.reshape(count, ATOMS_DEV, comps), "energy", split_axis=0, concat_axis=1, tiled=True
    )
    return result


def solution(mesh):
    return jax.shard_map(
        per_device,
        mesh=mesh,
        in_specs=(P("energy", "atoms", None), P(), P(), P("atoms", None), P("atoms", None)),
        out_specs=P("energy", "atoms", None),
        check_vma=False,
    )
```

time: 91.1 us -> 90.2 us (level)
  other arithmetic: 5.86 us -> 2.26 us
  local copies, waits for them, and re-layouts: 10.5 us -> 12.8 us
  waiting for transfers between devices: 2.04 us -> 1.09 us
    reshape x1 -> x2, local copies, waits for them, and re-layouts: 1.06 us -> 3.39 us  [the longest x1 2.69 us: per_device(): outgoing = coupled.reshape(peers, 2, local_energies * comps // 2)]
    unnamed x5 -> x14, local copies, waits for them, and re-layouts: 2.65 us -> 4.96 us
    concatenate x1 -> x0, other arithmetic: 2.2 us -> none  [padded(): block = jnp.concatenate([low, block, high], axis=dim)]
    transpose x1 -> x0, local copies, waits for them, and re-layouts: 1.59 us -> none  [per_device(): jnp.transpose(coupled, (1, 0, 2))]
    ppermute x2, waiting for transfers between devices: 2.04 us -> 1.09 us  [the longest x1 1.09 us: per_device(): low = lax.ppermute(green_t[group_size - EDGE:], 'atoms', forward)]
    slice x1, local copies, waits for them, and re-layouts: 0.97 us -> 0.04 us  [per_device(): high = lax.ppermute(green_t[:EDGE], 'atoms', backward)]
where the time goes in v7:
time: 90.2 us; the launch traced here: 89.4 us
  blocking collectives  57.9 us (64%)
  local copies, waits for them, and re-layouts  12.8 us (14%)
  Pallas kernels  9.43 us (10%)
  starting transfers between devices  5.88 us (7%)
  other arithmetic  2.26 us (3%)
  waiting for transfers between devices  1.09 us (1%)
    all_to_all x1, blocking collectives, per_device(): lax.all_to_all(outgoing, 'energy', split_axis=0, concat_axis=0, tiled=True)  33.2 us
    all_to_all x1, blocking collectives, per_device(): lax.all_to_all(product.reshape(count, ATOMS_DEV, comps), 'energy', split_...  24.6 us
    pallas_call x1, Pallas kernels, neighbour_apply(): pl.pallas_call(neighbour_kernel, out_shape=jax.ShapeDtypeStruct(green_t.s...  5.04 us
    unnamed x14, local copies, waits for them, and re-layouts  4.96 us
    ppermute x1, starting transfers between devices, per_device(): low = lax.ppermute(green_t[group_size - EDGE:], 'atoms', forward)  4.58 us
    pallas_call x1, Pallas kernels, toeplitz_apply(): pl.pallas_call(toeplitz_kernel, out_shape=jax.ShapeDtypeStruct((count, co...  4.38 us
    reshape x1, local copies, waits for them, and re-layouts, per_device(): outgoing = coupled.reshape(peers, 2, local_energies * comps // 2)  2.69 us
    reshape x1, other arithmetic, per_device(): product.reshape(count, ATOMS_DEV, comps)  2.26 us
  transfers between devices with their start and end apart: 2, of which 1 were waited for; matrix products, arithmetic and copies ran while one was open for 2% of the time, Pallas kernels for 0%

profile of v7, /device:TPU:1, one launch (start us, length us, event | category | flops | bytes accessed | tf_op | source)
XLA Modules:
  0.0 89.4 jit_solution(12192137286454523338)
XLA Ops:
  0.0 0.0 copy-start
  0.0 0.0 copy-start.4
  0.0 1.6 %copy.21 = bf16[16,64,288]{2,0,1:T(8,128)(2,1)S(1)} copy(bf16[16,64,288]{2,1,0:T(8,128)(2,1)} %param.5) | data formatting | bytes 1179648 | tf_op args[0]
  1.6 0.0 copy-start.1
  1.7 1.3 %collective-permute-start.1 = (bf16[16,16,288]{2,1,0:T(8,128)(2,1)S(1)}, bf16[16,16,288]{2,1,0:T(8,128)(2,1)S(1)}, u32[]{:S(2)}, u32[]{:S(2)}) collective-permute-start(bf16[16,16,288]{2,1,0:T(8,128)(2,1)S(1)} %get-tuple-element.9), channel_id=1, source_target_pairs={{1,0},{2,1},{3,2},{5,4},{6,5},{7,6},{9,8},{10,9},{11,10},{13,12},{... | collective-permute-start | bytes 442376 | tf_op jit(solution)/shard_map/ppermute | solution.py:101
  3.0 4.6 %collective-permute-start = (bf16[16,16,288]{2,1,0:T(8,128)(2,1)S(1)}, bf16[16,16,288]{2,1,0:T(8,128)(2,1)S(1)}, u32[]{:S(2)}, u32[]{:S(2)}) collective-permute-start(bf16[16,16,288]{2,1,0:T(8,128)(2,1)S(1)} %get-tuple-element.10), channel_id=1, source_target_pairs={{0,1},{1,2},{2,3},{4,5},{5,6},{6,7},{8,9},{9,10},{10,11},{12,13},{... | collective-permute-start | bytes 442376 | tf_op jit(solution)/shard_map/ppermute | solution.py:100
  7.6 0.0 copy-done.4
  7.6 0.1 copy.15
  7.7 0.7 reshape.13.index_ref
  8.4 0.0 copy-done
  8.4 0.7 constant_dynamic-slice_fusion
  9.1 0.0 collective-permute-done.1.high_ref
  9.1 0.0 copy-start.2
  9.1 1.1 %collective-permute-done.low_ref = bf16[16,16,288]{2,1,0:T(8,128)(2,1)S(1)} collective-permute-done((bf16[16,16,288]{2,1,0:T(8,128)(2,1)S(1)}, bf16[16,16,288]{2,1,0:T(8,128)(2,1)S(1)}, u32[]{:S(2)}, u32[]{:S(2)}) %collective-permute-start) | collective-permute-done | bytes 147488 | tf_op jit(solution)/shard_map/ppermute | solution.py:100
  10.2 0.0 copy-done.1
  10.2 0.0 copy-done.2
  10.2 0.0 copy-start.3
  10.2 0.7 copy-done.3
  10.8 5.0 %shard_map.55 = bf16[64,16,288]{2,1,0:T(8,128)(2,1)} custom-call(s32[256]{0:T(256)} %reshape.13.index_ref, bf16[16,16,288]{2,1,0:T(8,128)(2,1)} %copy-done.3, bf16[64,16,288]{2,1,0:T(8,128)(2,1)} %bitcast.11, bf16[16,16,288]{2,1,0:T(8,128)(2,1)} %copy-done.2, bf16[4,288,288]{2,1,0:T(8,128)(2,1)} %superop_ref.1), custom_call_target="tpu_custom_call" | custom-call | flops 679477248 | bytes 2138112 | tf_op jit(solution)/shard_map/pallas_call | solution.py:74
  15.9 2.7 %reshape.14 = bf16[64,2,2304]{2,1,0:T(2,128)(2,1)S(1)} reshape(bf16[64,16,288]{2,1,0:T(8,128)(2,1)} %shard_map.55) | data formatting | bytes 1179648 | tf_op jit(solution)/shard_map/reshape | solution.py:107
  18.6 33.2 %all_to_all.23 = bf16[64,2,2304]{2,1,0:T(2,128)(2,1)S(1)} all-to-all(bf16[64,2,2304]{2,1,0:T(2,128)(2,1)S(1)} %reshape.14), channel_id=1, replica_groups=mesh['energy'=64,'atoms'=4] {'energy'}, dimensions={0} | all-to-all | bytes 1179648 | tf_op jit(solution)/shard_map/all_to_all | solution.py:110
  51.8 2.0 %reshape.15.columns_ref = bf16[1024,288]{1,0:T(8,128)(2,1)} reshape(bf16[64,2,2304]{2,1,0:T(2,128)(2,1)S(1)} %all_to_all.23) | data formatting | bytes 1179648 | tf_op jit(solution)/shard_map/reshape | solution.py:111
  53.9 4.4 %shard_map.56 = bf16[1024,288]{1,0:T(8,128)(2,1)} custom-call(s32[1]{0:T(128)} %bitcast.owner_ref, bf16[64,2048]{1,0:T(8,128)(2,1)} %phonon_ref.1, bf16[1024,288]{1,0:T(8,128)(2,1)} %reshape.15.columns_ref), custom_call_target="tpu_custom_call" | custom-call | flops 603979776 | bytes 1441792 | tf_op jit(solution)/shard_map/pallas_call | solution.py:31
  58.3 0.5 broadcast
  58.8 2.3 %reduce = bf16[1024,288]{1,0:T(8,128)(2,1)S(1)} reduce(bf16[1024,1,288]{2,0,1:T(8,128)(2,1)} %bitcast.13, bf16[]{:T(256)} %broadcast), dimensions={1}, to_apply=%copy.17.reduce_sub_computation | reduce | bytes 1179650 | tf_op jit(solution)/shard_map/reshape | solution.py:113
  61.0 1.1 %reshape.17 = bf16[64,2,2304]{2,1,0:T(2,128)(2,1)S(1)} reshape(bf16[1024,288]{1,0:T(8,128)(2,1)S(1)} %reduce) | data formatting | bytes 1179648
  62.1 24.6 %all_to_all.24 = bf16[64,2,2304]{2,1,0:T(2,128)(2,1)S(1)} all-to-all(bf16[64,2,2304]{2,1,0:T(2,128)(2,1)S(1)} %reshape.17), channel_id=1, replica_groups=mesh['energy'=64,'atoms'=4] {'energy'}, dimensions={0} | all-to-all | bytes 1179648 | tf_op jit(solution)/shard_map/all_to_all | solution.py:112
  86.7 1.4 %reshape.18 = bf16[1024,1,288]{2,1,0:T(2,128)(2,1)S(1)} reshape(bf16[64,2,2304]{2,1,0:T(2,128)(2,1)S(1)} %all_to_all.24) | data formatting | bytes 1179648
  88.2 0.1 copy.19
  88.3 1.1 %copy.18 = bf16[16,64,288]{2,1,0:T(8,128)(2,1)} copy(bf16[16,64,288]{2,0,1:T(8,128)(2,1)S(1)} %bitcast.12) | data formatting | bytes 1179648 | tf_op jit(solution)/shard_map/all_to_all | solution.py:112
  (2 shorter events, 0.0 us)
Async XLA Ops:
  0.0 8.4 %copy-start = (s32[64,1]{0,1:T(1,128)S(1)}, s32[64,1]{0,1:T(1,128)}, u32[]{:S(2)}) copy-start(s32[64,1]{0,1:T(1,128)} %param.8) | copy-start | bytes 772
  0.0 7.6 %copy-start.4 = (s32[64,4]{0,1:T(4,128)S(1)}, s32[64,4]{0,1:T(4,128)}, u32[]{:S(2)}) copy-start(s32[64,4]{0,1:T(4,128)} %param.9) | copy-start | bytes 3076
  1.6 8.5 %copy-start.1 = (bf16[16,64,288]{2,0,1:T(8,128)(2,1)}, bf16[16,64,288]{2,0,1:T(8,128)(2,1)S(1)}, u32[]{:S(2)}) copy-start(bf16[16,64,288]{2,0,1:T(8,128)(2,1)S(1)} %copy.21) | copy-start | bytes 1769476
  1.7 7.4 %collective-permute-start.1 = (bf16[16,16,288]{2,1,0:T(8,128)(2,1)S(1)}, bf16[16,16,288]{2,1,0:T(8,128)(2,1)S(1)}, u32[]{:S(2)}, u32[]{:S(2)}) collective-permute-start(bf16[16,16,288]{2,1,0:T(8,128)(2,1)S(1)} %get-tuple-element.9), channel_id=1, source_target_pairs={{1,0},{2,1},{3,2},{5,4},{6,5},{7,6},{9,8},{10,9},{11,10},{13,12},{... | collective-permute-start | bytes 442376 | tf_op jit(solution)/shard_map/ppermute | solution.py:101
  3.0 7.2 %collective-permute-start = (bf16[16,16,288]{2,1,0:T(8,128)(2,1)S(1)}, bf16[16,16,288]{2,1,0:T(8,128)(2,1)S(1)}, u32[]{:S(2)}, u32[]{:S(2)}) collective-permute-start(bf16[16,16,288]{2,1,0:T(8,128)(2,1)S(1)} %get-tuple-element.10), channel_id=1, source_target_pairs={{0,1},{1,2},{2,3},{4,5},{5,6},{6,7},{8,9},{9,10},{10,11},{12,13},{... | collective-permute-start | bytes 442376 | tf_op jit(solution)/shard_map/ppermute | solution.py:100
  9.1 1.1 %copy-start.2 = (bf16[16,16,288]{2,1,0:T(8,128)(2,1)}, bf16[16,16,288]{2,1,0:T(8,128)(2,1)S(1)}, u32[]{:S(2)}) copy-start(bf16[16,16,288]{2,1,0:T(8,128)(2,1)S(1)} %collective-permute-done.1.high_ref) | copy-start | bytes 442372
  10.2 0.7 copy-start.3

commit v8 on v7

--- a/solution.py
+++ b/solution.py
@@ -6,7 +6,7 @@
 from jax.sharding import PartitionSpec as P
 
 HALO = 8
-EDGE = 16
+EDGE = 8
 ATOMS_DEV = 1
 
 
@@ -41,10 +41,12 @@
     )(owner, phonon, columns)
 
 
-def neighbour_kernel(index_ref, low_ref, green_ref, high_ref, superop_ref, out_ref, rows_ref, picked_ref):
+def neighbour_kernel(neighbours_ref, low_ref, green_ref, high_ref, superop_ref, out_ref, rows_ref, picked_ref):
     width = low_ref.shape[0]
     atoms, energies, comps = green_ref.shape
     slots = superop_ref.shape[0]
+    first = lax.axis_index("atoms") * atoms - width
+    empty = 2 * width + atoms
     rows_ref[:width] = low_ref[...]
     rows_ref[width:width + atoms] = green_ref[...]
     rows_ref[width + atoms:2 * width + atoms] = high_ref[...]
@@ -52,7 +54,9 @@
 
     def pick(atom, carry):
         for slot in range(slots):
-            picked_ref[slot, atom] = rows_ref[index_ref[atom * slots + slot]]
+            target = neighbours_ref[atom, slot]
+            row = jnp.where(target >= 0, target - first, empty)
+            picked_ref[slot, atom] = rows_ref[row]
         return carry
 
     lax.fori_loop(0, atoms, pick, 0, unroll=8)
@@ -66,7 +70,7 @@
     out_ref[...] = total.astype(out_ref.dtype).reshape(atoms, energies, comps)
 
 
-def neighbour_apply(index, low, green_t, high, superop):
+def neighbour_apply(neighbours, low, green_t, high, superop):
     width = low.shape[0]
     atoms, energies, comps = green_t.shape
     slots = superop.shape[0]
@@ -85,23 +89,20 @@
             bytes_accessed=2 * (2 * low.size + 2 * green_t.size + superop.size),
             transcendentals=0,
         ),
-    )(index, low, green_t, high, superop)
+    )(neighbours, low, green_t, high, superop)
 
 
 def per_device(green, superop, phonon, owner, neighbours):
     local_energies = green.shape[0]
     group_size = green.shape[1]
     comps = green.shape[2]
-    group = lax.axis_index("atoms")
     groups = lax.axis_size("atoms")
     green_t = jnp.transpose(green, (1, 0, 2))
     forward = [(i, i + 1) for i in range(groups - 1)]
     backward = [(i + 1, i) for i in range(groups - 1)]
     low = lax.ppermute(green_t[group_size - EDGE:], "atoms", forward)
     high = lax.ppermute(green_t[:EDGE], "atoms", backward)
-    present = neighbours >= 0
-    index = jnp.where(present, neighbours - group * group_size + EDGE, 2 * EDGE + group_size)
-    coupled = neighbour_apply(index.reshape(-1), low, green_t, high, superop)
+    coupled = neighbour_apply(neighbours, low, green_t, high, superop)
     count = local_energies * lax.axis_size("energy")
     peers = lax.axis_size("energy")
     outgoing = coupled.reshape(peers, 2, local_energies * comps // 2)

time: 90.2 us -> 88.3 us (0.979)
  blocking collectives: 57.9 us -> 56.9 us
    all_to_all x1, blocking collectives: 33.2 us -> 32.3 us  [per_device(): lax.all_to_all(outgoing, 'energy', split_axis=0, concat_axis=0, tiled=True)]
    unnamed x14 -> x15, local copies, waits for them, and re-layouts: 4.96 us -> 5.91 us
  transfers between devices with their start and end apart: 2 -> 2, of which waited for: 1 -> 1; matrix products, arithmetic and copies ran while one was open for 2% -> 1% of each run, Pallas kernels for 0% -> 0%
where the time goes in v8:
time: 88.3 us; the launch traced here: 87.6 us
  blocking collectives  56.9 us (64%)
  local copies, waits for them, and re-layouts  12.8 us (14%)
  Pallas kernels  9.35 us (11%)
  starting transfers between devices  5.87 us (7%)
  other arithmetic  2.26 us (3%)
    all_to_all x1, blocking collectives, per_device(): lax.all_to_all(outgoing, 'energy', split_axis=0, concat_axis=0, tiled=True)  32.3 us
    all_to_all x1, blocking collectives, per_device(): lax.all_to_all(product.reshape(count, ATOMS_DEV, comps), 'energy', split_...  24.6 us
    unnamed x15, local copies, waits for them, and re-layouts  5.91 us
    pallas_call x1, Pallas kernels, neighbour_apply(): pl.pallas_call(neighbour_kernel, out_shape=jax.ShapeDtypeStruct(green_t.s...  5.08 us
    ppermute x1, starting transfers between devices, per_device(): low = lax.ppermute(green_t[group_size - EDGE:], 'atoms', forward)  4.58 us
    pallas_call x1, Pallas kernels, toeplitz_apply(): pl.pallas_call(toeplitz_kernel, out_shape=jax.ShapeDtypeStruct((count, co...  4.26 us
    reshape x1, local copies, waits for them, and re-layouts, per_device(): outgoing = coupled.reshape(peers, 2, local_energies * comps // 2)  2.69 us
    reshape x1, other arithmetic, per_device(): product.reshape(count, ATOMS_DEV, comps)  2.26 us
  transfers between devices with their start and end apart: 2, of which 1 were waited for; matrix products, arithmetic and copies ran while one was open for 1% of the time, Pallas kernels for 0%

profile of v8, /device:TPU:1, one launch (start us, length us, event | category | flops | bytes accessed | tf_op | source)
XLA Modules:
  0.0 87.6 jit_solution(1785219727316316828)
XLA Ops:
  0.0 0.0 copy-start
  0.0 0.0 copy-start.4
  0.0 1.6 %copy.22 = bf16[16,64,288]{2,0,1:T(8,128)(2,1)S(1)} copy(bf16[16,64,288]{2,1,0:T(8,128)(2,1)} %param.5) | data formatting | bytes 1179648 | tf_op args[0]
  1.6 0.0 copy-start.1
  1.7 1.3 %collective-permute-start.1 = (bf16[8,16,288]{2,1,0:T(8,128)(2,1)S(1)}, bf16[8,16,288]{2,1,0:T(8,128)(2,1)S(1)}, u32[]{:S(2)}, u32[]{:S(2)}) collective-permute-start(bf16[8,16,288]{2,1,0:T(8,128)(2,1)S(1)} %get-tuple-element.9), channel_id=1, source_target_pairs={{1,0},{2,1},{3,2},{5,4},{6,5},{7,6},{9,8},{10,9},{11,10},{13,12},{... | collective-permute-start | bytes 221192 | tf_op jit(solution)/shard_map/ppermute | solution.py:104
  3.0 4.6 %collective-permute-start = (bf16[8,16,288]{2,1,0:T(8,128)(2,1)S(1)}, bf16[8,16,288]{2,1,0:T(8,128)(2,1)S(1)}, u32[]{:S(2)}, u32[]{:S(2)}) collective-permute-start(bf16[8,16,288]{2,1,0:T(8,128)(2,1)S(1)} %get-tuple-element.10), channel_id=1, source_target_pairs={{0,1},{1,2},{2,3},{4,5},{5,6},{6,7},{8,9},{9,10},{10,11},{12,13},{... | collective-permute-start | bytes 221192 | tf_op jit(solution)/shard_map/ppermute | solution.py:103
  7.6 0.0 copy-done.4
  7.6 0.7 copy.17.neighbours_ref
  8.3 0.0 copy-done
  8.3 0.6 constant_dynamic-slice_fusion
  8.8 0.0 collective-permute-done.1.high_ref
  8.8 0.0 copy-start.2
  8.8 0.3 collective-permute-done.low_ref
  9.2 0.0 copy-done.1
  9.2 0.3 copy-done.2
  9.5 0.0 copy-start.3
  9.5 0.6 copy-done.3
  10.1 5.1 %shard_map.55 = bf16[64,16,288]{2,1,0:T(8,128)(2,1)} custom-call(s32[64,4]{1,0:T(8,128)} %copy.17.neighbours_ref, bf16[8,16,288]{2,1,0:T(8,128)(2,1)} %copy-done.3, bf16[64,16,288]{2,1,0:T(8,128)(2,1)} %bitcast.11, bf16[8,16,288]{2,1,0:T(8,128)(2,1)} %copy-done.2, bf16[4,288,288]{2,1,0:T(8,128)(2,1)} %superop_ref.1), custom_call_target="tpu_custom_call" | custom-call | flops 679477248 | bytes 1990656 | tf_op jit(solution)/shard_map/pallas_call | solution.py:78
  15.2 2.7 %reshape.10 = bf16[64,2,2304]{2,1,0:T(2,128)(2,1)S(1)} reshape(bf16[64,16,288]{2,1,0:T(8,128)(2,1)} %shard_map.55) | data formatting | bytes 1179648 | tf_op jit(solution)/shard_map/reshape | solution.py:108
  17.9 32.3 %all_to_all.23 = bf16[64,2,2304]{2,1,0:T(2,128)(2,1)S(1)} all-to-all(bf16[64,2,2304]{2,1,0:T(2,128)(2,1)S(1)} %reshape.10), channel_id=1, replica_groups=mesh['energy'=64,'atoms'=4] {'energy'}, dimensions={0} | all-to-all | bytes 1179648 | tf_op jit(solution)/shard_map/all_to_all | solution.py:111
  50.1 2.0 %reshape.11.columns_ref = bf16[1024,288]{1,0:T(8,128)(2,1)} reshape(bf16[64,2,2304]{2,1,0:T(2,128)(2,1)S(1)} %all_to_all.23) | data formatting | bytes 1179648 | tf_op jit(solution)/shard_map/reshape | solution.py:112
  52.2 4.3 %shard_map.56 = bf16[1024,288]{1,0:T(8,128)(2,1)} custom-call(s32[1]{0:T(128)} %bitcast.owner_ref, bf16[64,2048]{1,0:T(8,128)(2,1)} %phonon_ref.1, bf16[1024,288]{1,0:T(8,128)(2,1)} %reshape.11.columns_ref), custom_call_target="tpu_custom_call" | custom-call | flops 603979776 | bytes 1441792 | tf_op jit(solution)/shard_map/pallas_call | solution.py:31
  56.4 0.5 broadcast
  57.0 2.3 %reduce = bf16[1024,288]{1,0:T(8,128)(2,1)S(1)} reduce(bf16[1024,1,288]{2,0,1:T(8,128)(2,1)} %bitcast.13, bf16[]{:T(256)} %broadcast), dimensions={1}, to_apply=%copy.18.reduce_sub_computation | reduce | bytes 1179650 | tf_op jit(solution)/shard_map/reshape | solution.py:114
  59.2 1.1 %reshape.13 = bf16[64,2,2304]{2,1,0:T(2,128)(2,1)S(1)} reshape(bf16[1024,288]{1,0:T(8,128)(2,1)S(1)} %reduce) | data formatting | bytes 1179648
  60.3 24.6 %all_to_all.24 = bf16[64,2,2304]{2,1,0:T(2,128)(2,1)S(1)} all-to-all(bf16[64,2,2304]{2,1,0:T(2,128)(2,1)S(1)} %reshape.13), channel_id=1, replica_groups=mesh['energy'=64,'atoms'=4] {'energy'}, dimensions={0} | all-to-all | bytes 1179648 | tf_op jit(solution)/shard_map/all_to_all | solution.py:113
  84.9 1.4 %reshape.14 = bf16[1024,1,288]{2,1,0:T(2,128)(2,1)S(1)} reshape(bf16[64,2,2304]{2,1,0:T(2,128)(2,1)S(1)} %all_to_all.24) | data formatting | bytes 1179648
  86.4 0.1 copy.20
  86.5 1.1 %copy.19 = bf16[16,64,288]{2,1,0:T(8,128)(2,1)} copy(bf16[16,64,288]{2,0,1:T(8,128)(2,1)S(1)} %bitcast.12) | data formatting | bytes 1179648 | tf_op jit(solution)/shard_map/all_to_all | solution.py:113
  (1 shorter events, 0.0 us)
Async XLA Ops:
  0.0 8.3 %copy-start = (s32[64,1]{0,1:T(1,128)S(1)}, s32[64,1]{0,1:T(1,128)}, u32[]{:S(2)}) copy-start(s32[64,1]{0,1:T(1,128)} %param.8) | copy-start | bytes 772
  0.0 7.6 %copy-start.4 = (s32[64,4]{0,1:T(4,128)S(1)}, s32[64,4]{0,1:T(4,128)}, u32[]{:S(2)}) copy-start(s32[64,4]{0,1:T(4,128)} %param.9) | copy-start | bytes 3076
  1.6 7.5 %copy-start.1 = (bf16[16,64,288]{2,0,1:T(8,128)(2,1)}, bf16[16,64,288]{2,0,1:T(8,128)(2,1)S(1)}, u32[]{:S(2)}) copy-start(bf16[16,64,288]{2,0,1:T(8,128)(2,1)S(1)} %copy.22) | copy-start | bytes 1769476
  1.7 7.2 %collective-permute-start.1 = (bf16[8,16,288]{2,1,0:T(8,128)(2,1)S(1)}, bf16[8,16,288]{2,1,0:T(8,128)(2,1)S(1)}, u32[]{:S(2)}, u32[]{:S(2)}) collective-permute-start(bf16[8,16,288]{2,1,0:T(8,128)(2,1)S(1)} %get-tuple-element.9), channel_id=1, source_target_pairs={{1,0},{2,1},{3,2},{5,4},{6,5},{7,6},{9,8},{10,9},{11,10},{13,12},{... | collective-permute-start | bytes 221192 | tf_op jit(solution)/shard_map/ppermute | solution.py:104
  3.0 6.2 %collective-permute-start = (bf16[8,16,288]{2,1,0:T(8,128)(2,1)S(1)}, bf16[8,16,288]{2,1,0:T(8,128)(2,1)S(1)}, u32[]{:S(2)}, u32[]{:S(2)}) collective-permute-start(bf16[8,16,288]{2,1,0:T(8,128)(2,1)S(1)} %get-tuple-element.10), channel_id=1, source_target_pairs={{0,1},{1,2},{2,3},{4,5},{5,6},{6,7},{8,9},{9,10},{10,11},{12,13},{... | collective-permute-start | bytes 221192 | tf_op jit(solution)/shard_map/ppermute | solution.py:103
  8.8 0.6 copy-start.2
  9.5 0.6 copy-start.3

commit v9 on v8

--- a/solution.py
+++ b/solution.py
@@ -110,10 +110,9 @@
     mine, outgoing = lax.optimization_barrier((mine, outgoing))
     columns = lax.all_to_all(outgoing, "energy", split_axis=0, concat_axis=0, tiled=True)
     product = toeplitz_apply(mine, phonon, columns.reshape(count, comps))
-    result = lax.all_to_all(
-        product.reshape(count, ATOMS_DEV, comps), "energy", split_axis=0, concat_axis=1, tiled=True
-    )
-    return result
+    returning = product.reshape(peers, local_energies, comps).reshape(peers, 2, local_energies * comps // 2)
+    result = lax.all_to_all(returning, "energy", split_axis=0, concat_axis=0, tiled=True)
+    return jnp.transpose(result.reshape(peers, local_energies, comps), (1, 0, 2))
 
 
 def solution(mesh):

time: 88.3 us -> 86.8 us (0.983)
  other arithmetic: 2.26 us -> 0 us
  local copies, waits for them, and re-layouts: 12.8 us -> 14.6 us
    another operation x0 -> x1, local copies, waits for them, and re-layouts: none -> 2.69 us  [per_device(): product.reshape(peers, local_energies, comps)]
    reshape x1 -> x0, other arithmetic: 2.26 us -> none  [per_device(): product.reshape(count, ATOMS_DEV, comps)]
    unnamed x15 -> x12, local copies, waits for them, and re-layouts: 5.91 us -> 4.25 us
    all_to_all x1 -> x0, local copies, waits for them, and re-layouts: 1.06 us -> none  [per_device(): lax.all_to_all(product.reshape(count, ATOMS_DEV, comps), 'energy', split_...]
    transpose x0 -> x1, local copies, waits for them, and re-layouts: none -> 1.06 us  [per_device(): jnp.transpose(result.reshape(peers, local_energies, comps), (1, 0, 2))]
  transfers between devices with their start and end apart: 2 -> 2, of which waited for: 1 -> 0; matrix products, arithmetic and copies ran while one was open for 1% -> 2% of each run, Pallas kernels for 0% -> 0%
where the time goes in v9:
time: 86.8 us; the launch traced here: 86.5 us
  blocking collectives  56.6 us (65%)
  local copies, waits for them, and re-layouts  14.6 us (17%)
  Pallas kernels  9.36 us (11%)
  starting transfers between devices  5.87 us (7%)
    all_to_all x1, blocking collectives, per_device(): lax.all_to_all(outgoing, 'energy', split_axis=0, concat_axis=0, tiled=True)  32 us
    all_to_all x1, blocking collectives, per_device(): lax.all_to_all(returning, 'energy', split_axis=0, concat_axis=0, tiled=True)  24.6 us
    pallas_call x1, Pallas kernels, neighbour_apply(): pl.pallas_call(neighbour_kernel, out_shape=jax.ShapeDtypeStruct(green_t.s...  5.07 us
    ppermute x1, starting transfers between devices, per_device(): low = lax.ppermute(green_t[group_size - EDGE:], 'atoms', forward)  4.58 us
    pallas_call x1, Pallas kernels, toeplitz_apply(): pl.pallas_call(toeplitz_kernel, out_shape=jax.ShapeDtypeStruct((count, co...  4.3 us
    unnamed x12, local copies, waits for them, and re-layouts  4.25 us
    reshape x1, local copies, waits for them, and re-layouts, per_device(): outgoing = coupled.reshape(peers, 2, local_energies * comps // 2)  2.69 us
    another operation x1, local copies, waits for them, and re-layouts, per_device(): product.reshape(peers, local_energies, comps)  2.69 us
  transfers between devices with their start and end apart: 2, of which 0 were waited for; matrix products, arithmetic and copies ran while one was open for 2% of the time, Pallas kernels for 0%

profile of v9, /device:TPU:1, one launch (start us, length us, event | category | flops | bytes accessed | tf_op | source)
XLA Modules:
  0.0 86.5 jit_solution(2664993127718846200)
XLA Ops:
  0.0 0.0 copy-start
  0.0 1.6 %copy.12 = bf16[16,64,288]{2,0,1:T(8,128)(2,1)S(1)} copy(bf16[16,64,288]{2,1,0:T(8,128)(2,1)} %param.5) | data formatting | bytes 1179648 | tf_op args[0]
  1.6 0.0 copy-start.1
  1.7 1.3 %collective-permute-start.1 = (bf16[8,16,288]{2,1,0:T(8,128)(2,1)S(1)}, bf16[8,16,288]{2,1,0:T(8,128)(2,1)S(1)}, u32[]{:S(2)}, u32[]{:S(2)}) collective-permute-start(bf16[8,16,288]{2,1,0:T(8,128)(2,1)S(1)} %get-tuple-element.9), channel_id=1, source_target_pairs={{1,0},{2,1},{3,2},{5,4},{6,5},{7,6},{9,8},{10,9},{11,10},{13,12},{... | collective-permute-start | bytes 221192 | tf_op jit(solution)/shard_map/ppermute | solution.py:104
  3.0 4.6 %collective-permute-start = (bf16[8,16,288]{2,1,0:T(8,128)(2,1)S(1)}, bf16[8,16,288]{2,1,0:T(8,128)(2,1)S(1)}, u32[]{:S(2)}, u32[]{:S(2)}) collective-permute-start(bf16[8,16,288]{2,1,0:T(8,128)(2,1)S(1)} %get-tuple-element.10), channel_id=1, source_target_pairs={{0,1},{1,2},{2,3},{4,5},{5,6},{6,7},{8,9},{9,10},{10,11},{12,13},{... | collective-permute-start | bytes 221192 | tf_op jit(solution)/shard_map/ppermute | solution.py:103
  7.5 0.0 copy-start.4
  7.6 0.7 copy-done.4
  8.2 0.7 copy.9.neighbours_ref
  8.9 0.0 copy-done
  8.9 0.6 constant_dynamic-slice_fusion
  9.6 0.0 collective-permute-done.1.high_ref
  9.6 0.0 copy-start.2
  9.6 0.0 collective-permute-done.low_ref
  9.6 0.0 copy-done.1
  9.6 0.6 copy-done.2
  10.2 0.0 copy-start.3
  10.2 0.6 copy-done.3
  10.9 5.1 %shard_map.55 = bf16[64,16,288]{2,1,0:T(8,128)(2,1)} custom-call(s32[64,4]{1,0:T(8,128)} %copy.9.neighbours_ref, bf16[8,16,288]{2,1,0:T(8,128)(2,1)} %copy-done.3, bf16[64,16,288]{2,1,0:T(8,128)(2,1)} %bitcast.6, bf16[8,16,288]{2,1,0:T(8,128)(2,1)} %copy-done.2, bf16[4,288,288]{2,1,0:T(8,128)(2,1)} %superop_ref.1), custom_call_target="tpu_custom_call" | custom-call | flops 679477248 | bytes 1990656 | tf_op jit(solution)/shard_map/pallas_call | solution.py:78
  15.9 2.7 %reshape.10 = bf16[64,2,2304]{2,1,0:T(2,128)(2,1)S(1)} reshape(bf16[64,16,288]{2,1,0:T(8,128)(2,1)} %shard_map.55) | data formatting | bytes 1179648 | tf_op jit(solution)/shard_map/reshape | solution.py:108
  18.6 32.0 %all_to_all.10 = bf16[64,2,2304]{2,1,0:T(2,128)(2,1)S(1)} all-to-all(bf16[64,2,2304]{2,1,0:T(2,128)(2,1)S(1)} %reshape.10), channel_id=1, replica_groups=mesh['energy'=64,'atoms'=4] {'energy'}, dimensions={0} | all-to-all | bytes 1179648 | tf_op jit(solution)/shard_map/all_to_all | solution.py:111
  50.6 2.0 %reshape.11.columns_ref = bf16[1024,288]{1,0:T(8,128)(2,1)} reshape(bf16[64,2,2304]{2,1,0:T(2,128)(2,1)S(1)} %all_to_all.10) | data formatting | bytes 1179648 | tf_op jit(solution)/shard_map/reshape | solution.py:112
  52.6 4.3 %shard_map.56 = bf16[1024,288]{1,0:T(8,128)(2,1)} custom-call(s32[1]{0:T(128)} %bitcast.owner_ref, bf16[64,2048]{1,0:T(8,128)(2,1)} %phonon_ref.1, bf16[1024,288]{1,0:T(8,128)(2,1)} %reshape.11.columns_ref), custom_call_target="tpu_custom_call" | custom-call | flops 603979776 | bytes 1441792 | tf_op jit(solution)/shard_map/pallas_call | solution.py:31
  56.9 2.7 %reshape_reshape.3 = bf16[64,2,2304]{2,1,0:T(2,128)(2,1)S(1)} reshape(bf16[1024,288]{1,0:T(8,128)(2,1)} %shard_map.56) | data formatting | bytes 1179648 | tf_op jit(solution)/shard_map/reshape;reshape | solution.py:113
  59.6 24.6 %all_to_all.11 = bf16[64,2,2304]{2,1,0:T(2,128)(2,1)S(1)} all-to-all(bf16[64,2,2304]{2,1,0:T(2,128)(2,1)S(1)} %reshape_reshape.3), channel_id=1, replica_groups=mesh['energy'=64,'atoms'=4] {'energy'}, dimensions={0} | all-to-all | bytes 1179648 | tf_op jit(solution)/shard_map/all_to_all | solution.py:114
  84.3 1.2 %reshape.12 = bf16[64,16,288]{2,1,0:T(8,128)(2,1)S(1)} reshape(bf16[64,2,2304]{2,1,0:T(2,128)(2,1)S(1)} %all_to_all.11) | data formatting | bytes 1179648 | tf_op jit(solution)/shard_map/reshape | solution.py:115
  85.4 1.1 %copy.10 = bf16[16,64,288]{2,1,0:T(8,128)(2,1)} copy(bf16[16,64,288]{2,0,1:T(8,128)(2,1)S(1)} %bitcast.7) | data formatting | bytes 1179648 | tf_op jit(solution)/shard_map/transpose | solution.py:115
  (1 shorter events, 0.0 us)
Async XLA Ops:
  0.0 8.9 %copy-start = (s32[64,1]{0,1:T(1,128)S(1)}, s32[64,1]{0,1:T(1,128)}, u32[]{:S(2)}) copy-start(s32[64,1]{0,1:T(1,128)} %param.8) | copy-start | bytes 772
  1.6 8.0 %copy-start.1 = (bf16[16,64,288]{2,0,1:T(8,128)(2,1)}, bf16[16,64,288]{2,0,1:T(8,128)(2,1)S(1)}, u32[]{:S(2)}) copy-start(bf16[16,64,288]{2,0,1:T(8,128)(2,1)S(1)} %copy.12) | copy-start | bytes 1769476
  1.7 7.9 %collective-permute-start.1 = (bf16[8,16,288]{2,1,0:T(8,128)(2,1)S(1)}, bf16[8,16,288]{2,1,0:T(8,128)(2,1)S(1)}, u32[]{:S(2)}, u32[]{:S(2)}) collective-permute-start(bf16[8,16,288]{2,1,0:T(8,128)(2,1)S(1)} %get-tuple-element.9), channel_id=1, source_target_pairs={{1,0},{2,1},{3,2},{5,4},{6,5},{7,6},{9,8},{10,9},{11,10},{13,12},{... | collective-permute-start | bytes 221192 | tf_op jit(solution)/shard_map/ppermute | solution.py:104
  3.0 6.6 %collective-permute-start = (bf16[8,16,288]{2,1,0:T(8,128)(2,1)S(1)}, bf16[8,16,288]{2,1,0:T(8,128)(2,1)S(1)}, u32[]{:S(2)}, u32[]{:S(2)}) collective-permute-start(bf16[8,16,288]{2,1,0:T(8,128)(2,1)S(1)} %get-tuple-element.10), channel_id=1, source_target_pairs={{0,1},{1,2},{2,3},{4,5},{5,6},{6,7},{8,9},{9,10},{10,11},{12,13},{... | collective-permute-start | bytes 221192 | tf_op jit(solution)/shard_map/ppermute | solution.py:103
  7.5 0.7 copy-start.4
  9.6 0.6 copy-start.2
  10.2 0.6 copy-start.3

commit v10 on v9

--- a/solution.py
+++ b/solution.py
@@ -10,8 +10,46 @@
 ATOMS_DEV = 1
 
 
-def toeplitz_kernel(owner_ref, phonon_ref, columns_ref, out_ref):
-    count = columns_ref.shape[0]
+def store_packed(out_ref, blocks):
+    energies, comps = blocks.shape[1], blocks.shape[2]
+    half = energies // 2
+    for h in range(2):
+        for e in range(half):
+            out_ref[:, h, e * comps:(e + 1) * comps] = blocks[:, h * half + e, :]
+
+
+def load_packed(packed_ref, blocks_ref):
+    energies, comps = blocks_ref.shape[1], blocks_ref.shape[2]
+    half = energies // 2
+    for h in range(2):
+        for e in range(half):
+            blocks_ref[:, h * half + e, :] = packed_ref[:, h, e * comps:(e + 1) * comps]
+
+
+def unpack_kernel(packed_ref, out_ref):
+    energies, comps = out_ref.shape[0], out_ref.shape[2]
+    half = energies // 2
+    for h in range(2):
+        for e in range(half):
+            out_ref[h * half + e] = packed_ref[:, h, e * comps:(e + 1) * comps]
+
+
+def unpack(packed, energies):
+    atoms = packed.shape[0]
+    comps = packed.shape[2] * 2 // energies
+    vmem = pl.BlockSpec(memory_space=pltpu.VMEM)
+    return pl.pallas_call(
+        unpack_kernel,
+        out_shape=jax.ShapeDtypeStruct((energies, atoms, comps), packed.dtype),
+        in_specs=[vmem],
+        out_specs=vmem,
+    )(packed)
+
+
+def toeplitz_kernel(owner_ref, phonon_ref, packed_ref, out_ref, blocks_ref):
+    peers, energies, comps = blocks_ref.shape
+    count = peers * energies
+    load_packed(packed_ref, blocks_ref)
     domain = owner_ref[0]
     base = pl.multiple_of((domain // 16) * 16, 16)
     block = phonon_ref[pl.ds(base, 16), :].astype(jnp.float32)
@@ -20,25 +58,30 @@
     wide = jnp.broadcast_to(row, (count, 2 * count))
     rolled = pltpu.roll(wide, shift=count, axis=1, stride=1, stride_axis=0)
     kernel_t = rolled[:, :count].astype(jnp.bfloat16)
-    out_ref[...] = lax.dot_general(
-        kernel_t, columns_ref[...], (((0,), (0,)), ((), ())), preferred_element_type=jnp.float32
-    ).astype(out_ref.dtype)
+    product = lax.dot_general(
+        kernel_t, blocks_ref[...].reshape(count, comps), (((0,), (0,)), ((), ())),
+        preferred_element_type=jnp.float32,
+    )
+    store_packed(out_ref, product.astype(out_ref.dtype).reshape(peers, energies, comps))
 
 
-def toeplitz_apply(owner, phonon, columns):
-    count, comps = columns.shape
+def toeplitz_apply(owner, phonon, packed, energies):
+    peers = packed.shape[0]
+    comps = packed.shape[2] * 2 // energies
+    count = peers * energies
     vmem = pl.BlockSpec(memory_space=pltpu.VMEM)
     return pl.pallas_call(
         toeplitz_kernel,
-        out_shape=jax.ShapeDtypeStruct((count, comps), jnp.bfloat16),
+        out_shape=jax.ShapeDtypeStruct(packed.shape, jnp.bfloat16),
         in_specs=[pl.BlockSpec(memory_space=pltpu.SMEM), vmem, vmem],
         out_specs=vmem,
+        scratch_shapes=[pltpu.VMEM((peers, energies, comps), jnp.bfloat16)],
         cost_estimate=pl.CostEstimate(
             flops=2 * count * count * comps,
             bytes_accessed=2 * (phonon.size + 2 * count * comps),
             transcendentals=0,
         ),
-    )(owner, phonon, columns)
+    )(owner, phonon, packed)
 
 
 def neighbour_kernel(neighbours_ref, low_ref, green_ref, high_ref, superop_ref, out_ref, rows_ref, picked_ref):
@@ -67,7 +110,7 @@
             superop_ref[slot],
             preferred_element_type=jnp.float32,
         )
-    out_ref[...] = total.astype(out_ref.dtype).reshape(atoms, energies, comps)
+    store_packed(out_ref, total.astype(out_ref.dtype).reshape(atoms, energies, comps))
 
 
 def neighbour_apply(neighbours, low, green_t, high, superop):
@@ -77,7 +120,7 @@
     vmem = pl.BlockSpec(memory_space=pltpu.VMEM)
     return pl.pallas_call(
         neighbour_kernel,
-        out_shape=jax.ShapeDtypeStruct(green_t.shape, jnp.bfloat16),
+        out_shape=jax.ShapeDtypeStruct((atoms, 2, energies * comps // 2), jnp.bfloat16),
         in_specs=[pl.BlockSpec(memory_space=pltpu.SMEM)] + [vmem] * 4,
         out_specs=vmem,
         scratch_shapes=[
@@ -102,17 +145,13 @@
     backward = [(i + 1, i) for i in range(groups - 1)]
     low = lax.ppermute(green_t[group_size - EDGE:], "atoms", forward)
     high = lax.ppermute(green_t[:EDGE], "atoms", backward)
-    coupled = neighbour_apply(neighbours, low, green_t, high, superop)
-    count = local_energies * lax.axis_size("energy")
-    peers = lax.axis_size("energy")
-    outgoing = coupled.reshape(peers, 2, local_energies * comps // 2)
+    outgoing = neighbour_apply(neighbours, low, green_t, high, superop)
     mine = lax.dynamic_slice_in_dim(owner[:, 0], lax.axis_index("energy"), 1)
     mine, outgoing = lax.optimization_barrier((mine, outgoing))
     columns = lax.all_to_all(outgoing, "energy", split_axis=0, concat_axis=0, tiled=True)
-    product = toeplitz_apply(mine, phonon, columns.reshape(count, comps))
-    returning = product.reshape(peers, local_energies, comps).reshape(peers, 2, local_energies * comps // 2)
-    result = lax.all_to_all(returning, "energy", split_axis=0, concat_axis=0, tiled=True)
-    return jnp.transpose(result.reshape(peers, local_energies, comps), (1, 0, 2))
+    product = toeplitz_apply(mine, phonon, columns, local_energies)
+    result = lax.all_to_all(product, "energy", split_axis=0, concat_axis=0, tiled=True)
+    return unpack(result, local_energies)
 
 
 def solution(mesh):

time: 86.8 us -> 85.1 us (0.980)
  local copies, waits for them, and re-layouts: 14.6 us -> 4.87 us
  Pallas kernels: 9.36 us -> 16.7 us
    pallas_call x2 -> x3, Pallas kernels: 9.36 us -> 16.7 us  [the longest x1 6.74 us: toeplitz_apply(): pl.pallas_call(toeplitz_kernel, out_shape=jax.ShapeDtypeStruct(packed.sha...]
    reshape x3 -> x0, local copies, waits for them, and re-layouts: 5.9 us -> none  [the longest x1 2.69 us: per_device(): outgoing = coupled.reshape(peers, 2, local_energies * comps // 2)]
    another operation x1 -> x0, local copies, waits for them, and re-layouts: 2.69 us -> none  [per_device(): product.reshape(peers, local_energies, comps)]
    transpose x1 -> x0, local copies, waits for them, and re-layouts: 1.06 us -> none  [per_device(): jnp.transpose(result.reshape(peers, local_energies, comps), (1, 0, 2))]
where the time goes in v10:
time: 85.1 us; the launch traced here: 84.7 us
  blocking collectives  57.2 us (67%)
  Pallas kernels  16.7 us (20%)
  starting transfers between devices  5.87 us (7%)
  local copies, waits for them, and re-layouts  4.87 us (6%)
    all_to_all x1, blocking collectives, per_device(): lax.all_to_all(outgoing, 'energy', split_axis=0, concat_axis=0, tiled=True)  32.3 us
    all_to_all x1, blocking collectives, per_device(): lax.all_to_all(product, 'energy', split_axis=0, concat_axis=0, tiled=True)  24.9 us
    pallas_call x1, Pallas kernels, toeplitz_apply(): pl.pallas_call(toeplitz_kernel, out_shape=jax.ShapeDtypeStruct(packed.sha...  6.74 us
    pallas_call x1, Pallas kernels, neighbour_apply(): pl.pallas_call(neighbour_kernel, out_shape=jax.ShapeDtypeStruct((atoms, 2...  6.07 us
    ppermute x1, starting transfers between devices, per_device(): low = lax.ppermute(green_t[group_size - EDGE:], 'atoms', forward)  4.58 us
    unnamed x12, local copies, waits for them, and re-layouts  4.23 us
    pallas_call x1, Pallas kernels, unpack(): pl.pallas_call(unpack_kernel, out_shape=jax.ShapeDtypeStruct((energies, a...  3.86 us
  transfers between devices with their start and end apart: 2, of which 0 were waited for; matrix products, arithmetic and copies ran while one was open for 2% of the time, Pallas kernels for 0%

profile of v10, /device:TPU:1, one launch (start us, length us, event | category | flops | bytes accessed | tf_op | source)
XLA Modules:
  0.0 84.7 jit_solution(9855991431248323482)
XLA Ops:
  0.0 0.0 copy-start
  0.0 1.6 %copy.9 = bf16[16,64,288]{2,0,1:T(8,128)(2,1)S(1)} copy(bf16[16,64,288]{2,1,0:T(8,128)(2,1)} %param.5) | data formatting | bytes 1179648 | tf_op args[0]
  1.6 0.0 copy-start.1
  1.7 1.3 %collective-permute-start.1 = (bf16[8,16,288]{2,1,0:T(8,128)(2,1)S(1)}, bf16[8,16,288]{2,1,0:T(8,128)(2,1)S(1)}, u32[]{:S(2)}, u32[]{:S(2)}) collective-permute-start(bf16[8,16,288]{2,1,0:T(8,128)(2,1)S(1)} %get-tuple-element.9), channel_id=1, source_target_pairs={{1,0},{2,1},{3,2},{5,4},{6,5},{7,6},{9,8},{10,9},{11,10},{13,12},{... | collective-permute-start | bytes 221192 | tf_op jit(solution)/shard_map/ppermute | solution.py:147
  3.0 4.6 %collective-permute-start = (bf16[8,16,288]{2,1,0:T(8,128)(2,1)S(1)}, bf16[8,16,288]{2,1,0:T(8,128)(2,1)S(1)}, u32[]{:S(2)}, u32[]{:S(2)}) collective-permute-start(bf16[8,16,288]{2,1,0:T(8,128)(2,1)S(1)} %get-tuple-element.10), channel_id=1, source_target_pairs={{0,1},{1,2},{2,3},{4,5},{5,6},{6,7},{8,9},{9,10},{10,11},{12,13},{... | collective-permute-start | bytes 221192 | tf_op jit(solution)/shard_map/ppermute | solution.py:146
  7.5 0.0 copy-start.2
  7.6 0.7 copy-done.2
  8.2 0.7 copy.7.neighbours_ref
  8.9 0.0 copy-done
  8.9 0.6 constant_dynamic-slice_fusion
  9.5 0.0 collective-permute-done.1.high_ref
  9.5 0.0 copy-start.3
  9.5 0.0 collective-permute-done.low_ref
  9.6 0.0 copy-done.1
  9.6 0.6 copy-done.3
  10.2 0.0 copy-start.4
  10.2 0.6 copy-done.4
  10.8 6.1 %shard_map.55 = bf16[64,2,2304]{2,1,0:T(2,128)(2,1)} custom-call(s32[64,4]{1,0:T(8,128)} %copy.7.neighbours_ref, bf16[8,16,288]{2,1,0:T(8,128)(2,1)} %copy-done.4, bf16[64,16,288]{2,1,0:T(8,128)(2,1)} %bitcast.5, bf16[8,16,288]{2,1,0:T(8,128)(2,1)} %copy-done.3, bf16[4,288,288]{2,1,0:T(8,128)(2,1)} %superop_ref.1), custom_call_target="tpu_custom_call" | custom-call | flops 679477248 | bytes 1990656 | tf_op jit(solution)/shard_map/pallas_call | solution.py:121
  16.9 32.3 %all_to_all.10.packed_ref = bf16[64,2,2304]{2,1,0:T(2,128)(2,1)} all-to-all(bf16[64,2,2304]{2,1,0:T(2,128)(2,1)} %shard_map.55), channel_id=1, replica_groups=mesh['energy'=64,'atoms'=4] {'energy'}, dimensions={0} | all-to-all | bytes 1179648 | tf_op jit(solution)/shard_map/all_to_all | solution.py:151
  49.2 6.7 %shard_map.56 = bf16[64,2,2304]{2,1,0:T(2,128)(2,1)} custom-call(s32[1]{0:T(128)} %bitcast.owner_ref, bf16[64,2048]{1,0:T(8,128)(2,1)} %phonon_ref.1, bf16[64,2,2304]{2,1,0:T(2,128)(2,1)} %all_to_all.10.packed_ref), custom_call_target="tpu_custom_call" | custom-call | flops 603979776 | bytes 1441792 | tf_op jit(solution)/shard_map/pallas_call | solution.py:73
  55.9 24.9 %all_to_all.11.packed_ref = bf16[64,2,2304]{2,1,0:T(2,128)(2,1)} all-to-all(bf16[64,2,2304]{2,1,0:T(2,128)(2,1)} %shard_map.56), channel_id=1, replica_groups=mesh['energy'=64,'atoms'=4] {'energy'}, dimensions={0} | all-to-all | bytes 1179648 | tf_op jit(solution)/shard_map/all_to_all | solution.py:153
  80.8 3.9 %shard_map.57 = bf16[16,64,288]{2,1,0:T(8,128)(2,1)} custom-call(bf16[64,2,2304]{2,1,0:T(2,128)(2,1)} %all_to_all.11.packed_ref), custom_call_target="tpu_custom_call" | custom-call | tf_op jit(solution)/shard_map/pallas_call | solution.py:41
  (1 shorter events, 0.0 us)
Async XLA Ops:
  0.0 8.9 %copy-start = (s32[64,1]{0,1:T(1,128)S(1)}, s32[64,1]{0,1:T(1,128)}, u32[]{:S(2)}) copy-start(s32[64,1]{0,1:T(1,128)} %param.8) | copy-start | bytes 772
  1.6 7.9 %copy-start.1 = (bf16[16,64,288]{2,0,1:T(8,128)(2,1)}, bf16[16,64,288]{2,0,1:T(8,128)(2,1)S(1)}, u32[]{:S(2)}) copy-start(bf16[16,64,288]{2,0,1:T(8,128)(2,1)S(1)} %copy.9) | copy-start | bytes 1769476
  1.7 7.9 %collective-permute-start.1 = (bf16[8,16,288]{2,1,0:T(8,128)(2,1)S(1)}, bf16[8,16,288]{2,1,0:T(8,128)(2,1)S(1)}, u32[]{:S(2)}, u32[]{:S(2)}) collective-permute-start(bf16[8,16,288]{2,1,0:T(8,128)(2,1)S(1)} %get-tuple-element.9), channel_id=1, source_target_pairs={{1,0},{2,1},{3,2},{5,4},{6,5},{7,6},{9,8},{10,9},{11,10},{13,12},{... | collective-permute-start | bytes 221192 | tf_op jit(solution)/shard_map/ppermute | solution.py:147
  3.0 6.6 %collective-permute-start = (bf16[8,16,288]{2,1,0:T(8,128)(2,1)S(1)}, bf16[8,16,288]{2,1,0:T(8,128)(2,1)S(1)}, u32[]{:S(2)}, u32[]{:S(2)}) collective-permute-start(bf16[8,16,288]{2,1,0:T(8,128)(2,1)S(1)} %get-tuple-element.10), channel_id=1, source_target_pairs={{0,1},{1,2},{2,3},{4,5},{5,6},{6,7},{8,9},{9,10},{10,11},{12,13},{... | collective-permute-start | bytes 221192 | tf_op jit(solution)/shard_map/ppermute | solution.py:146
  7.5 0.7 copy-start.2
  9.5 0.6 copy-start.3
  10.2 0.6 copy-start.4

commit v11 on v10

--- a/solution.py
+++ b/solution.py
@@ -24,26 +24,6 @@
     for h in range(2):
         for e in range(half):
             blocks_ref[:, h * half + e, :] = packed_ref[:, h, e * comps:(e + 1) * comps]
-
-
-def unpack_kernel(packed_ref, out_ref):
-    energies, comps = out_ref.shape[0], out_ref.shape[2]
-    half = energies // 2
-    for h in range(2):
-        for e in range(half):
-            out_ref[h * half + e] = packed_ref[:, h, e * comps:(e + 1) * comps]
-
-
-def unpack(packed, energies):
-    atoms = packed.shape[0]
-    comps = packed.shape[2] * 2 // energies
-    vmem = pl.BlockSpec(memory_space=pltpu.VMEM)
-    return pl.pallas_call(
-        unpack_kernel,
-        out_shape=jax.ShapeDtypeStruct((energies, atoms, comps), packed.dtype),
-        in_specs=[vmem],
-        out_specs=vmem,
-    )(packed)
 
 
 def toeplitz_kernel(owner_ref, phonon_ref, packed_ref, out_ref, blocks_ref):
@@ -151,7 +131,8 @@
     columns = lax.all_to_all(outgoing, "energy", split_axis=0, concat_axis=0, tiled=True)
     product = toeplitz_apply(mine, phonon, columns, local_energies)
     result = lax.all_to_all(product, "energy", split_axis=0, concat_axis=0, tiled=True)
-    return unpack(result, local_energies)
+    result = result.reshape(result.shape[0], local_energies, comps)
+    return jnp.transpose(result, (1, 0, 2))
 
 
 def solution(mesh):

time: 85.1 us -> 83.3 us (0.979)
  Pallas kernels: 16.7 us -> 12.8 us
  local copies, waits for them, and re-layouts: 4.87 us -> 7.09 us
    pallas_call x1 -> x0, Pallas kernels: 3.86 us -> none  [unpack(): pl.pallas_call(unpack_kernel, out_shape=jax.ShapeDtypeStruct((energies, a...]
    reshape x0 -> x2, local copies, waits for them, and re-layouts: none -> 2.22 us  [per_device(): result = result.reshape(result.shape[0], local_energies, comps)]
where the time goes in v11:
time: 83.3 us; the launch traced here: 82.9 us
  blocking collectives  57.1 us (69%)
  Pallas kernels  12.8 us (15%)
  local copies, waits for them, and re-layouts  7.09 us (9%)
  starting transfers between devices  5.87 us (7%)
    all_to_all x1, blocking collectives, per_device(): lax.all_to_all(outgoing, 'energy', split_axis=0, concat_axis=0, tiled=True)  32.3 us
    all_to_all x1, blocking collectives, per_device(): lax.all_to_all(product, 'energy', split_axis=0, concat_axis=0, tiled=True)  24.8 us
    pallas_call x1, Pallas kernels, toeplitz_apply(): pl.pallas_call(toeplitz_kernel, out_shape=jax.ShapeDtypeStruct(packed.sha...  6.74 us
    pallas_call x1, Pallas kernels, neighbour_apply(): pl.pallas_call(neighbour_kernel, out_shape=jax.ShapeDtypeStruct((atoms, 2...  6.07 us
    ppermute x1, starting transfers between devices, per_device(): low = lax.ppermute(green_t[group_size - EDGE:], 'atoms', forward)  4.58 us
    unnamed x12, local copies, waits for them, and re-layouts  4.23 us
    reshape x2, local copies, waits for them, and re-layouts, per_device(): result = result.reshape(result.shape[0], local_energies, comps)  2.22 us
  transfers between devices with their start and end apart: 2, of which 0 were waited for; matrix products, arithmetic and copies ran while one was open for 2% of the time, Pallas kernels for 0%

profile of v11, /device:TPU:1, one launch (start us, length us, event | category | flops | bytes accessed | tf_op | source)
XLA Modules:
  0.0 82.9 jit_solution(5675169949017704115)
XLA Ops:
  0.0 0.0 copy-start
  0.0 1.6 %copy.12 = bf16[16,64,288]{2,0,1:T(8,128)(2,1)S(1)} copy(bf16[16,64,288]{2,1,0:T(8,128)(2,1)} %param.5) | data formatting | bytes 1179648 | tf_op args[0]
  1.6 0.0 copy-start.1
  1.7 1.3 %collective-permute-start.1 = (bf16[8,16,288]{2,1,0:T(8,128)(2,1)S(1)}, bf16[8,16,288]{2,1,0:T(8,128)(2,1)S(1)}, u32[]{:S(2)}, u32[]{:S(2)}) collective-permute-start(bf16[8,16,288]{2,1,0:T(8,128)(2,1)S(1)} %get-tuple-element.9), channel_id=1, source_target_pairs={{1,0},{2,1},{3,2},{5,4},{6,5},{7,6},{9,8},{10,9},{11,10},{13,12},{... | collective-permute-start | bytes 221192 | tf_op jit(solution)/shard_map/ppermute | solution.py:127
  3.0 4.6 %collective-permute-start = (bf16[8,16,288]{2,1,0:T(8,128)(2,1)S(1)}, bf16[8,16,288]{2,1,0:T(8,128)(2,1)S(1)}, u32[]{:S(2)}, u32[]{:S(2)}) collective-permute-start(bf16[8,16,288]{2,1,0:T(8,128)(2,1)S(1)} %get-tuple-element.10), channel_id=1, source_target_pairs={{0,1},{1,2},{2,3},{4,5},{5,6},{6,7},{8,9},{9,10},{10,11},{12,13},{... | collective-permute-start | bytes 221192 | tf_op jit(solution)/shard_map/ppermute | solution.py:126
  7.5 0.0 copy-start.2
  7.6 0.7 copy-done.2
  8.2 0.7 copy.7.neighbours_ref
  8.9 0.0 copy-done
  8.9 0.6 constant_dynamic-slice_fusion
  9.5 0.0 collective-permute-done.1.high_ref
  9.5 0.0 copy-start.3
  9.5 0.0 collective-permute-done.low_ref
  9.6 0.0 copy-done.1
  9.6 0.6 copy-done.3
  10.2 0.0 copy-start.4
  10.2 0.6 copy-done.4
  10.8 6.1 %shard_map.55 = bf16[64,2,2304]{2,1,0:T(2,128)(2,1)} custom-call(s32[64,4]{1,0:T(8,128)} %copy.7.neighbours_ref, bf16[8,16,288]{2,1,0:T(8,128)(2,1)} %copy-done.4, bf16[64,16,288]{2,1,0:T(8,128)(2,1)} %bitcast.8, bf16[8,16,288]{2,1,0:T(8,128)(2,1)} %copy-done.3, bf16[4,288,288]{2,1,0:T(8,128)(2,1)} %superop_ref.1), custom_call_target="tpu_custom_call" | custom-call | flops 679477248 | bytes 1990656 | tf_op jit(solution)/shard_map/pallas_call | solution.py:101
  16.9 32.3 %all_to_all.10.packed_ref = bf16[64,2,2304]{2,1,0:T(2,128)(2,1)} all-to-all(bf16[64,2,2304]{2,1,0:T(2,128)(2,1)} %shard_map.55), channel_id=1, replica_groups=mesh['energy'=64,'atoms'=4] {'energy'}, dimensions={0} | all-to-all | bytes 1179648 | tf_op jit(solution)/shard_map/all_to_all | solution.py:131
  49.2 6.7 %shard_map.56 = bf16[64,2,2304]{2,1,0:T(2,128)(2,1)} custom-call(s32[1]{0:T(128)} %bitcast.owner_ref, bf16[64,2048]{1,0:T(8,128)(2,1)} %phonon_ref.1, bf16[64,2,2304]{2,1,0:T(2,128)(2,1)} %all_to_all.10.packed_ref), custom_call_target="tpu_custom_call" | custom-call | flops 603979776 | bytes 1441792 | tf_op jit(solution)/shard_map/pallas_call | solution.py:53
  55.9 24.8 %all_to_all.11 = bf16[64,2,2304]{2,1,0:T(2,128)(2,1)S(1)} all-to-all(bf16[64,2,2304]{2,1,0:T(2,128)(2,1)} %shard_map.56), channel_id=1, replica_groups=mesh['energy'=64,'atoms'=4] {'energy'}, dimensions={0} | all-to-all | bytes 1179648 | tf_op jit(solution)/shard_map/all_to_all | solution.py:133
  80.7 1.2 %reshape.4 = bf16[64,16,288]{2,1,0:T(8,128)(2,1)S(1)} reshape(bf16[64,2,2304]{2,1,0:T(2,128)(2,1)S(1)} %all_to_all.11) | data formatting | bytes 1179648 | tf_op jit(solution)/shard_map/reshape | solution.py:134
  81.9 1.1 %copy.11 = bf16[64,16,288]{2,0,1:T(8,128)(2,1)} copy(bf16[64,16,288]{2,1,0:T(8,128)(2,1)S(1)} %reshape.4) | data formatting | bytes 1179648 | tf_op jit(solution)/shard_map/reshape | solution.py:134
  (1 shorter events, 0.0 us)
Async XLA Ops:
  0.0 8.9 %copy-start = (s32[64,1]{0,1:T(1,128)S(1)}, s32[64,1]{0,1:T(1,128)}, u32[]{:S(2)}) copy-start(s32[64,1]{0,1:T(1,128)} %param.8) | copy-start | bytes 772
  1.6 7.9 %copy-start.1 = (bf16[16,64,288]{2,0,1:T(8,128)(2,1)}, bf16[16,64,288]{2,0,1:T(8,128)(2,1)S(1)}, u32[]{:S(2)}) copy-start(bf16[16,64,288]{2,0,1:T(8,128)(2,1)S(1)} %copy.12) | copy-start | bytes 1769476
  1.7 7.9 %collective-permute-start.1 = (bf16[8,16,288]{2,1,0:T(8,128)(2,1)S(1)}, bf16[8,16,288]{2,1,0:T(8,128)(2,1)S(1)}, u32[]{:S(2)}, u32[]{:S(2)}) collective-permute-start(bf16[8,16,288]{2,1,0:T(8,128)(2,1)S(1)} %get-tuple-element.9), channel_id=1, source_target_pairs={{1,0},{2,1},{3,2},{5,4},{6,5},{7,6},{9,8},{10,9},{11,10},{13,12},{... | collective-permute-start | bytes 221192 | tf_op jit(solution)/shard_map/ppermute | solution.py:127
  3.0 6.6 %collective-permute-start = (bf16[8,16,288]{2,1,0:T(8,128)(2,1)S(1)}, bf16[8,16,288]{2,1,0:T(8,128)(2,1)S(1)}, u32[]{:S(2)}, u32[]{:S(2)}) collective-permute-start(bf16[8,16,288]{2,1,0:T(8,128)(2,1)S(1)} %get-tuple-element.10), channel_id=1, source_target_pairs={{0,1},{1,2},{2,3},{4,5},{5,6},{6,7},{8,9},{9,10},{10,11},{12,13},{... | collective-permute-start | bytes 221192 | tf_op jit(solution)/shard_map/ppermute | solution.py:126
  7.5 0.7 copy-start.2
  9.5 0.6 copy-start.3
  10.2 0.6 copy-start.4

commit v12 on v11

--- a/solution.py
+++ b/solution.py
@@ -30,7 +30,7 @@
     peers, energies, comps = blocks_ref.shape
     count = peers * energies
     load_packed(packed_ref, blocks_ref)
-    domain = owner_ref[0]
+    domain = owner_ref[0, lax.axis_index("energy")]
     base = pl.multiple_of((domain // 16) * 16, 16)
     block = phonon_ref[pl.ds(base, 16), :].astype(jnp.float32)
     rows = lax.broadcasted_iota(jnp.int32, block.shape, 0)
@@ -65,19 +65,20 @@
 
 
 def neighbour_kernel(neighbours_ref, low_ref, green_ref, high_ref, superop_ref, out_ref, rows_ref, picked_ref):
-    width = low_ref.shape[0]
+    width = low_ref.shape[1]
     atoms, energies, comps = green_ref.shape
     slots = superop_ref.shape[0]
     first = lax.axis_index("atoms") * atoms - width
     empty = 2 * width + atoms
-    rows_ref[:width] = low_ref[...]
     rows_ref[width:width + atoms] = green_ref[...]
-    rows_ref[width + atoms:2 * width + atoms] = high_ref[...]
+    for atom in range(width):
+        rows_ref[atom] = low_ref[:, atom, :]
+        rows_ref[width + atoms + atom] = high_ref[:, atom, :]
     rows_ref[2 * width + atoms] = jnp.zeros((energies, comps), rows_ref.dtype)
 
     def pick(atom, carry):
         for slot in range(slots):
-            target = neighbours_ref[atom, slot]
+            target = neighbours_ref[slot, atom]
             row = jnp.where(target >= 0, target - first, empty)
             picked_ref[slot, atom] = rows_ref[row]
         return carry
@@ -94,7 +95,7 @@
 
 
 def neighbour_apply(neighbours, low, green_t, high, superop):
-    width = low.shape[0]
+    width = low.shape[1]
     atoms, energies, comps = green_t.shape
     slots = superop.shape[0]
     vmem = pl.BlockSpec(memory_space=pltpu.VMEM)
@@ -123,13 +124,12 @@
     green_t = jnp.transpose(green, (1, 0, 2))
     forward = [(i, i + 1) for i in range(groups - 1)]
     backward = [(i + 1, i) for i in range(groups - 1)]
-    low = lax.ppermute(green_t[group_size - EDGE:], "atoms", forward)
-    high = lax.ppermute(green_t[:EDGE], "atoms", backward)
-    outgoing = neighbour_apply(neighbours, low, green_t, high, superop)
-    mine = lax.dynamic_slice_in_dim(owner[:, 0], lax.axis_index("energy"), 1)
-    mine, outgoing = lax.optimization_barrier((mine, outgoing))
+    low = lax.ppermute(green[:, group_size - EDGE:], "atoms", forward)
+    high = lax.ppermute(green[:, :EDGE], "atoms", backward)
+    outgoing = neighbour_apply(neighbours.T, low, green_t, high, superop)
+    owner_t, outgoing = lax.optimization_barrier((owner.T, outgoing))
     columns = lax.all_to_all(outgoing, "energy", split_axis=0, concat_axis=0, tiled=True)
-    product = toeplitz_apply(mine, phonon, columns, local_energies)
+    product = toeplitz_apply(owner_t, phonon, columns, local_energies)
     result = lax.all_to_all(product, "energy", split_axis=0, concat_axis=0, tiled=True)
     result = result.reshape(result.shape[0], local_energies, comps)
     return jnp.transpose(result, (1, 0, 2))

time: 83.3 us -> 82.4 us (0.989)
    unnamed x12 -> x5, local copies, waits for them, and re-layouts: 4.23 us -> 3.13 us
    slice x1, local copies, waits for them, and re-layouts: 0.02 us -> 0.96 us  [per_device(): high = lax.ppermute(green[:, :EDGE], 'atoms', backward)]
  transfers between devices with their start and end apart: 2 -> 2, of which waited for: 0 -> 0; matrix products, arithmetic and copies ran while one was open for 2% -> 3% of each run, Pallas kernels for 0% -> 0%
where the time goes in v12:
time: 82.4 us; the launch traced here: 81.9 us
  blocking collectives  57.1 us (69%)
  Pallas kernels  12.6 us (15%)
  local copies, waits for them, and re-layouts  6.31 us (8%)
  starting transfers between devices  5.87 us (7%)
    all_to_all x1, blocking collectives, per_device(): lax.all_to_all(outgoing, 'energy', split_axis=0, concat_axis=0, tiled=True)  32.3 us
    all_to_all x1, blocking collectives, per_device(): lax.all_to_all(product, 'energy', split_axis=0, concat_axis=0, tiled=True)  24.9 us
    pallas_call x1, Pallas kernels, neighbour_apply(): pl.pallas_call(neighbour_kernel, out_shape=jax.ShapeDtypeStruct((atoms, 2...  6.48 us
    pallas_call x1, Pallas kernels, toeplitz_apply(): pl.pallas_call(toeplitz_kernel, out_shape=jax.ShapeDtypeStruct(packed.sha...  6.11 us
    ppermute x1, starting transfers between devices, per_device(): low = lax.ppermute(green[:, group_size - EDGE:], 'atoms', forward)  4.58 us
    unnamed x5, local copies, waits for them, and re-layouts  3.13 us
    reshape x2, local copies, waits for them, and re-layouts, per_device(): result = result.reshape(result.shape[0], local_energies, comps)  2.22 us
  transfers between devices with their start and end apart: 2, of which 0 were waited for; matrix products, arithmetic and copies ran while one was open for 3% of the time, Pallas kernels for 0%

profile of v12, /device:TPU:1, one launch (start us, length us, event | category | flops | bytes accessed | tf_op | source)
XLA Modules:
  0.0 81.9 jit_solution(2367378930506576108)
XLA Ops:
  0.0 1.0 %fusion = (bf16[16,8,288]{2,1,0:T(8,128)(2,1)S(1)}, bf16[16,8,288]{2,1,0:T(8,128)(2,1)S(1)}) fusion(bf16[16,64,288]{2,1,0:T(8,128)(2,1)} %param.5), kind=kLoop, calls=%fused_computation.2 | loop fusion | bytes 294912 | tf_op jit(solution)/shard_map/slice | solution.py:128
  1.0 1.3 %collective-permute-start.1 = (bf16[16,8,288]{2,1,0:T(8,128)(2,1)S(1)}, bf16[16,8,288]{2,1,0:T(8,128)(2,1)S(1)}, u32[]{:S(2)}, u32[]{:S(2)}) collective-permute-start(bf16[16,8,288]{2,1,0:T(8,128)(2,1)S(1)} %get-tuple-element.9), channel_id=1, source_target_pairs={{1,0},{2,1},{3,2},{5,4},{6,5},{7,6},{9,8},{10,9},{11,10},{13,12},{... | collective-permute-start | bytes 221192 | tf_op jit(solution)/shard_map/ppermute | solution.py:128
  2.3 4.6 %collective-permute-start = (bf16[16,8,288]{2,1,0:T(8,128)(2,1)S(1)}, bf16[16,8,288]{2,1,0:T(8,128)(2,1)S(1)}, u32[]{:S(2)}, u32[]{:S(2)}) collective-permute-start(bf16[16,8,288]{2,1,0:T(8,128)(2,1)S(1)} %get-tuple-element.10), channel_id=1, source_target_pairs={{0,1},{1,2},{2,3},{4,5},{5,6},{6,7},{8,9},{9,10},{10,11},{12,13},{... | collective-permute-start | bytes 221192 | tf_op jit(solution)/shard_map/ppermute | solution.py:127
  6.9 2.5 %copy.11 = bf16[16,64,288]{2,0,1:T(8,128)(2,1)} copy(bf16[16,64,288]{2,1,0:T(8,128)(2,1)} %param.5) | data formatting | bytes 1179648 | tf_op args[0]
  9.3 0.0 collective-permute-done.1.high_ref
  9.3 0.0 copy-start
  9.3 0.0 collective-permute-done.low_ref
  9.3 0.0 copy-start.1
  9.3 0.6 copy-done
  10.0 0.0 copy-done.1
  10.0 6.5 %shard_map.55 = bf16[64,2,2304]{2,1,0:T(2,128)(2,1)} custom-call(s32[4,64]{1,0:T(4,128)} %bitcast.9, bf16[16,8,288]{2,1,0:T(8,128)(2,1)} %copy-done.1, bf16[64,16,288]{2,1,0:T(8,128)(2,1)} %bitcast.8, bf16[16,8,288]{2,1,0:T(8,128)(2,1)} %copy-done, bf16[4,288,288]{2,1,0:T(8,128)(2,1)} %superop_ref.1), custom_call_target="tpu_custom_call" | custom-call | flops 679477248 | bytes 1990656 | tf_op jit(solution)/shard_map/pallas_call | solution.py:102
  16.5 32.3 %all_to_all.10.packed_ref = bf16[64,2,2304]{2,1,0:T(2,128)(2,1)} all-to-all(bf16[64,2,2304]{2,1,0:T(2,128)(2,1)} %shard_map.55), channel_id=1, replica_groups=mesh['energy'=64,'atoms'=4] {'energy'}, dimensions={0} | all-to-all | bytes 1179648 | tf_op jit(solution)/shard_map/all_to_all | solution.py:131
  48.8 6.1 %shard_map.56 = bf16[64,2,2304]{2,1,0:T(2,128)(2,1)} custom-call(s32[1,64]{1,0:T(1,128)} %bitcast.10, bf16[64,2048]{1,0:T(8,128)(2,1)} %phonon_ref.1, bf16[64,2,2304]{2,1,0:T(2,128)(2,1)} %all_to_all.10.packed_ref), custom_call_target="tpu_custom_call" | custom-call | flops 603979776 | bytes 1441792 | tf_op jit(solution)/shard_map/pallas_call | solution.py:53
  54.9 24.9 %all_to_all.11 = bf16[64,2,2304]{2,1,0:T(2,128)(2,1)S(1)} all-to-all(bf16[64,2,2304]{2,1,0:T(2,128)(2,1)} %shard_map.56), channel_id=1, replica_groups=mesh['energy'=64,'atoms'=4] {'energy'}, dimensions={0} | all-to-all | bytes 1179648 | tf_op jit(solution)/shard_map/all_to_all | solution.py:133
  79.7 1.2 %reshape.3 = bf16[64,16,288]{2,1,0:T(8,128)(2,1)S(1)} reshape(bf16[64,2,2304]{2,1,0:T(2,128)(2,1)S(1)} %all_to_all.11) | data formatting | bytes 1179648 | tf_op jit(solution)/shard_map/reshape | solution.py:134
  80.9 1.1 %copy.10 = bf16[64,16,288]{2,0,1:T(8,128)(2,1)} copy(bf16[64,16,288]{2,1,0:T(8,128)(2,1)S(1)} %reshape.3) | data formatting | bytes 1179648 | tf_op jit(solution)/shard_map/reshape | solution.py:134
Async XLA Ops:
  1.0 8.4 %collective-permute-start.1 = (bf16[16,8,288]{2,1,0:T(8,128)(2,1)S(1)}, bf16[16,8,288]{2,1,0:T(8,128)(2,1)S(1)}, u32[]{:S(2)}, u32[]{:S(2)}) collective-permute-start(bf16[16,8,288]{2,1,0:T(8,128)(2,1)S(1)} %get-tuple-element.9), channel_id=1, source_target_pairs={{1,0},{2,1},{3,2},{5,4},{6,5},{7,6},{9,8},{10,9},{11,10},{13,12},{... | collective-permute-start | bytes 221192 | tf_op jit(solution)/shard_map/ppermute | solution.py:128
  2.3 7.1 %collective-permute-start = (bf16[16,8,288]{2,1,0:T(8,128)(2,1)S(1)}, bf16[16,8,288]{2,1,0:T(8,128)(2,1)S(1)}, u32[]{:S(2)}, u32[]{:S(2)}) collective-permute-start(bf16[16,8,288]{2,1,0:T(8,128)(2,1)S(1)} %get-tuple-element.10), channel_id=1, source_target_pairs={{0,1},{1,2},{2,3},{4,5},{5,6},{6,7},{8,9},{9,10},{10,11},{12,13},{... | collective-permute-start | bytes 221192 | tf_op jit(solution)/shard_map/ppermute | solution.py:127
  9.3 0.6 copy-start
  9.3 0.7 copy-start.1

commit v13 on v12

--- a/solution.py
+++ b/solution.py
@@ -66,11 +66,12 @@
 
 def neighbour_kernel(neighbours_ref, low_ref, green_ref, high_ref, superop_ref, out_ref, rows_ref, picked_ref):
     width = low_ref.shape[1]
-    atoms, energies, comps = green_ref.shape
+    energies, atoms, comps = green_ref.shape
     slots = superop_ref.shape[0]
     first = lax.axis_index("atoms") * atoms - width
     empty = 2 * width + atoms
-    rows_ref[width:width + atoms] = green_ref[...]
+    for atom in range(atoms):
+        rows_ref[width + atom] = green_ref[:, atom, :]
     for atom in range(width):
         rows_ref[atom] = low_ref[:, atom, :]
         rows_ref[width + atoms + atom] = high_ref[:, atom, :]
@@ -94,9 +95,9 @@
     store_packed(out_ref, total.astype(out_ref.dtype).reshape(atoms, energies, comps))
 
 
-def neighbour_apply(neighbours, low, green_t, high, superop):
+def neighbour_apply(neighbours, low, green, high, superop):
     width = low.shape[1]
-    atoms, energies, comps = green_t.shape
+    energies, atoms, comps = green.shape
     slots = superop.shape[0]
     vmem = pl.BlockSpec(memory_space=pltpu.VMEM)
     return pl.pallas_call(
@@ -110,10 +111,10 @@
         ],
         cost_estimate=pl.CostEstimate(
             flops=2 * slots * atoms * energies * comps * comps,
-            bytes_accessed=2 * (2 * low.size + 2 * green_t.size + superop.size),
+            bytes_accessed=2 * (2 * low.size + 2 * green.size + superop.size),
             transcendentals=0,
         ),
-    )(neighbours, low, green_t, high, superop)
+    )(neighbours, low, green, high, superop)
 
 
 def per_device(green, superop, phonon, owner, neighbours):
@@ -121,12 +122,11 @@
     group_size = green.shape[1]
     comps = green.shape[2]
     groups = lax.axis_size("atoms")
-    green_t = jnp.transpose(green, (1, 0, 2))
     forward = [(i, i + 1) for i in range(groups - 1)]
     backward = [(i + 1, i) for i in range(groups - 1)]
     low = lax.ppermute(green[:, group_size - EDGE:], "atoms", forward)
     high = lax.ppermute(green[:, :EDGE], "atoms", backward)
-    outgoing = neighbour_apply(neighbours.T, low, green_t, high, superop)
+    outgoing = neighbour_apply(neighbours.T, low, green, high, superop)
     owner_t, outgoing = lax.optimization_barrier((owner.T, outgoing))
     columns = lax.all_to_all(outgoing, "energy", split_axis=0, concat_axis=0, tiled=True)
     product = toeplitz_apply(owner_t, phonon, columns, local_energies)

time: 82.4 us -> 83.4 us (1.012)
  local copies, waits for them, and re-layouts: 6.31 us -> 3.82 us
  waiting for transfers between devices: 0.01 us -> 1.61 us
  Pallas kernels: 12.6 us -> 13.6 us
    unnamed x5 -> x4, local copies, waits for them, and re-layouts: 3.13 us -> 0.64 us
    ppermute x1, waiting for transfers between devices: 0.01 us -> 1.55 us  [per_device(): low = lax.ppermute(green[:, group_size - EDGE:], 'atoms', forward)]
    pallas_call x1, Pallas kernels: 6.48 us -> 7.47 us  [neighbour_apply(): pl.pallas_call(neighbour_kernel, out_shape=jax.ShapeDtypeStruct((atoms, 2...]
  transfers between devices with their start and end apart: 2 -> 2, of which waited for: 0 -> 2; matrix products, arithmetic and copies ran while one was open for 3% -> 0% of each run, Pallas kernels for 0% -> 0%
where the time goes in v13:
time: 83.4 us; the launch traced here: 82.6 us
  blocking collectives  57.7 us (69%)
  Pallas kernels  13.6 us (16%)
  starting transfers between devices  5.87 us (7%)
  local copies, waits for them, and re-layouts  3.82 us (5%)
  waiting for transfers between devices  1.61 us (2%)
    all_to_all x1, blocking collectives, per_device(): lax.all_to_all(outgoing, 'energy', split_axis=0, concat_axis=0, tiled=True)  32.8 us
    all_to_all x1, blocking collectives, per_device(): lax.all_to_all(product, 'energy', split_axis=0, concat_axis=0, tiled=True)  24.8 us
    pallas_call x1, Pallas kernels, neighbour_apply(): pl.pallas_call(neighbour_kernel, out_shape=jax.ShapeDtypeStruct((atoms, 2...  7.47 us
    pallas_call x1, Pallas kernels, toeplitz_apply(): pl.pallas_call(toeplitz_kernel, out_shape=jax.ShapeDtypeStruct(packed.sha...  6.12 us
    ppermute x1, starting transfers between devices, per_device(): low = lax.ppermute(green[:, group_size - EDGE:], 'atoms', forward)  4.58 us
    reshape x2, local copies, waits for them, and re-layouts, per_device(): result = result.reshape(result.shape[0], local_energies, comps)  2.22 us
  transfers between devices with their start and end apart: 2, of which 2 were waited for; matrix products, arithmetic and copies ran while one was open for 0% of the time, Pallas kernels for 0%

profile of v13, /device:TPU:1, one launch (start us, length us, event | category | flops | bytes accessed | tf_op | source)
XLA Modules:
  0.0 82.6 jit_solution(6648592028671398668)
XLA Ops:
  0.0 1.0 %fusion = (bf16[16,8,288]{2,1,0:T(8,128)(2,1)S(1)}, bf16[16,8,288]{2,1,0:T(8,128)(2,1)S(1)}) fusion(bf16[16,64,288]{2,1,0:T(8,128)(2,1)} %green_ref.1), kind=kLoop, calls=%fused_computation.1 | loop fusion | bytes 294912 | tf_op jit(solution)/shard_map/slice | solution.py:128
  1.0 1.3 %collective-permute-start.1 = (bf16[16,8,288]{2,1,0:T(8,128)(2,1)S(1)}, bf16[16,8,288]{2,1,0:T(8,128)(2,1)S(1)}, u32[]{:S(2)}, u32[]{:S(2)}) collective-permute-start(bf16[16,8,288]{2,1,0:T(8,128)(2,1)S(1)} %get-tuple-element.9), channel_id=1, source_target_pairs={{1,0},{2,1},{3,2},{5,4},{6,5},{7,6},{9,8},{10,9},{11,10},{13,12},{... | collective-permute-start | bytes 221192 | tf_op jit(solution)/shard_map/ppermute | solution.py:128
  2.3 4.6 %collective-permute-start = (bf16[16,8,288]{2,1,0:T(8,128)(2,1)S(1)}, bf16[16,8,288]{2,1,0:T(8,128)(2,1)S(1)}, u32[]{:S(2)}, u32[]{:S(2)}) collective-permute-start(bf16[16,8,288]{2,1,0:T(8,128)(2,1)S(1)} %get-tuple-element.10), channel_id=1, source_target_pairs={{0,1},{1,2},{2,3},{4,5},{5,6},{6,7},{8,9},{9,10},{10,11},{12,13},{... | collective-permute-start | bytes 221192 | tf_op jit(solution)/shard_map/ppermute | solution.py:127
  6.9 0.1 collective-permute-done.1.high_ref
  6.9 0.0 copy-start
  6.9 1.6 %collective-permute-done.low_ref = bf16[16,8,288]{2,1,0:T(8,128)(2,1)S(1)} collective-permute-done((bf16[16,8,288]{2,1,0:T(8,128)(2,1)S(1)}, bf16[16,8,288]{2,1,0:T(8,128)(2,1)S(1)}, u32[]{:S(2)}, u32[]{:S(2)}) %collective-permute-start) | collective-permute-done | bytes 73760 | tf_op jit(solution)/shard_map/ppermute | solution.py:127
  8.5 0.0 copy-start.1
  8.5 0.0 copy-done
  8.5 0.6 copy-done.1
  9.1 7.5 %shard_map.55 = bf16[64,2,2304]{2,1,0:T(2,128)(2,1)} custom-call(s32[4,64]{1,0:T(4,128)} %bitcast.5, bf16[16,8,288]{2,1,0:T(8,128)(2,1)} %copy-done.1, bf16[16,64,288]{2,1,0:T(8,128)(2,1)} %green_ref.1, bf16[16,8,288]{2,1,0:T(8,128)(2,1)} %copy-done, bf16[4,288,288]{2,1,0:T(8,128)(2,1)} %superop_ref.1), custom_call_target="tpu_custom_call" | custom-call | flops 679477248 | bytes 1990656 | tf_op jit(solution)/shard_map/pallas_call | solution.py:103
  16.6 32.8 %all_to_all.10.packed_ref = bf16[64,2,2304]{2,1,0:T(2,128)(2,1)} all-to-all(bf16[64,2,2304]{2,1,0:T(2,128)(2,1)} %shard_map.55), channel_id=1, replica_groups=mesh['energy'=64,'atoms'=4] {'energy'}, dimensions={0} | all-to-all | bytes 1179648 | tf_op jit(solution)/shard_map/all_to_all | solution.py:131
  49.4 6.1 %shard_map.56 = bf16[64,2,2304]{2,1,0:T(2,128)(2,1)} custom-call(s32[1,64]{1,0:T(1,128)} %bitcast.6, bf16[64,2048]{1,0:T(8,128)(2,1)} %phonon_ref.1, bf16[64,2,2304]{2,1,0:T(2,128)(2,1)} %all_to_all.10.packed_ref), custom_call_target="tpu_custom_call" | custom-call | flops 603979776 | bytes 1441792 | tf_op jit(solution)/shard_map/pallas_call | solution.py:53
  55.5 24.8 %all_to_all.11 = bf16[64,2,2304]{2,1,0:T(2,128)(2,1)S(1)} all-to-all(bf16[64,2,2304]{2,1,0:T(2,128)(2,1)} %shard_map.56), channel_id=1, replica_groups=mesh['energy'=64,'atoms'=4] {'energy'}, dimensions={0} | all-to-all | bytes 1179648 | tf_op jit(solution)/shard_map/all_to_all | solution.py:133
  80.4 1.2 %reshape.3 = bf16[64,16,288]{2,1,0:T(8,128)(2,1)S(1)} reshape(bf16[64,2,2304]{2,1,0:T(2,128)(2,1)S(1)} %all_to_all.11) | data formatting | bytes 1179648 | tf_op jit(solution)/shard_map/reshape | solution.py:134
  81.5 1.1 %copy.8 = bf16[64,16,288]{2,0,1:T(8,128)(2,1)} copy(bf16[64,16,288]{2,1,0:T(8,128)(2,1)S(1)} %reshape.3) | data formatting | bytes 1179648 | tf_op jit(solution)/shard_map/reshape | solution.py:134
Async XLA Ops:
  1.0 5.9 %collective-permute-start.1 = (bf16[16,8,288]{2,1,0:T(8,128)(2,1)S(1)}, bf16[16,8,288]{2,1,0:T(8,128)(2,1)S(1)}, u32[]{:S(2)}, u32[]{:S(2)}) collective-permute-start(bf16[16,8,288]{2,1,0:T(8,128)(2,1)S(1)} %get-tuple-element.9), channel_id=1, source_target_pairs={{1,0},{2,1},{3,2},{5,4},{6,5},{7,6},{9,8},{10,9},{11,10},{13,12},{... | collective-permute-start | bytes 221192 | tf_op jit(solution)/shard_map/ppermute | solution.py:128
  2.3 6.2 %collective-permute-start = (bf16[16,8,288]{2,1,0:T(8,128)(2,1)S(1)}, bf16[16,8,288]{2,1,0:T(8,128)(2,1)S(1)}, u32[]{:S(2)}, u32[]{:S(2)}) collective-permute-start(bf16[16,8,288]{2,1,0:T(8,128)(2,1)S(1)} %get-tuple-element.10), channel_id=1, source_target_pairs={{0,1},{1,2},{2,3},{4,5},{5,6},{6,7},{8,9},{9,10},{10,11},{12,13},{... | collective-permute-start | bytes 221192 | tf_op jit(solution)/shard_map/ppermute | solution.py:127
  6.9 1.6 %copy-start = (bf16[16,8,288]{2,1,0:T(8,128)(2,1)}, bf16[16,8,288]{2,1,0:T(8,128)(2,1)S(1)}, u32[]{:S(2)}) copy-start(bf16[16,8,288]{2,1,0:T(8,128)(2,1)S(1)} %collective-permute-done.1.high_ref) | copy-start | bytes 221188
  8.5 0.6 copy-start.1

commit v14 on v12

--- a/solution.py
+++ b/solution.py
@@ -35,9 +35,9 @@
     block = phonon_ref[pl.ds(base, 16), :].astype(jnp.float32)
     rows = lax.broadcasted_iota(jnp.int32, block.shape, 0)
     row = jnp.sum(jnp.where(rows == domain - base, block, 0.0), axis=0, keepdims=True)
-    wide = jnp.broadcast_to(row, (count, 2 * count))
+    wide = jnp.broadcast_to(row.astype(jnp.bfloat16), (count, 2 * count))
     rolled = pltpu.roll(wide, shift=count, axis=1, stride=1, stride_axis=0)
-    kernel_t = rolled[:, :count].astype(jnp.bfloat16)
+    kernel_t = rolled[:, :count]
     product = lax.dot_general(
         kernel_t, blocks_ref[...].reshape(count, comps), (((0,), (0,)), ((), ())),
         preferred_element_type=jnp.float32,
@@ -83,7 +83,7 @@
             picked_ref[slot, atom] = rows_ref[row]
         return carry
 
-    lax.fori_loop(0, atoms, pick, 0, unroll=8)
+    lax.fori_loop(0, atoms, pick, 0, unroll=True)
     total = jnp.zeros((atoms * energies, comps), jnp.float32)
     for slot in range(slots):
         total = total + jnp.dot(

time: 82.4 us -> 81.8 us (level)
  no operation moved by 1% of the time
where the time goes in v14:
time: 81.8 us; the launch traced here: 81.3 us
  blocking collectives  57.1 us (70%)
  Pallas kernels  12 us (15%)
  local copies, waits for them, and re-layouts  6.31 us (8%)
  starting transfers between devices  5.87 us (7%)
    all_to_all x1, blocking collectives, per_device(): lax.all_to_all(outgoing, 'energy', split_axis=0, concat_axis=0, tiled=True)  32.3 us
    all_to_all x1, blocking collectives, per_device(): lax.all_to_all(product, 'energy', split_axis=0, concat_axis=0, tiled=True)  24.8 us
    pallas_call x1, Pallas kernels, toeplitz_apply(): pl.pallas_call(toeplitz_kernel, out_shape=jax.ShapeDtypeStruct(packed.sha...  6.16 us
    pallas_call x1, Pallas kernels, neighbour_apply(): pl.pallas_call(neighbour_kernel, out_shape=jax.ShapeDtypeStruct((atoms, 2...  5.8 us
    ppermute x1, starting transfers between devices, per_device(): low = lax.ppermute(green[:, group_size - EDGE:], 'atoms', forward)  4.58 us
    unnamed x5, local copies, waits for them, and re-layouts  3.13 us
    reshape x2, local copies, waits for them, and re-layouts, per_device(): result = result.reshape(result.shape[0], local_energies, comps)  2.22 us
  transfers between devices with their start and end apart: 2, of which 0 were waited for; matrix products, arithmetic and copies ran while one was open for 3% of the time, Pallas kernels for 0%

profile of v14, /device:TPU:1, one launch (start us, length us, event | category | flops | bytes accessed | tf_op | source)
XLA Modules:
  0.0 81.3 jit_solution(17062560009308136845)
XLA Ops:
  0.0 1.0 %fusion = (bf16[16,8,288]{2,1,0:T(8,128)(2,1)S(1)}, bf16[16,8,288]{2,1,0:T(8,128)(2,1)S(1)}) fusion(bf16[16,64,288]{2,1,0:T(8,128)(2,1)} %param.5), kind=kLoop, calls=%fused_computation.2 | loop fusion | bytes 294912 | tf_op jit(solution)/shard_map/slice | solution.py:128
  1.0 1.3 %collective-permute-start.1 = (bf16[16,8,288]{2,1,0:T(8,128)(2,1)S(1)}, bf16[16,8,288]{2,1,0:T(8,128)(2,1)S(1)}, u32[]{:S(2)}, u32[]{:S(2)}) collective-permute-start(bf16[16,8,288]{2,1,0:T(8,128)(2,1)S(1)} %get-tuple-element.9), channel_id=1, source_target_pairs={{1,0},{2,1},{3,2},{5,4},{6,5},{7,6},{9,8},{10,9},{11,10},{13,12},{... | collective-permute-start | bytes 221192 | tf_op jit(solution)/shard_map/ppermute | solution.py:128
  2.3 4.6 %collective-permute-start = (bf16[16,8,288]{2,1,0:T(8,128)(2,1)S(1)}, bf16[16,8,288]{2,1,0:T(8,128)(2,1)S(1)}, u32[]{:S(2)}, u32[]{:S(2)}) collective-permute-start(bf16[16,8,288]{2,1,0:T(8,128)(2,1)S(1)} %get-tuple-element.10), channel_id=1, source_target_pairs={{0,1},{1,2},{2,3},{4,5},{5,6},{6,7},{8,9},{9,10},{10,11},{12,13},{... | collective-permute-start | bytes 221192 | tf_op jit(solution)/shard_map/ppermute | solution.py:127
  6.9 2.5 %copy.11 = bf16[16,64,288]{2,0,1:T(8,128)(2,1)} copy(bf16[16,64,288]{2,1,0:T(8,128)(2,1)} %param.5) | data formatting | bytes 1179648 | tf_op args[0]
  9.3 0.0 collective-permute-done.1.high_ref
  9.3 0.0 copy-start
  9.3 0.0 collective-permute-done.low_ref
  9.3 0.0 copy-start.1
  9.3 0.6 copy-done
  10.0 0.0 copy-done.1
  10.0 5.8 %shard_map.55 = bf16[64,2,2304]{2,1,0:T(2,128)(2,1)} custom-call(s32[4,64]{1,0:T(4,128)} %bitcast.9, bf16[16,8,288]{2,1,0:T(8,128)(2,1)} %copy-done.1, bf16[64,16,288]{2,1,0:T(8,128)(2,1)} %bitcast.8, bf16[16,8,288]{2,1,0:T(8,128)(2,1)} %copy-done, bf16[4,288,288]{2,1,0:T(8,128)(2,1)} %superop_ref.1), custom_call_target="tpu_custom_call" | custom-call | flops 679477248 | bytes 1990656 | tf_op jit(solution)/shard_map/pallas_call | solution.py:102
  15.8 32.3 %all_to_all.10.packed_ref = bf16[64,2,2304]{2,1,0:T(2,128)(2,1)} all-to-all(bf16[64,2,2304]{2,1,0:T(2,128)(2,1)} %shard_map.55), channel_id=1, replica_groups=mesh['energy'=64,'atoms'=4] {'energy'}, dimensions={0} | all-to-all | bytes 1179648 | tf_op jit(solution)/shard_map/all_to_all | solution.py:131
  48.1 6.2 %shard_map.56 = bf16[64,2,2304]{2,1,0:T(2,128)(2,1)} custom-call(s32[1,64]{1,0:T(1,128)} %bitcast.10, bf16[64,2048]{1,0:T(8,128)(2,1)} %phonon_ref.1, bf16[64,2,2304]{2,1,0:T(2,128)(2,1)} %all_to_all.10.packed_ref), custom_call_target="tpu_custom_call" | custom-call | flops 603979776 | bytes 1441792 | tf_op jit(solution)/shard_map/pallas_call | solution.py:53
  54.2 24.8 %all_to_all.11 = bf16[64,2,2304]{2,1,0:T(2,128)(2,1)S(1)} all-to-all(bf16[64,2,2304]{2,1,0:T(2,128)(2,1)} %shard_map.56), channel_id=1, replica_groups=mesh['energy'=64,'atoms'=4] {'energy'}, dimensions={0} | all-to-all | bytes 1179648 | tf_op jit(solution)/shard_map/all_to_all | solution.py:133
  79.1 1.2 %reshape.3 = bf16[64,16,288]{2,1,0:T(8,128)(2,1)S(1)} reshape(bf16[64,2,2304]{2,1,0:T(2,128)(2,1)S(1)} %all_to_all.11) | data formatting | bytes 1179648 | tf_op jit(solution)/shard_map/reshape | solution.py:134
  80.2 1.1 %copy.10 = bf16[64,16,288]{2,0,1:T(8,128)(2,1)} copy(bf16[64,16,288]{2,1,0:T(8,128)(2,1)S(1)} %reshape.3) | data formatting | bytes 1179648 | tf_op jit(solution)/shard_map/reshape | solution.py:134
Async XLA Ops:
  1.0 8.4 %collective-permute-start.1 = (bf16[16,8,288]{2,1,0:T(8,128)(2,1)S(1)}, bf16[16,8,288]{2,1,0:T(8,128)(2,1)S(1)}, u32[]{:S(2)}, u32[]{:S(2)}) collective-permute-start(bf16[16,8,288]{2,1,0:T(8,128)(2,1)S(1)} %get-tuple-element.9), channel_id=1, source_target_pairs={{1,0},{2,1},{3,2},{5,4},{6,5},{7,6},{9,8},{10,9},{11,10},{13,12},{... | collective-permute-start | bytes 221192 | tf_op jit(solution)/shard_map/ppermute | solution.py:128
  2.3 7.1 %collective-permute-start = (bf16[16,8,288]{2,1,0:T(8,128)(2,1)S(1)}, bf16[16,8,288]{2,1,0:T(8,128)(2,1)S(1)}, u32[]{:S(2)}, u32[]{:S(2)}) collective-permute-start(bf16[16,8,288]{2,1,0:T(8,128)(2,1)S(1)} %get-tuple-element.10), channel_id=1, source_target_pairs={{0,1},{1,2},{2,3},{4,5},{5,6},{6,7},{8,9},{9,10},{10,11},{12,13},{... | collective-permute-start | bytes 221192 | tf_op jit(solution)/shard_map/ppermute | solution.py:127
  9.3 0.6 copy-start
  9.3 0.7 copy-start.1

commit v15 on v14

--- a/solution.py
+++ b/solution.py
@@ -26,10 +26,8 @@
             blocks_ref[:, h * half + e, :] = packed_ref[:, h, e * comps:(e + 1) * comps]
 
 
-def toeplitz_kernel(owner_ref, phonon_ref, packed_ref, out_ref, blocks_ref):
-    peers, energies, comps = blocks_ref.shape
-    count = peers * energies
-    load_packed(packed_ref, blocks_ref)
+def toeplitz_build_kernel(owner_ref, phonon_ref, out_ref):
+    count = out_ref.shape[0]
     domain = owner_ref[0, lax.axis_index("energy")]
     base = pl.multiple_of((domain // 16) * 16, 16)
     block = phonon_ref[pl.ds(base, 16), :].astype(jnp.float32)
@@ -37,15 +35,33 @@
     row = jnp.sum(jnp.where(rows == domain - base, block, 0.0), axis=0, keepdims=True)
     wide = jnp.broadcast_to(row.astype(jnp.bfloat16), (count, 2 * count))
     rolled = pltpu.roll(wide, shift=count, axis=1, stride=1, stride_axis=0)
-    kernel_t = rolled[:, :count]
+    out_ref[...] = rolled[:, :count]
+
+
+def toeplitz_build(owner, phonon, count):
+    return pl.pallas_call(
+        toeplitz_build_kernel,
+        out_shape=jax.ShapeDtypeStruct((count, count), jnp.bfloat16),
+        in_specs=[pl.BlockSpec(memory_space=pltpu.SMEM), pl.BlockSpec(memory_space=pltpu.VMEM)],
+        out_specs=pl.BlockSpec(memory_space=pltpu.VMEM),
+        cost_estimate=pl.CostEstimate(
+            flops=0, bytes_accessed=2 * (phonon.size + count * count), transcendentals=0
+        ),
+    )(owner, phonon)
+
+
+def toeplitz_kernel(kernel_ref, packed_ref, out_ref, blocks_ref):
+    peers, energies, comps = blocks_ref.shape
+    count = peers * energies
+    load_packed(packed_ref, blocks_ref)
     product = lax.dot_general(
-        kernel_t, blocks_ref[...].reshape(count, comps), (((0,), (0,)), ((), ())),
+        kernel_ref[...], blocks_ref[...].reshape(count, comps), (((0,), (0,)), ((), ())),
         preferred_element_type=jnp.float32,
     )
     store_packed(out_ref, product.astype(out_ref.dtype).reshape(peers, energies, comps))
 
 
-def toeplitz_apply(owner, phonon, packed, energies):
+def toeplitz_apply(kernel_t, packed, energies):
     peers = packed.shape[0]
     comps = packed.shape[2] * 2 // energies
     count = peers * energies
@@ -53,15 +69,15 @@
     return pl.pallas_call(
         toeplitz_kernel,
         out_shape=jax.ShapeDtypeStruct(packed.shape, jnp.bfloat16),
-        in_specs=[pl.BlockSpec(memory_space=pltpu.SMEM), vmem, vmem],
+        in_specs=[vmem, vmem],
         out_specs=vmem,
         scratch_shapes=[pltpu.VMEM((peers, energies, comps), jnp.bfloat16)],
         cost_estimate=pl.CostEstimate(
             flops=2 * count * count * comps,
-            bytes_accessed=2 * (phonon.size + 2 * count * comps),
+            bytes_accessed=2 * (count * count + 2 * count * comps),
             transcendentals=0,
         ),
-    )(owner, phonon, packed)
+    )(kernel_t, packed)
 
 
 def neighbour_kernel(neighbours_ref, low_ref, green_ref, high_ref, superop_ref, out_ref, rows_ref, picked_ref):
@@ -127,9 +143,10 @@
     low = lax.ppermute(green[:, group_size - EDGE:], "atoms", forward)
     high = lax.ppermute(green[:, :EDGE], "atoms", backward)
     outgoing = neighbour_apply(neighbours.T, low, green_t, high, superop)
-    owner_t, outgoing = lax.optimization_barrier((owner.T, outgoing))
+    count = local_energies * lax.axis_size("energy")
+    kernel_t = toeplitz_build(owner.T, phonon, count)
     columns = lax.all_to_all(outgoing, "energy", split_axis=0, concat_axis=0, tiled=True)
-    product = toeplitz_apply(owner_t, phonon, columns, local_energies)
+    product = toeplitz_apply(kernel_t, columns, local_energies)
     result = lax.all_to_all(product, "energy", split_axis=0, concat_axis=0, tiled=True)
     result = result.reshape(result.shape[0], local_energies, comps)
     return jnp.transpose(result, (1, 0, 2))

time: 81.8 us -> 82.8 us (1.012)
  blocking collectives: 57.1 us -> 24.8 us
  waiting for transfers between devices: 0.01 us -> 16.5 us
  starting transfers between devices: 5.87 us -> 19 us
  Pallas kernels: 12 us -> 14.8 us
    all_to_all x1 -> x0, blocking collectives: 32.3 us -> none  [per_device(): lax.all_to_all(outgoing, 'energy', split_axis=0, concat_axis=0, tiled=True)]
    all_to_all x0 -> x1, waiting for transfers between devices: none -> 16.5 us  [per_device(): lax.all_to_all(outgoing, 'energy', split_axis=0, concat_axis=0, tiled=True)]
    all_to_all x0 -> x1, starting transfers between devices: none -> 13.1 us  [per_device(): lax.all_to_all(outgoing, 'energy', split_axis=0, concat_axis=0, tiled=True)]
    pallas_call x0 -> x1, Pallas kernels: none -> 2.57 us  [toeplitz_build(): pl.pallas_call(toeplitz_build_kernel, out_shape=jax.ShapeDtypeStruct((cou...]
    unnamed x5 -> x7, local copies, waits for them, and re-layouts: 3.13 us -> 3.95 us
  transfers between devices with their start and end apart: 2 -> 3, of which waited for: 0 -> 1; matrix products, arithmetic and copies ran while one was open for 3% -> 3% of each run, Pallas kernels for 0% -> 3%
where the time goes in v15:
time: 82.8 us; the launch traced here: 82.3 us
  blocking collectives  24.8 us (30%)
  starting transfers between devices  19 us (23%)
  waiting for transfers between devices  16.5 us (20%)
  Pallas kernels  14.8 us (18%)
  local copies, waits for them, and re-layouts  7.13 us (9%)
    all_to_all x1, blocking collectives, per_device(): lax.all_to_all(product, 'energy', split_axis=0, concat_axis=0, tiled=True)  24.8 us
    all_to_all x1, waiting for transfers between devices, per_device(): lax.all_to_all(outgoing, 'energy', split_axis=0, concat_axis=0, tiled=True)  16.5 us
    all_to_all x1, starting transfers between devices, per_device(): lax.all_to_all(outgoing, 'energy', split_axis=0, concat_axis=0, tiled=True)  13.1 us
    pallas_call x1, Pallas kernels, toeplitz_apply(): pl.pallas_call(toeplitz_kernel, out_shape=jax.ShapeDtypeStruct(packed.sha...  6.46 us
    pallas_call x1, Pallas kernels, neighbour_apply(): pl.pallas_call(neighbour_kernel, out_shape=jax.ShapeDtypeStruct((atoms, 2...  5.8 us
    ppermute x1, starting transfers between devices, per_device(): low = lax.ppermute(green[:, group_size - EDGE:], 'atoms', forward)  4.58 us
    unnamed x7, local copies, waits for them, and re-layouts  3.95 us
    pallas_call x1, Pallas kernels, toeplitz_build(): pl.pallas_call(toeplitz_build_kernel, out_shape=jax.ShapeDtypeStruct((cou...  2.57 us
  transfers between devices with their start and end apart: 3, of which 1 were waited for; matrix products, arithmetic and copies ran while one was open for 3% of the time, Pallas kernels for 3%

profile of v15, /device:TPU:1, one launch (start us, length us, event | category | flops | bytes accessed | tf_op | source)
XLA Modules:
  0.0 82.3 jit_solution(8657218330153781253)
XLA Ops:
  0.0 1.0 %fusion = (bf16[16,8,288]{2,1,0:T(8,128)(2,1)S(1)}, bf16[16,8,288]{2,1,0:T(8,128)(2,1)S(1)}) fusion(bf16[16,64,288]{2,1,0:T(8,128)(2,1)} %param.5), kind=kLoop, calls=%fused_computation.2 | loop fusion | bytes 294912 | tf_op jit(solution)/shard_map/slice | solution.py:144
  1.0 1.3 %collective-permute-start.1 = (bf16[16,8,288]{2,1,0:T(8,128)(2,1)S(1)}, bf16[16,8,288]{2,1,0:T(8,128)(2,1)S(1)}, u32[]{:S(2)}, u32[]{:S(2)}) collective-permute-start(bf16[16,8,288]{2,1,0:T(8,128)(2,1)S(1)} %get-tuple-element.5), channel_id=1, source_target_pairs={{1,0},{2,1},{3,2},{5,4},{6,5},{7,6},{9,8},{10,9},{11,10},{13,12},{... | collective-permute-start | bytes 221192 | tf_op jit(solution)/shard_map/ppermute | solution.py:144
  2.3 4.6 %collective-permute-start = (bf16[16,8,288]{2,1,0:T(8,128)(2,1)S(1)}, bf16[16,8,288]{2,1,0:T(8,128)(2,1)S(1)}, u32[]{:S(2)}, u32[]{:S(2)}) collective-permute-start(bf16[16,8,288]{2,1,0:T(8,128)(2,1)S(1)} %get-tuple-element.6), channel_id=1, source_target_pairs={{0,1},{1,2},{2,3},{4,5},{5,6},{6,7},{8,9},{9,10},{10,11},{12,13},{... | collective-permute-start | bytes 221192 | tf_op jit(solution)/shard_map/ppermute | solution.py:143
  6.9 2.5 %copy.11 = bf16[16,64,288]{2,0,1:T(8,128)(2,1)} copy(bf16[16,64,288]{2,1,0:T(8,128)(2,1)} %param.5) | data formatting | bytes 1179648 | tf_op args[0]
  9.3 0.0 collective-permute-done.1.high_ref
  9.3 0.0 copy-start.1
  9.3 0.0 collective-permute-done.low_ref
  9.3 0.0 copy-start.2
  9.3 0.6 copy-done.1
  10.0 0.1 copy-done.2
  10.0 5.8 %shard_map.56 = bf16[64,2,2304]{2,1,0:T(2,128)(2,1)} custom-call(s32[4,64]{1,0:T(4,128)} %bitcast.10, bf16[16,8,288]{2,1,0:T(8,128)(2,1)} %copy-done.2, bf16[64,16,288]{2,1,0:T(8,128)(2,1)} %bitcast.8, bf16[16,8,288]{2,1,0:T(8,128)(2,1)} %copy-done.1, bf16[4,288,288]{2,1,0:T(8,128)(2,1)} %superop_ref.1), custom_call_target="tpu_custom_call" | custom-call | flops 679477248 | bytes 1990656 | tf_op jit(solution)/shard_map/pallas_call | solution.py:118
  15.8 13.1 %all-to-all-start = ((bf16[64,2,2304]{2,1,0:T(2,128)(2,1)}), bf16[64,2,2304]{2,1,0:T(2,128)(2,1)S(1)}, u32[]{:S(2)}, u32[]{:S(2)}) async-start(bf16[64,2,2304]{2,1,0:T(2,128)(2,1)} %shard_map.56), calls=%async_computation | async-start | bytes 1179648 | tf_op jit(solution)/shard_map/all_to_all | solution.py:148
  29.0 2.6 %shard_map.55.kernel_ref = bf16[1024,1024]{1,0:T(8,128)(2,1)} custom-call(s32[1,64]{1,0:T(1,128)} %bitcast.9, bf16[64,2048]{1,0:T(8,128)(2,1)} %phonon_ref.1), custom_call_target="tpu_custom_call" | custom-call | bytes 2359296 | tf_op jit(solution)/shard_map/pallas_call | solution.py:42
  31.5 16.5 %all-to-all-done.packed_ref = bf16[64,2,2304]{2,1,0:T(2,128)(2,1)S(1)} async-done(((bf16[64,2,2304]{2,1,0:T(2,128)(2,1)}), bf16[64,2,2304]{2,1,0:T(2,128)(2,1)S(1)}, u32[]{:S(2)}, u32[]{:S(2)}) %all-to-all-start) | async-done | bytes 589856 | tf_op jit(solution)/shard_map/all_to_all | solution.py:148
  48.0 0.0 copy-start
  48.0 0.8 copy-done
  48.8 6.5 %shard_map.57 = bf16[64,2,2304]{2,1,0:T(2,128)(2,1)} custom-call(bf16[1024,1024]{1,0:T(8,128)(2,1)} %shard_map.55.kernel_ref, bf16[64,2,2304]{2,1,0:T(2,128)(2,1)} %copy-done), custom_call_target="tpu_custom_call" | custom-call | flops 603979776 | bytes 3276800 | tf_op jit(solution)/shard_map/pallas_call | solution.py:69
  55.3 24.8 %all_to_all.10 = bf16[64,2,2304]{2,1,0:T(2,128)(2,1)S(1)} all-to-all(bf16[64,2,2304]{2,1,0:T(2,128)(2,1)} %shard_map.57), channel_id=1, replica_groups=mesh['energy'=64,'atoms'=4] {'energy'}, dimensions={0} | all-to-all | bytes 1179648 | tf_op jit(solution)/shard_map/all_to_all | solution.py:150
  80.1 1.2 %reshape.3 = bf16[64,16,288]{2,1,0:T(8,128)(2,1)S(1)} reshape(bf16[64,2,2304]{2,1,0:T(2,128)(2,1)S(1)} %all_to_all.10) | data formatting | bytes 1179648 | tf_op jit(solution)/shard_map/reshape | solution.py:151
  81.3 1.1 %copy.10 = bf16[64,16,288]{2,0,1:T(8,128)(2,1)} copy(bf16[64,16,288]{2,1,0:T(8,128)(2,1)S(1)} %reshape.3) | data formatting | bytes 1179648 | tf_op jit(solution)/shard_map/reshape | solution.py:151
Async XLA Ops:
  1.0 8.4 %collective-permute-start.1 = (bf16[16,8,288]{2,1,0:T(8,128)(2,1)S(1)}, bf16[16,8,288]{2,1,0:T(8,128)(2,1)S(1)}, u32[]{:S(2)}, u32[]{:S(2)}) collective-permute-start(bf16[16,8,288]{2,1,0:T(8,128)(2,1)S(1)} %get-tuple-element.5), channel_id=1, source_target_pairs={{1,0},{2,1},{3,2},{5,4},{6,5},{7,6},{9,8},{10,9},{11,10},{13,12},{... | collective-permute-start | bytes 221192 | tf_op jit(solution)/shard_map/ppermute | solution.py:144
  2.3 7.1 %collective-permute-start = (bf16[16,8,288]{2,1,0:T(8,128)(2,1)S(1)}, bf16[16,8,288]{2,1,0:T(8,128)(2,1)S(1)}, u32[]{:S(2)}, u32[]{:S(2)}) collective-permute-start(bf16[16,8,288]{2,1,0:T(8,128)(2,1)S(1)} %get-tuple-element.6), channel_id=1, source_target_pairs={{0,1},{1,2},{2,3},{4,5},{5,6},{6,7},{8,9},{9,10},{10,11},{12,13},{... | collective-permute-start | bytes 221192 | tf_op jit(solution)/shard_map/ppermute | solution.py:143
  9.3 0.6 copy-start.1
  9.3 0.7 copy-start.2
  15.8 32.2 %all-to-all-start = ((bf16[64,2,2304]{2,1,0:T(2,128)(2,1)}), bf16[64,2,2304]{2,1,0:T(2,128)(2,1)S(1)}, u32[]{:S(2)}, u32[]{:S(2)}) async-start(bf16[64,2,2304]{2,1,0:T(2,128)(2,1)} %shard_map.56), calls=%async_computation | async-start | bytes 1179648 | tf_op jit(solution)/shard_map/all_to_all | solution.py:148
  48.0 0.8 copy-start

commit v16 on v15

--- a/solution.py
+++ b/solution.py
@@ -33,9 +33,9 @@
     block = phonon_ref[pl.ds(base, 16), :].astype(jnp.float32)
     rows = lax.broadcasted_iota(jnp.int32, block.shape, 0)
     row = jnp.sum(jnp.where(rows == domain - base, block, 0.0), axis=0, keepdims=True)
-    wide = jnp.broadcast_to(row.astype(jnp.bfloat16), (count, 2 * count))
+    wide = jnp.broadcast_to(row, (count, 2 * count))
     rolled = pltpu.roll(wide, shift=count, axis=1, stride=1, stride_axis=0)
-    out_ref[...] = rolled[:, :count]
+    out_ref[...] = jnp.transpose(rolled[:, :count]).astype(out_ref.dtype)
 
 
 def toeplitz_build(owner, phonon, count):
@@ -54,9 +54,8 @@
     peers, energies, comps = blocks_ref.shape
     count = peers * energies
     load_packed(packed_ref, blocks_ref)
-    product = lax.dot_general(
-        kernel_ref[...], blocks_ref[...].reshape(count, comps), (((0,), (0,)), ((), ())),
-        preferred_element_type=jnp.float32,
+    product = jnp.dot(
+        kernel_ref[...], blocks_ref[...].reshape(count, comps), preferred_element_type=jnp.float32
     )
     store_packed(out_ref, product.astype(out_ref.dtype).reshape(peers, energies, comps))
 

time: 82.8 us -> 82.4 us (level)
  no operation moved by 1% of the time
where the time goes in v16:
time: 82.4 us; the launch traced here: 81.9 us
  blocking collectives  24.8 us (30%)
  starting transfers between devices  19 us (23%)
  waiting for transfers between devices  16.3 us (20%)
  Pallas kernels  14.6 us (18%)
  local copies, waits for them, and re-layouts  7.13 us (9%)
    all_to_all x1, blocking collectives, per_device(): lax.all_to_all(product, 'energy', split_axis=0, concat_axis=0, tiled=True)  24.8 us
    all_to_all x1, waiting for transfers between devices, per_device(): lax.all_to_all(outgoing, 'energy', split_axis=0, concat_axis=0, tiled=True)  16.3 us
    all_to_all x1, starting transfers between devices, per_device(): lax.all_to_all(outgoing, 'energy', split_axis=0, concat_axis=0, tiled=True)  13.1 us
    pallas_call x1, Pallas kernels, toeplitz_apply(): pl.pallas_call(toeplitz_kernel, out_shape=jax.ShapeDtypeStruct(packed.sha...  6.08 us
    pallas_call x1, Pallas kernels, neighbour_apply(): pl.pallas_call(neighbour_kernel, out_shape=jax.ShapeDtypeStruct((atoms, 2...  5.8 us
    ppermute x1, starting transfers between devices, per_device(): low = lax.ppermute(green[:, group_size - EDGE:], 'atoms', forward)  4.58 us
    unnamed x7, local copies, waits for them, and re-layouts  3.95 us
    pallas_call x1, Pallas kernels, toeplitz_build(): pl.pallas_call(toeplitz_build_kernel, out_shape=jax.ShapeDtypeStruct((cou...  2.73 us
  transfers between devices with their start and end apart: 3, of which 1 were waited for; matrix products, arithmetic and copies ran while one was open for 3% of the time, Pallas kernels for 3%

profile of v16, /device:TPU:1, one launch (start us, length us, event | category | flops | bytes accessed | tf_op | source)
XLA Modules:
  0.0 81.9 jit_solution(10672429205642726686)
XLA Ops:
  0.0 1.0 %fusion = (bf16[16,8,288]{2,1,0:T(8,128)(2,1)S(1)}, bf16[16,8,288]{2,1,0:T(8,128)(2,1)S(1)}) fusion(bf16[16,64,288]{2,1,0:T(8,128)(2,1)} %param.5), kind=kLoop, calls=%fused_computation.2 | loop fusion | bytes 294912 | tf_op jit(solution)/shard_map/slice | solution.py:143
  1.0 1.3 %collective-permute-start.1 = (bf16[16,8,288]{2,1,0:T(8,128)(2,1)S(1)}, bf16[16,8,288]{2,1,0:T(8,128)(2,1)S(1)}, u32[]{:S(2)}, u32[]{:S(2)}) collective-permute-start(bf16[16,8,288]{2,1,0:T(8,128)(2,1)S(1)} %get-tuple-element.5), channel_id=1, source_target_pairs={{1,0},{2,1},{3,2},{5,4},{6,5},{7,6},{9,8},{10,9},{11,10},{13,12},{... | collective-permute-start | bytes 221192 | tf_op jit(solution)/shard_map/ppermute | solution.py:143
  2.3 4.6 %collective-permute-start = (bf16[16,8,288]{2,1,0:T(8,128)(2,1)S(1)}, bf16[16,8,288]{2,1,0:T(8,128)(2,1)S(1)}, u32[]{:S(2)}, u32[]{:S(2)}) collective-permute-start(bf16[16,8,288]{2,1,0:T(8,128)(2,1)S(1)} %get-tuple-element.6), channel_id=1, source_target_pairs={{0,1},{1,2},{2,3},{4,5},{5,6},{6,7},{8,9},{9,10},{10,11},{12,13},{... | collective-permute-start | bytes 221192 | tf_op jit(solution)/shard_map/ppermute | solution.py:142
  6.9 2.5 %copy.11 = bf16[16,64,288]{2,0,1:T(8,128)(2,1)} copy(bf16[16,64,288]{2,1,0:T(8,128)(2,1)} %param.5) | data formatting | bytes 1179648 | tf_op args[0]
  9.3 0.0 collective-permute-done.1.high_ref
  9.3 0.0 copy-start.1
  9.3 0.0 collective-permute-done.low_ref
  9.3 0.0 copy-start.2
  9.3 0.6 copy-done.1
  10.0 0.1 copy-done.2
  10.0 5.8 %shard_map.56 = bf16[64,2,2304]{2,1,0:T(2,128)(2,1)} custom-call(s32[4,64]{1,0:T(4,128)} %bitcast.10, bf16[16,8,288]{2,1,0:T(8,128)(2,1)} %copy-done.2, bf16[64,16,288]{2,1,0:T(8,128)(2,1)} %bitcast.8, bf16[16,8,288]{2,1,0:T(8,128)(2,1)} %copy-done.1, bf16[4,288,288]{2,1,0:T(8,128)(2,1)} %superop_ref.1), custom_call_target="tpu_custom_call" | custom-call | flops 679477248 | bytes 1990656 | tf_op jit(solution)/shard_map/pallas_call | solution.py:117
  15.8 13.1 %all-to-all-start = ((bf16[64,2,2304]{2,1,0:T(2,128)(2,1)}), bf16[64,2,2304]{2,1,0:T(2,128)(2,1)S(1)}, u32[]{:S(2)}, u32[]{:S(2)}) async-start(bf16[64,2,2304]{2,1,0:T(2,128)(2,1)} %shard_map.56), calls=%async_computation | async-start | bytes 1179648 | tf_op jit(solution)/shard_map/all_to_all | solution.py:147
  28.9 2.7 %shard_map.55.kernel_ref = bf16[1024,1024]{1,0:T(8,128)(2,1)} custom-call(s32[1,64]{1,0:T(1,128)} %bitcast.9, bf16[64,2048]{1,0:T(8,128)(2,1)} %phonon_ref.1), custom_call_target="tpu_custom_call" | custom-call | bytes 2359296 | tf_op jit(solution)/shard_map/pallas_call | solution.py:42
  31.7 16.3 %all-to-all-done.packed_ref = bf16[64,2,2304]{2,1,0:T(2,128)(2,1)S(1)} async-done(((bf16[64,2,2304]{2,1,0:T(2,128)(2,1)}), bf16[64,2,2304]{2,1,0:T(2,128)(2,1)S(1)}, u32[]{:S(2)}, u32[]{:S(2)}) %all-to-all-start) | async-done | bytes 589856 | tf_op jit(solution)/shard_map/all_to_all | solution.py:147
  48.0 0.0 copy-start
  48.0 0.8 copy-done
  48.8 6.1 %shard_map.57 = bf16[64,2,2304]{2,1,0:T(2,128)(2,1)} custom-call(bf16[1024,1024]{1,0:T(8,128)(2,1)} %shard_map.55.kernel_ref, bf16[64,2,2304]{2,1,0:T(2,128)(2,1)} %copy-done), custom_call_target="tpu_custom_call" | custom-call | flops 603979776 | bytes 3276800 | tf_op jit(solution)/shard_map/pallas_call | solution.py:68
  54.9 24.8 %all_to_all.10 = bf16[64,2,2304]{2,1,0:T(2,128)(2,1)S(1)} all-to-all(bf16[64,2,2304]{2,1,0:T(2,128)(2,1)} %shard_map.57), channel_id=1, replica_groups=mesh['energy'=64,'atoms'=4] {'energy'}, dimensions={0} | all-to-all | bytes 1179648 | tf_op jit(solution)/shard_map/all_to_all | solution.py:149
  79.7 1.2 %reshape.3 = bf16[64,16,288]{2,1,0:T(8,128)(2,1)S(1)} reshape(bf16[64,2,2304]{2,1,0:T(2,128)(2,1)S(1)} %all_to_all.10) | data formatting | bytes 1179648 | tf_op jit(solution)/shard_map/reshape | solution.py:150
  80.9 1.1 %copy.10 = bf16[64,16,288]{2,0,1:T(8,128)(2,1)} copy(bf16[64,16,288]{2,1,0:T(8,128)(2,1)S(1)} %reshape.3) | data formatting | bytes 1179648 | tf_op jit(solution)/shard_map/reshape | solution.py:150
Async XLA Ops:
  1.0 8.4 %collective-permute-start.1 = (bf16[16,8,288]{2,1,0:T(8,128)(2,1)S(1)}, bf16[16,8,288]{2,1,0:T(8,128)(2,1)S(1)}, u32[]{:S(2)}, u32[]{:S(2)}) collective-permute-start(bf16[16,8,288]{2,1,0:T(8,128)(2,1)S(1)} %get-tuple-element.5), channel_id=1, source_target_pairs={{1,0},{2,1},{3,2},{5,4},{6,5},{7,6},{9,8},{10,9},{11,10},{13,12},{... | collective-permute-start | bytes 221192 | tf_op jit(solution)/shard_map/ppermute | solution.py:143
  2.3 7.1 %collective-permute-start = (bf16[16,8,288]{2,1,0:T(8,128)(2,1)S(1)}, bf16[16,8,288]{2,1,0:T(8,128)(2,1)S(1)}, u32[]{:S(2)}, u32[]{:S(2)}) collective-permute-start(bf16[16,8,288]{2,1,0:T(8,128)(2,1)S(1)} %get-tuple-element.6), channel_id=1, source_target_pairs={{0,1},{1,2},{2,3},{4,5},{5,6},{6,7},{8,9},{9,10},{10,11},{12,13},{... | collective-permute-start | bytes 221192 | tf_op jit(solution)/shard_map/ppermute | solution.py:142
  9.3 0.6 copy-start.1
  9.3 0.7 copy-start.2
  15.8 32.2 %all-to-all-start = ((bf16[64,2,2304]{2,1,0:T(2,128)(2,1)}), bf16[64,2,2304]{2,1,0:T(2,128)(2,1)S(1)}, u32[]{:S(2)}, u32[]{:S(2)}) async-start(bf16[64,2,2304]{2,1,0:T(2,128)(2,1)} %shard_map.56), calls=%async_computation | async-start | bytes 1179648 | tf_op jit(solution)/shard_map/all_to_all | solution.py:147
  48.0 0.8 copy-start

commit v17 on v16

--- a/solution.py
+++ b/solution.py
@@ -7,6 +7,7 @@
 
 HALO = 8
 EDGE = 8
+PACK = 16
 ATOMS_DEV = 1
 
 
@@ -35,7 +36,15 @@
     row = jnp.sum(jnp.where(rows == domain - base, block, 0.0), axis=0, keepdims=True)
     wide = jnp.broadcast_to(row, (count, 2 * count))
     rolled = pltpu.roll(wide, shift=count, axis=1, stride=1, stride_axis=0)
-    out_ref[...] = jnp.transpose(rolled[:, :count]).astype(out_ref.dtype)
+    kernel = jnp.transpose(rolled[:, :count]).astype(jnp.bfloat16)
+    peers = count // PACK
+    place = lax.broadcasted_iota(jnp.int32, (count, count), 0)
+    energy = lax.broadcasted_iota(jnp.int32, (count, count), 1)
+    order = (energy == PACK * (place % peers) + place // peers).astype(jnp.bfloat16)
+    rows_first = jnp.dot(order, kernel, preferred_element_type=jnp.float32).astype(jnp.bfloat16)
+    out_ref[...] = lax.dot_general(
+        rows_first, order, (((1,), (1,)), ((), ())), preferred_element_type=jnp.float32
+    ).astype(out_ref.dtype)
 
 
 def toeplitz_build(owner, phonon, count):
@@ -50,14 +59,20 @@
     )(owner, phonon)
 
 
-def toeplitz_kernel(kernel_ref, packed_ref, out_ref, blocks_ref):
-    peers, energies, comps = blocks_ref.shape
-    count = peers * energies
-    load_packed(packed_ref, blocks_ref)
-    product = jnp.dot(
-        kernel_ref[...], blocks_ref[...].reshape(count, comps), preferred_element_type=jnp.float32
-    )
-    store_packed(out_ref, product.astype(out_ref.dtype).reshape(peers, energies, comps))
+def toeplitz_kernel(kernel_ref, packed_ref, out_ref, columns_ref):
+    peers = packed_ref.shape[0]
+    comps = columns_ref.shape[1]
+    half = packed_ref.shape[2] // comps
+    for h in range(2):
+        for e in range(half):
+            block = (h * half + e) * peers
+            columns_ref[block:block + peers, :] = packed_ref[:, h, e * comps:(e + 1) * comps]
+    product = jnp.dot(kernel_ref[...], columns_ref[...], preferred_element_type=jnp.float32)
+    product = product.astype(out_ref.dtype)
+    for h in range(2):
+        for e in range(half):
+            block = (h * half + e) * peers
+            out_ref[:, h, e * comps:(e + 1) * comps] = product[block:block + peers, :]
 
 
 def toeplitz_apply(kernel_t, packed, energies):
@@ -70,7 +85,7 @@
         out_shape=jax.ShapeDtypeStruct(packed.shape, jnp.bfloat16),
         in_specs=[vmem, vmem],
         out_specs=vmem,
-        scratch_shapes=[pltpu.VMEM((peers, energies, comps), jnp.bfloat16)],
+        scratch_shapes=[pltpu.VMEM((count, comps), jnp.bfloat16)],
         cost_estimate=pl.CostEstimate(
             flops=2 * count * count * comps,
             bytes_accessed=2 * (count * count + 2 * count * comps),

time: 82.4 us -> 82.5 us (level)
  Pallas kernels: 14.6 us -> 19 us
  waiting for transfers between devices: 16.3 us -> 12 us
    all_to_all x1, waiting for transfers between devices: 16.3 us -> 12 us  [per_device(): lax.all_to_all(outgoing, 'energy', split_axis=0, concat_axis=0, tiled=True)]
    pallas_call x1, Pallas kernels: 2.73 us -> 7.02 us  [toeplitz_build(): pl.pallas_call(toeplitz_build_kernel, out_shape=jax.ShapeDtypeStruct((cou...]
  transfers between devices with their start and end apart: 3 -> 3, of which waited for: 1 -> 1; matrix products, arithmetic and copies ran while one was open for 3% -> 3% of each run, Pallas kernels for 3% -> 9%
where the time goes in v17:
time: 82.5 us; the launch traced here: 82 us
  blocking collectives  24.8 us (30%)
  starting transfers between devices  19 us (23%)
  Pallas kernels  19 us (23%)
  waiting for transfers between devices  12 us (15%)
  local copies, waits for them, and re-layouts  7.13 us (9%)
    all_to_all x1, blocking collectives, per_device(): lax.all_to_all(product, 'energy', split_axis=0, concat_axis=0, tiled=True)  24.8 us
    all_to_all x1, starting transfers between devices, per_device(): lax.all_to_all(outgoing, 'energy', split_axis=0, concat_axis=0, tiled=True)  13.1 us
    all_to_all x1, waiting for transfers between devices, per_device(): lax.all_to_all(outgoing, 'energy', split_axis=0, concat_axis=0, tiled=True)  12 us
    pallas_call x1, Pallas kernels, toeplitz_build(): pl.pallas_call(toeplitz_build_kernel, out_shape=jax.ShapeDtypeStruct((cou...  7.02 us
    pallas_call x1, Pallas kernels, toeplitz_apply(): pl.pallas_call(toeplitz_kernel, out_shape=jax.ShapeDtypeStruct(packed.sha...  6.17 us
    pallas_call x1, Pallas kernels, neighbour_apply(): pl.pallas_call(neighbour_kernel, out_shape=jax.ShapeDtypeStruct((atoms, 2...  5.8 us
    ppermute x1, starting transfers between devices, per_device(): low = lax.ppermute(green[:, group_size - EDGE:], 'atoms', forward)  4.58 us
    unnamed x7, local copies, waits for them, and re-layouts  3.95 us
  transfers between devices with their start and end apart: 3, of which 1 were waited for; matrix products, arithmetic and copies ran while one was open for 3% of the time, Pallas kernels for 9%

profile of v17, /device:TPU:1, one launch (start us, length us, event | category | flops | bytes accessed | tf_op | source)
XLA Modules:
  0.0 82.0 jit_solution(9802449130382130721)
XLA Ops:
  0.0 1.0 %fusion = (bf16[16,8,288]{2,1,0:T(8,128)(2,1)S(1)}, bf16[16,8,288]{2,1,0:T(8,128)(2,1)S(1)}) fusion(bf16[16,64,288]{2,1,0:T(8,128)(2,1)} %param.5), kind=kLoop, calls=%fused_computation.2 | loop fusion | bytes 294912 | tf_op jit(solution)/shard_map/slice | solution.py:158
  1.0 1.3 %collective-permute-start.1 = (bf16[16,8,288]{2,1,0:T(8,128)(2,1)S(1)}, bf16[16,8,288]{2,1,0:T(8,128)(2,1)S(1)}, u32[]{:S(2)}, u32[]{:S(2)}) collective-permute-start(bf16[16,8,288]{2,1,0:T(8,128)(2,1)S(1)} %get-tuple-element.5), channel_id=1, source_target_pairs={{1,0},{2,1},{3,2},{5,4},{6,5},{7,6},{9,8},{10,9},{11,10},{13,12},{... | collective-permute-start | bytes 221192 | tf_op jit(solution)/shard_map/ppermute | solution.py:158
  2.3 4.6 %collective-permute-start = (bf16[16,8,288]{2,1,0:T(8,128)(2,1)S(1)}, bf16[16,8,288]{2,1,0:T(8,128)(2,1)S(1)}, u32[]{:S(2)}, u32[]{:S(2)}) collective-permute-start(bf16[16,8,288]{2,1,0:T(8,128)(2,1)S(1)} %get-tuple-element.6), channel_id=1, source_target_pairs={{0,1},{1,2},{2,3},{4,5},{5,6},{6,7},{8,9},{9,10},{10,11},{12,13},{... | collective-permute-start | bytes 221192 | tf_op jit(solution)/shard_map/ppermute | solution.py:157
  6.9 2.5 %copy.11 = bf16[16,64,288]{2,0,1:T(8,128)(2,1)} copy(bf16[16,64,288]{2,1,0:T(8,128)(2,1)} %param.5) | data formatting | bytes 1179648 | tf_op args[0]
  9.3 0.0 collective-permute-done.1.high_ref
  9.3 0.0 copy-start.1
  9.3 0.0 collective-permute-done.low_ref
  9.3 0.0 copy-start.2
  9.3 0.6 copy-done.1
  10.0 0.1 copy-done.2
  10.0 5.8 %shard_map.56 = bf16[64,2,2304]{2,1,0:T(2,128)(2,1)} custom-call(s32[4,64]{1,0:T(4,128)} %bitcast.10, bf16[16,8,288]{2,1,0:T(8,128)(2,1)} %copy-done.2, bf16[64,16,288]{2,1,0:T(8,128)(2,1)} %bitcast.8, bf16[16,8,288]{2,1,0:T(8,128)(2,1)} %copy-done.1, bf16[4,288,288]{2,1,0:T(8,128)(2,1)} %superop_ref.1), custom_call_target="tpu_custom_call" | custom-call | flops 679477248 | bytes 1990656 | tf_op jit(solution)/shard_map/pallas_call | solution.py:132
  15.8 13.1 %all-to-all-start = ((bf16[64,2,2304]{2,1,0:T(2,128)(2,1)}), bf16[64,2,2304]{2,1,0:T(2,128)(2,1)S(1)}, u32[]{:S(2)}, u32[]{:S(2)}) async-start(bf16[64,2,2304]{2,1,0:T(2,128)(2,1)} %shard_map.56), calls=%async_computation | async-start | bytes 1179648 | tf_op jit(solution)/shard_map/all_to_all | solution.py:162
  28.9 7.0 %shard_map.55.kernel_ref = bf16[1024,1024]{1,0:T(8,128)(2,1)} custom-call(s32[1,64]{1,0:T(1,128)} %bitcast.9, bf16[64,2048]{1,0:T(8,128)(2,1)} %phonon_ref.1), custom_call_target="tpu_custom_call" | custom-call | bytes 2359296 | tf_op jit(solution)/shard_map/pallas_call | solution.py:51
  36.0 12.0 %all-to-all-done.packed_ref = bf16[64,2,2304]{2,1,0:T(2,128)(2,1)S(1)} async-done(((bf16[64,2,2304]{2,1,0:T(2,128)(2,1)}), bf16[64,2,2304]{2,1,0:T(2,128)(2,1)S(1)}, u32[]{:S(2)}, u32[]{:S(2)}) %all-to-all-start) | async-done | bytes 589856 | tf_op jit(solution)/shard_map/all_to_all | solution.py:162
  48.0 0.0 copy-start
  48.0 0.8 copy-done
  48.8 6.2 %shard_map.57 = bf16[64,2,2304]{2,1,0:T(2,128)(2,1)} custom-call(bf16[1024,1024]{1,0:T(8,128)(2,1)} %shard_map.55.kernel_ref, bf16[64,2,2304]{2,1,0:T(2,128)(2,1)} %copy-done), custom_call_target="tpu_custom_call" | custom-call | flops 603979776 | bytes 3276800 | tf_op jit(solution)/shard_map/pallas_call | solution.py:83
  55.0 24.8 %all_to_all.10 = bf16[64,2,2304]{2,1,0:T(2,128)(2,1)S(1)} all-to-all(bf16[64,2,2304]{2,1,0:T(2,128)(2,1)} %shard_map.57), channel_id=1, replica_groups=mesh['energy'=64,'atoms'=4] {'energy'}, dimensions={0} | all-to-all | bytes 1179648 | tf_op jit(solution)/shard_map/all_to_all | solution.py:164
  79.8 1.2 %reshape.3 = bf16[64,16,288]{2,1,0:T(8,128)(2,1)S(1)} reshape(bf16[64,2,2304]{2,1,0:T(2,128)(2,1)S(1)} %all_to_all.10) | data formatting | bytes 1179648 | tf_op jit(solution)/shard_map/reshape | solution.py:165
  81.0 1.1 %copy.10 = bf16[64,16,288]{2,0,1:T(8,128)(2,1)} copy(bf16[64,16,288]{2,1,0:T(8,128)(2,1)S(1)} %reshape.3) | data formatting | bytes 1179648 | tf_op jit(solution)/shard_map/reshape | solution.py:165
Async XLA Ops:
  1.0 8.4 %collective-permute-start.1 = (bf16[16,8,288]{2,1,0:T(8,128)(2,1)S(1)}, bf16[16,8,288]{2,1,0:T(8,128)(2,1)S(1)}, u32[]{:S(2)}, u32[]{:S(2)}) collective-permute-start(bf16[16,8,288]{2,1,0:T(8,128)(2,1)S(1)} %get-tuple-element.5), channel_id=1, source_target_pairs={{1,0},{2,1},{3,2},{5,4},{6,5},{7,6},{9,8},{10,9},{11,10},{13,12},{... | collective-permute-start | bytes 221192 | tf_op jit(solution)/shard_map/ppermute | solution.py:158
  2.3 7.1 %collective-permute-start = (bf16[16,8,288]{2,1,0:T(8,128)(2,1)S(1)}, bf16[16,8,288]{2,1,0:T(8,128)(2,1)S(1)}, u32[]{:S(2)}, u32[]{:S(2)}) collective-permute-start(bf16[16,8,288]{2,1,0:T(8,128)(2,1)S(1)} %get-tuple-element.6), channel_id=1, source_target_pairs={{0,1},{1,2},{2,3},{4,5},{5,6},{6,7},{8,9},{9,10},{10,11},{12,13},{... | collective-permute-start | bytes 221192 | tf_op jit(solution)/shard_map/ppermute | solution.py:157
  9.3 0.6 copy-start.1
  9.3 0.7 copy-start.2
  15.8 32.2 %all-to-all-start = ((bf16[64,2,2304]{2,1,0:T(2,128)(2,1)}), bf16[64,2,2304]{2,1,0:T(2,128)(2,1)S(1)}, u32[]{:S(2)}, u32[]{:S(2)}) async-start(bf16[64,2,2304]{2,1,0:T(2,128)(2,1)} %shard_map.56), calls=%async_computation | async-start | bytes 1179648 | tf_op jit(solution)/shard_map/all_to_all | solution.py:162
  48.0 0.8 copy-start

commit v18 on v14

--- a/solution.py
+++ b/solution.py
@@ -35,12 +35,11 @@
     block = phonon_ref[pl.ds(base, 16), :].astype(jnp.float32)
     rows = lax.broadcasted_iota(jnp.int32, block.shape, 0)
     row = jnp.sum(jnp.where(rows == domain - base, block, 0.0), axis=0, keepdims=True)
-    wide = jnp.broadcast_to(row.astype(jnp.bfloat16), (count, 2 * count))
+    wide = jnp.broadcast_to(row, (count, 2 * count))
     rolled = pltpu.roll(wide, shift=count, axis=1, stride=1, stride_axis=0)
-    kernel_t = rolled[:, :count]
-    product = lax.dot_general(
-        kernel_t, blocks_ref[...].reshape(count, comps), (((0,), (0,)), ((), ())),
-        preferred_element_type=jnp.float32,
+    kernel = jnp.transpose(rolled[:, :count]).astype(jnp.bfloat16)
+    product = jnp.dot(
+        kernel, blocks_ref[...].reshape(count, comps), preferred_element_type=jnp.float32
     )
     store_packed(out_ref, product.astype(out_ref.dtype).reshape(peers, energies, comps))
 

time: 81.8 us -> 81.7 us (level)
  no operation moved by 1% of the time
where the time goes in v18:
time: 81.7 us; the launch traced here: 81.2 us
  blocking collectives  57.1 us (70%)
  Pallas kernels  11.9 us (15%)
  local copies, waits for them, and re-layouts  6.31 us (8%)
  starting transfers between devices  5.87 us (7%)
    all_to_all x1, blocking collectives, per_device(): lax.all_to_all(outgoing, 'energy', split_axis=0, concat_axis=0, tiled=True)  32.3 us
    all_to_all x1, blocking collectives, per_device(): lax.all_to_all(product, 'energy', split_axis=0, concat_axis=0, tiled=True)  24.8 us
    pallas_call x1, Pallas kernels, toeplitz_apply(): pl.pallas_call(toeplitz_kernel, out_shape=jax.ShapeDtypeStruct(packed.sha...  6.08 us
    pallas_call x1, Pallas kernels, neighbour_apply(): pl.pallas_call(neighbour_kernel, out_shape=jax.ShapeDtypeStruct((atoms, 2...  5.8 us
    ppermute x1, starting transfers between devices, per_device(): low = lax.ppermute(green[:, group_size - EDGE:], 'atoms', forward)  4.58 us
    unnamed x5, local copies, waits for them, and re-layouts  3.13 us
    reshape x2, local copies, waits for them, and re-layouts, per_device(): result = result.reshape(result.shape[0], local_energies, comps)  2.22 us
  transfers between devices with their start and end apart: 2, of which 0 were waited for; matrix products, arithmetic and copies ran while one was open for 3% of the time, Pallas kernels for 0%

profile of v18, /device:TPU:1, one launch (start us, length us, event | category | flops | bytes accessed | tf_op | source)
XLA Modules:
  0.0 81.2 jit_solution(9192225635533925998)
XLA Ops:
  0.0 1.0 %fusion = (bf16[16,8,288]{2,1,0:T(8,128)(2,1)S(1)}, bf16[16,8,288]{2,1,0:T(8,128)(2,1)S(1)}) fusion(bf16[16,64,288]{2,1,0:T(8,128)(2,1)} %param.5), kind=kLoop, calls=%fused_computation.2 | loop fusion | bytes 294912 | tf_op jit(solution)/shard_map/slice | solution.py:127
  1.0 1.3 %collective-permute-start.1 = (bf16[16,8,288]{2,1,0:T(8,128)(2,1)S(1)}, bf16[16,8,288]{2,1,0:T(8,128)(2,1)S(1)}, u32[]{:S(2)}, u32[]{:S(2)}) collective-permute-start(bf16[16,8,288]{2,1,0:T(8,128)(2,1)S(1)} %get-tuple-element.9), channel_id=1, source_target_pairs={{1,0},{2,1},{3,2},{5,4},{6,5},{7,6},{9,8},{10,9},{11,10},{13,12},{... | collective-permute-start | bytes 221192 | tf_op jit(solution)/shard_map/ppermute | solution.py:127
  2.3 4.6 %collective-permute-start = (bf16[16,8,288]{2,1,0:T(8,128)(2,1)S(1)}, bf16[16,8,288]{2,1,0:T(8,128)(2,1)S(1)}, u32[]{:S(2)}, u32[]{:S(2)}) collective-permute-start(bf16[16,8,288]{2,1,0:T(8,128)(2,1)S(1)} %get-tuple-element.10), channel_id=1, source_target_pairs={{0,1},{1,2},{2,3},{4,5},{5,6},{6,7},{8,9},{9,10},{10,11},{12,13},{... | collective-permute-start | bytes 221192 | tf_op jit(solution)/shard_map/ppermute | solution.py:126
  6.9 2.5 %copy.11 = bf16[16,64,288]{2,0,1:T(8,128)(2,1)} copy(bf16[16,64,288]{2,1,0:T(8,128)(2,1)} %param.5) | data formatting | bytes 1179648 | tf_op args[0]
  9.3 0.0 collective-permute-done.1.high_ref
  9.3 0.0 copy-start
  9.3 0.0 collective-permute-done.low_ref
  9.3 0.0 copy-start.1
  9.3 0.6 copy-done
  10.0 0.0 copy-done.1
  10.0 5.8 %shard_map.55 = bf16[64,2,2304]{2,1,0:T(2,128)(2,1)} custom-call(s32[4,64]{1,0:T(4,128)} %bitcast.9, bf16[16,8,288]{2,1,0:T(8,128)(2,1)} %copy-done.1, bf16[64,16,288]{2,1,0:T(8,128)(2,1)} %bitcast.8, bf16[16,8,288]{2,1,0:T(8,128)(2,1)} %copy-done, bf16[4,288,288]{2,1,0:T(8,128)(2,1)} %superop_ref.1), custom_call_target="tpu_custom_call" | custom-call | flops 679477248 | bytes 1990656 | tf_op jit(solution)/shard_map/pallas_call | solution.py:101
  15.8 32.3 %all_to_all.10.packed_ref = bf16[64,2,2304]{2,1,0:T(2,128)(2,1)} all-to-all(bf16[64,2,2304]{2,1,0:T(2,128)(2,1)} %shard_map.55), channel_id=1, replica_groups=mesh['energy'=64,'atoms'=4] {'energy'}, dimensions={0} | all-to-all | bytes 1179648 | tf_op jit(solution)/shard_map/all_to_all | solution.py:130
  48.1 6.1 %shard_map.56 = bf16[64,2,2304]{2,1,0:T(2,128)(2,1)} custom-call(s32[1,64]{1,0:T(1,128)} %bitcast.10, bf16[64,2048]{1,0:T(8,128)(2,1)} %phonon_ref.1, bf16[64,2,2304]{2,1,0:T(2,128)(2,1)} %all_to_all.10.packed_ref), custom_call_target="tpu_custom_call" | custom-call | flops 603979776 | bytes 1441792 | tf_op jit(solution)/shard_map/pallas_call | solution.py:52
  54.2 24.8 %all_to_all.11 = bf16[64,2,2304]{2,1,0:T(2,128)(2,1)S(1)} all-to-all(bf16[64,2,2304]{2,1,0:T(2,128)(2,1)} %shard_map.56), channel_id=1, replica_groups=mesh['energy'=64,'atoms'=4] {'energy'}, dimensions={0} | all-to-all | bytes 1179648 | tf_op jit(solution)/shard_map/all_to_all | solution.py:132
  79.0 1.2 %reshape.3 = bf16[64,16,288]{2,1,0:T(8,128)(2,1)S(1)} reshape(bf16[64,2,2304]{2,1,0:T(2,128)(2,1)S(1)} %all_to_all.11) | data formatting | bytes 1179648 | tf_op jit(solution)/shard_map/reshape | solution.py:133
  80.2 1.1 %copy.10 = bf16[64,16,288]{2,0,1:T(8,128)(2,1)} copy(bf16[64,16,288]{2,1,0:T(8,128)(2,1)S(1)} %reshape.3) | data formatting | bytes 1179648 | tf_op jit(solution)/shard_map/reshape | solution.py:133
Async XLA Ops:
  1.0 8.4 %collective-permute-start.1 = (bf16[16,8,288]{2,1,0:T(8,128)(2,1)S(1)}, bf16[16,8,288]{2,1,0:T(8,128)(2,1)S(1)}, u32[]{:S(2)}, u32[]{:S(2)}) collective-permute-start(bf16[16,8,288]{2,1,0:T(8,128)(2,1)S(1)} %get-tuple-element.9), channel_id=1, source_target_pairs={{1,0},{2,1},{3,2},{5,4},{6,5},{7,6},{9,8},{10,9},{11,10},{13,12},{... | collective-permute-start | bytes 221192 | tf_op jit(solution)/shard_map/ppermute | solution.py:127
  2.3 7.1 %collective-permute-start = (bf16[16,8,288]{2,1,0:T(8,128)(2,1)S(1)}, bf16[16,8,288]{2,1,0:T(8,128)(2,1)S(1)}, u32[]{:S(2)}, u32[]{:S(2)}) collective-permute-start(bf16[16,8,288]{2,1,0:T(8,128)(2,1)S(1)} %get-tuple-element.10), channel_id=1, source_target_pairs={{0,1},{1,2},{2,3},{4,5},{5,6},{6,7},{8,9},{9,10},{10,11},{12,13},{... | collective-permute-start | bytes 221192 | tf_op jit(solution)/shard_map/ppermute | solution.py:126
  9.3 0.6 copy-start
  9.3 0.7 copy-start.1

commit v19 on v18

--- a/solution.py
+++ b/solution.py
@@ -35,9 +35,9 @@
     block = phonon_ref[pl.ds(base, 16), :].astype(jnp.float32)
     rows = lax.broadcasted_iota(jnp.int32, block.shape, 0)
     row = jnp.sum(jnp.where(rows == domain - base, block, 0.0), axis=0, keepdims=True)
-    wide = jnp.broadcast_to(row, (count, 2 * count))
+    wide = jnp.broadcast_to(row.astype(jnp.bfloat16), (count, 2 * count))
     rolled = pltpu.roll(wide, shift=count, axis=1, stride=1, stride_axis=0)
-    kernel = jnp.transpose(rolled[:, :count]).astype(jnp.bfloat16)
+    kernel = jnp.transpose(rolled[:, :count])
     product = jnp.dot(
         kernel, blocks_ref[...].reshape(count, comps), preferred_element_type=jnp.float32
     )

time: 81.7 us -> 81.7 us (level)
  no operation moved by 1% of the time
where the time goes in v19:
time: 81.7 us; the launch traced here: 81.3 us
  blocking collectives  57.1 us (70%)
  Pallas kernels  12 us (15%)
  local copies, waits for them, and re-layouts  6.31 us (8%)
  starting transfers between devices  5.87 us (7%)
    all_to_all x1, blocking collectives, per_device(): lax.all_to_all(outgoing, 'energy', split_axis=0, concat_axis=0, tiled=True)  32.3 us
    all_to_all x1, blocking collectives, per_device(): lax.all_to_all(product, 'energy', split_axis=0, concat_axis=0, tiled=True)  24.8 us
    pallas_call x1, Pallas kernels, toeplitz_apply(): pl.pallas_call(toeplitz_kernel, out_shape=jax.ShapeDtypeStruct(packed.sha...  6.15 us
    pallas_call x1, Pallas kernels, neighbour_apply(): pl.pallas_call(neighbour_kernel, out_shape=jax.ShapeDtypeStruct((atoms, 2...  5.81 us
    ppermute x1, starting transfers between devices, per_device(): low = lax.ppermute(green[:, group_size - EDGE:], 'atoms', forward)  4.58 us
    unnamed x5, local copies, waits for them, and re-layouts  3.13 us
    reshape x2, local copies, waits for them, and re-layouts, per_device(): result = result.reshape(result.shape[0], local_energies, comps)  2.22 us
  transfers between devices with their start and end apart: 2, of which 0 were waited for; matrix products, arithmetic and copies ran while one was open for 3% of the time, Pallas kernels for 0%

profile of v19, /device:TPU:1, one launch (start us, length us, event | category | flops | bytes accessed | tf_op | source)
XLA Modules:
  0.0 81.3 jit_solution(17062560009308136845)
XLA Ops:
  0.0 1.0 %fusion = (bf16[16,8,288]{2,1,0:T(8,128)(2,1)S(1)}, bf16[16,8,288]{2,1,0:T(8,128)(2,1)S(1)}) fusion(bf16[16,64,288]{2,1,0:T(8,128)(2,1)} %param.5), kind=kLoop, calls=%fused_computation.2 | loop fusion | bytes 294912 | tf_op jit(solution)/shard_map/slice | solution.py:127
  1.0 1.3 %collective-permute-start.1 = (bf16[16,8,288]{2,1,0:T(8,128)(2,1)S(1)}, bf16[16,8,288]{2,1,0:T(8,128)(2,1)S(1)}, u32[]{:S(2)}, u32[]{:S(2)}) collective-permute-start(bf16[16,8,288]{2,1,0:T(8,128)(2,1)S(1)} %get-tuple-element.9), channel_id=1, source_target_pairs={{1,0},{2,1},{3,2},{5,4},{6,5},{7,6},{9,8},{10,9},{11,10},{13,12},{... | collective-permute-start | bytes 221192 | tf_op jit(solution)/shard_map/ppermute | solution.py:127
  2.3 4.6 %collective-permute-start = (bf16[16,8,288]{2,1,0:T(8,128)(2,1)S(1)}, bf16[16,8,288]{2,1,0:T(8,128)(2,1)S(1)}, u32[]{:S(2)}, u32[]{:S(2)}) collective-permute-start(bf16[16,8,288]{2,1,0:T(8,128)(2,1)S(1)} %get-tuple-element.10), channel_id=1, source_target_pairs={{0,1},{1,2},{2,3},{4,5},{5,6},{6,7},{8,9},{9,10},{10,11},{12,13},{... | collective-permute-start | bytes 221192 | tf_op jit(solution)/shard_map/ppermute | solution.py:126
  6.9 2.5 %copy.11 = bf16[16,64,288]{2,0,1:T(8,128)(2,1)} copy(bf16[16,64,288]{2,1,0:T(8,128)(2,1)} %param.5) | data formatting | bytes 1179648 | tf_op args[0]
  9.3 0.0 collective-permute-done.1.high_ref
  9.3 0.0 copy-start
  9.3 0.0 collective-permute-done.low_ref
  9.3 0.0 copy-start.1
  9.3 0.6 copy-done
  10.0 0.0 copy-done.1
  10.0 5.8 %shard_map.55 = bf16[64,2,2304]{2,1,0:T(2,128)(2,1)} custom-call(s32[4,64]{1,0:T(4,128)} %bitcast.9, bf16[16,8,288]{2,1,0:T(8,128)(2,1)} %copy-done.1, bf16[64,16,288]{2,1,0:T(8,128)(2,1)} %bitcast.8, bf16[16,8,288]{2,1,0:T(8,128)(2,1)} %copy-done, bf16[4,288,288]{2,1,0:T(8,128)(2,1)} %superop_ref.1), custom_call_target="tpu_custom_call" | custom-call | flops 679477248 | bytes 1990656 | tf_op jit(solution)/shard_map/pallas_call | solution.py:101
  15.8 32.3 %all_to_all.10.packed_ref = bf16[64,2,2304]{2,1,0:T(2,128)(2,1)} all-to-all(bf16[64,2,2304]{2,1,0:T(2,128)(2,1)} %shard_map.55), channel_id=1, replica_groups=mesh['energy'=64,'atoms'=4] {'energy'}, dimensions={0} | all-to-all | bytes 1179648 | tf_op jit(solution)/shard_map/all_to_all | solution.py:130
  48.1 6.2 %shard_map.56 = bf16[64,2,2304]{2,1,0:T(2,128)(2,1)} custom-call(s32[1,64]{1,0:T(1,128)} %bitcast.10, bf16[64,2048]{1,0:T(8,128)(2,1)} %phonon_ref.1, bf16[64,2,2304]{2,1,0:T(2,128)(2,1)} %all_to_all.10.packed_ref), custom_call_target="tpu_custom_call" | custom-call | flops 603979776 | bytes 1441792 | tf_op jit(solution)/shard_map/pallas_call | solution.py:52
  54.2 24.8 %all_to_all.11 = bf16[64,2,2304]{2,1,0:T(2,128)(2,1)S(1)} all-to-all(bf16[64,2,2304]{2,1,0:T(2,128)(2,1)} %shard_map.56), channel_id=1, replica_groups=mesh['energy'=64,'atoms'=4] {'energy'}, dimensions={0} | all-to-all | bytes 1179648 | tf_op jit(solution)/shard_map/all_to_all | solution.py:132
  79.1 1.2 %reshape.3 = bf16[64,16,288]{2,1,0:T(8,128)(2,1)S(1)} reshape(bf16[64,2,2304]{2,1,0:T(2,128)(2,1)S(1)} %all_to_all.11) | data formatting | bytes 1179648 | tf_op jit(solution)/shard_map/reshape | solution.py:133
  80.2 1.1 %copy.10 = bf16[64,16,288]{2,0,1:T(8,128)(2,1)} copy(bf16[64,16,288]{2,1,0:T(8,128)(2,1)S(1)} %reshape.3) | data formatting | bytes 1179648 | tf_op jit(solution)/shard_map/reshape | solution.py:133
Async XLA Ops:
  1.0 8.4 %collective-permute-start.1 = (bf16[16,8,288]{2,1,0:T(8,128)(2,1)S(1)}, bf16[16,8,288]{2,1,0:T(8,128)(2,1)S(1)}, u32[]{:S(2)}, u32[]{:S(2)}) collective-permute-start(bf16[16,8,288]{2,1,0:T(8,128)(2,1)S(1)} %get-tuple-element.9), channel_id=1, source_target_pairs={{1,0},{2,1},{3,2},{5,4},{6,5},{7,6},{9,8},{10,9},{11,10},{13,12},{... | collective-permute-start | bytes 221192 | tf_op jit(solution)/shard_map/ppermute | solution.py:127
  2.3 7.1 %collective-permute-start = (bf16[16,8,288]{2,1,0:T(8,128)(2,1)S(1)}, bf16[16,8,288]{2,1,0:T(8,128)(2,1)S(1)}, u32[]{:S(2)}, u32[]{:S(2)}) collective-permute-start(bf16[16,8,288]{2,1,0:T(8,128)(2,1)S(1)} %get-tuple-element.10), channel_id=1, source_target_pairs={{0,1},{1,2},{2,3},{4,5},{5,6},{6,7},{8,9},{9,10},{10,11},{12,13},{... | collective-permute-start | bytes 221192 | tf_op jit(solution)/shard_map/ppermute | solution.py:126
  9.3 0.6 copy-start
  9.3 0.7 copy-start.1

commit v20 on v19

--- a/solution.py
+++ b/solution.py
@@ -130,8 +130,8 @@
     columns = lax.all_to_all(outgoing, "energy", split_axis=0, concat_axis=0, tiled=True)
     product = toeplitz_apply(owner_t, phonon, columns, local_energies)
     result = lax.all_to_all(product, "energy", split_axis=0, concat_axis=0, tiled=True)
-    result = result.reshape(result.shape[0], local_energies, comps)
-    return jnp.transpose(result, (1, 0, 2))
+    result = result.reshape(result.shape[0], 2, local_energies // 2, comps)
+    return jnp.transpose(result, (1, 2, 0, 3)).reshape(local_energies, result.shape[0], comps)
 
 
 def solution(mesh):

time: 81.7 us -> 81.8 us (level)
    transpose x0 -> x1, local copies, waits for them, and re-layouts: none -> 1.06 us  [per_device(): jnp.transpose(result, (1, 2, 0, 3))]
    reshape x2 -> x1, local copies, waits for them, and re-layouts: 2.22 us -> 1.16 us  [per_device(): result = result.reshape(result.shape[0], 2, local_energies // 2, comps)]
where the time goes in v20:
time: 81.8 us; the launch traced here: 81.3 us
  blocking collectives  57.1 us (70%)
  Pallas kernels  12 us (15%)
  local copies, waits for them, and re-layouts  6.32 us (8%)
  starting transfers between devices  5.87 us (7%)
    all_to_all x1, blocking collectives, per_device(): lax.all_to_all(outgoing, 'energy', split_axis=0, concat_axis=0, tiled=True)  32.3 us
    all_to_all x1, blocking collectives, per_device(): lax.all_to_all(product, 'energy', split_axis=0, concat_axis=0, tiled=True)  24.8 us
    pallas_call x1, Pallas kernels, toeplitz_apply(): pl.pallas_call(toeplitz_kernel, out_shape=jax.ShapeDtypeStruct(packed.sha...  6.16 us
    pallas_call x1, Pallas kernels, neighbour_apply(): pl.pallas_call(neighbour_kernel, out_shape=jax.ShapeDtypeStruct((atoms, 2...  5.81 us
    ppermute x1, starting transfers between devices, per_device(): low = lax.ppermute(green[:, group_size - EDGE:], 'atoms', forward)  4.58 us
    unnamed x5, local copies, waits for them, and re-layouts  3.13 us
  transfers between devices with their start and end apart: 2, of which 0 were waited for; matrix products, arithmetic and copies ran while one was open for 3% of the time, Pallas kernels for 0%

profile of v20, /device:TPU:1, one launch (start us, length us, event | category | flops | bytes accessed | tf_op | source)
XLA Modules:
  0.0 81.3 jit_solution(16884646042769421877)
XLA Ops:
  0.0 1.0 %fusion = (bf16[16,8,288]{2,1,0:T(8,128)(2,1)S(1)}, bf16[16,8,288]{2,1,0:T(8,128)(2,1)S(1)}) fusion(bf16[16,64,288]{2,1,0:T(8,128)(2,1)} %param.5), kind=kLoop, calls=%fused_computation.1 | loop fusion | bytes 294912 | tf_op jit(solution)/shard_map/slice | solution.py:127
  1.0 1.3 %collective-permute-start.1 = (bf16[16,8,288]{2,1,0:T(8,128)(2,1)S(1)}, bf16[16,8,288]{2,1,0:T(8,128)(2,1)S(1)}, u32[]{:S(2)}, u32[]{:S(2)}) collective-permute-start(bf16[16,8,288]{2,1,0:T(8,128)(2,1)S(1)} %get-tuple-element.9), channel_id=1, source_target_pairs={{1,0},{2,1},{3,2},{5,4},{6,5},{7,6},{9,8},{10,9},{11,10},{13,12},{... | collective-permute-start | bytes 221192 | tf_op jit(solution)/shard_map/ppermute | solution.py:127
  2.3 4.6 %collective-permute-start = (bf16[16,8,288]{2,1,0:T(8,128)(2,1)S(1)}, bf16[16,8,288]{2,1,0:T(8,128)(2,1)S(1)}, u32[]{:S(2)}, u32[]{:S(2)}) collective-permute-start(bf16[16,8,288]{2,1,0:T(8,128)(2,1)S(1)} %get-tuple-element.10), channel_id=1, source_target_pairs={{0,1},{1,2},{2,3},{4,5},{5,6},{6,7},{8,9},{9,10},{10,11},{12,13},{... | collective-permute-start | bytes 221192 | tf_op jit(solution)/shard_map/ppermute | solution.py:126
  6.9 2.5 %copy.9 = bf16[16,64,288]{2,0,1:T(8,128)(2,1)} copy(bf16[16,64,288]{2,1,0:T(8,128)(2,1)} %param.5) | data formatting | bytes 1179648 | tf_op args[0]
  9.3 0.0 collective-permute-done.1.high_ref
  9.3 0.0 copy-start
  9.3 0.0 collective-permute-done.low_ref
  9.3 0.0 copy-start.1
  9.3 0.6 copy-done
  10.0 0.0 copy-done.1
  10.0 5.8 %shard_map.55 = bf16[64,2,2304]{2,1,0:T(2,128)(2,1)} custom-call(s32[4,64]{1,0:T(4,128)} %bitcast.9, bf16[16,8,288]{2,1,0:T(8,128)(2,1)} %copy-done.1, bf16[64,16,288]{2,1,0:T(8,128)(2,1)} %bitcast.8, bf16[16,8,288]{2,1,0:T(8,128)(2,1)} %copy-done, bf16[4,288,288]{2,1,0:T(8,128)(2,1)} %superop_ref.1), custom_call_target="tpu_custom_call" | custom-call | flops 679477248 | bytes 1990656 | tf_op jit(solution)/shard_map/pallas_call | solution.py:101
  15.8 32.3 %all_to_all.10.packed_ref = bf16[64,2,2304]{2,1,0:T(2,128)(2,1)} all-to-all(bf16[64,2,2304]{2,1,0:T(2,128)(2,1)} %shard_map.55), channel_id=1, replica_groups=mesh['energy'=64,'atoms'=4] {'energy'}, dimensions={0} | all-to-all | bytes 1179648 | tf_op jit(solution)/shard_map/all_to_all | solution.py:130
  48.1 6.2 %shard_map.56 = bf16[64,2,2304]{2,1,0:T(2,128)(2,1)} custom-call(s32[1,64]{1,0:T(1,128)} %bitcast.10, bf16[64,2048]{1,0:T(8,128)(2,1)} %phonon_ref.1, bf16[64,2,2304]{2,1,0:T(2,128)(2,1)} %all_to_all.10.packed_ref), custom_call_target="tpu_custom_call" | custom-call | flops 603979776 | bytes 1441792 | tf_op jit(solution)/shard_map/pallas_call | solution.py:52
  54.2 24.8 %all_to_all.11 = bf16[64,2,2304]{2,1,0:T(2,128)(2,1)S(1)} all-to-all(bf16[64,2,2304]{2,1,0:T(2,128)(2,1)} %shard_map.56), channel_id=1, replica_groups=mesh['energy'=64,'atoms'=4] {'energy'}, dimensions={0} | all-to-all | bytes 1179648 | tf_op jit(solution)/shard_map/all_to_all | solution.py:132
  79.1 1.2 %reshape.6 = bf16[64,2,8,288]{3,2,1,0:T(8,128)(2,1)S(1)} reshape(bf16[64,2,2304]{2,1,0:T(2,128)(2,1)S(1)} %all_to_all.11) | data formatting | bytes 1179648 | tf_op jit(solution)/shard_map/reshape | solution.py:133
  80.2 1.1 %copy.7 = bf16[2,8,64,288]{3,2,1,0:T(8,128)(2,1)} copy(bf16[2,8,64,288]{3,1,0,2:T(8,128)(2,1)S(1)} %bitcast.7) | data formatting | bytes 1179648 | tf_op jit(solution)/shard_map/transpose | solution.py:134
Async XLA Ops:
  1.0 8.4 %collective-permute-start.1 = (bf16[16,8,288]{2,1,0:T(8,128)(2,1)S(1)}, bf16[16,8,288]{2,1,0:T(8,128)(2,1)S(1)}, u32[]{:S(2)}, u32[]{:S(2)}) collective-permute-start(bf16[16,8,288]{2,1,0:T(8,128)(2,1)S(1)} %get-tuple-element.9), channel_id=1, source_target_pairs={{1,0},{2,1},{3,2},{5,4},{6,5},{7,6},{9,8},{10,9},{11,10},{13,12},{... | collective-permute-start | bytes 221192 | tf_op jit(solution)/shard_map/ppermute | solution.py:127
  2.3 7.1 %collective-permute-start = (bf16[16,8,288]{2,1,0:T(8,128)(2,1)S(1)}, bf16[16,8,288]{2,1,0:T(8,128)(2,1)S(1)}, u32[]{:S(2)}, u32[]{:S(2)}) collective-permute-start(bf16[16,8,288]{2,1,0:T(8,128)(2,1)S(1)} %get-tuple-element.10), channel_id=1, source_target_pairs={{0,1},{1,2},{2,3},{4,5},{5,6},{6,7},{8,9},{9,10},{10,11},{12,13},{... | collective-permute-start | bytes 221192 | tf_op jit(solution)/shard_map/ppermute | solution.py:126
  9.3 0.6 copy-start
  9.3 0.7 copy-start.1
